TPU v7x, 512 devices: a whole 4x4x16 slice. The times are simulated.
512 devices in a mesh: tile: 64 (over z, x_hi, core), chan: 8 (over x_lo, y).
Axes of the slice: x: 4 (x_hi: 2, x_lo: 2; x = x_hi * 2 + x_lo), y: 4, z: 16, core: 2. Of those that a mesh axis runs over, the one named last changes fastest.
Arguments:
- analysis: bfloat16 [64, 524288], P('chan', 'tile'), may hold values from -6 to 6
- send_rows: int32 [64, 5, 128], P('tile'), may hold values from 0 to 8191
- send_count: int32 [64, 5], P('tile'), may hold values from 64 to 128, as said below
- corner_slot: int32 [4, 2048, 256], P(None, 'tile'), may hold values from 0 to 639, as said below
- corner_weight: float32 [4, 2048, 256], P(None, 'tile'), may hold values from 0.1 to 0.6
- beside: int32 [2048, 8], P('tile'), may hold values from 0 to 2047, as said below
- quarter_turns: int32 [2048, 8], P('tile'), may hold values from 0 to 3
- kernel_one: bfloat16 [9, 128, 64], P(None, 'chan'), may hold values from -0.375 to 0.375
- kernel_two: bfloat16 [9, 128, 128], P(None, 'chan'), may hold values from -0.25 to 0.25
- kernel_three: bfloat16 [9, 128, 128], P(None, 'chan'), may hold values from -0.25 to 0.25
Outputs:
- forecast: bfloat16 [128, 2048, 256], P('chan', 'tile')
Inputs may be any that keep to these rules, and one draw needn't show every extreme that they name: send_count[s, d] is at least 64; every shard sends 128 to itself (d = 2), and some receiver gets 128 from each of its 5 senders. corner_slot[j, t, i] = d * 128 + k names a live slot, k < send_count[s, d], of the block that shard s = (e - d + 2) mod the shard count sends to the shard e holding tile t; the four corners of a pixel are slots k, k + 1, k + 2, k + 3 of one block. beside[t, k] = (t + d) mod 2048 with 1 <= |d| <= 2.
All inputs are finite; a program needn't handle non-finite values.
Results may differ from a plain program's by a relative error of at most 0.007.
Values may be sent and summed in bfloat16 or wider, within the bound.
No kernel may reach another device: no remote copies, remote signals or barrier semaphores. Data moves between devices by JAX's collectives and lax.ppermute only.
A program may use at most 64 MiB of HBM per device.

v0:
```python
import jax
import jax.numpy as jnp
import numpy as np
from jax import lax
from jax.sharding import PartitionSpec as P

P_SIZE = 16
REACH = 2


def from_behind(value, axis, steps):
    count = lax.axis_size(axis)
    pairs = [(source, (source + steps) % count) for source in range(count)]
    return lax.ppermute(value, axis, pairs)


def extended_2(x, sides, width):
    for axis, dim in sides:
        size, length = (lax.axis_size(axis), x.shape[dim])
        up = [(i, (i + 1) % size) for i in range(size)]
        down = [(j, i) for i, j in up]
        last = lax.slice_in_dim(x, length - width, length, axis=dim)
        initial = lax.slice_in_dim(x, 0, width, axis=dim)
        before = lax.ppermute(last, axis, up)
        after = lax.ppermute(initial, axis, down)
        x = jnp.concatenate([before, x, after], axis=dim)
    return x


def cycle_table(extent):
    length = 4 * extent - 4
    entries = []
    for cycle_pos in range(length):
        if cycle_pos < extent:
            row_at, col_at = (cycle_pos, 0)
        elif cycle_pos < 2 * extent - 1:
            row_at, col_at = (extent - 1, cycle_pos - extent + 1)
        elif cycle_pos < 3 * extent - 2:
            row_at, col_at = (3 * extent - 3 - cycle_pos, extent - 1)
        else:
            row_at, col_at = (0, 4 * extent - 4 - cycle_pos)
        entries.append(row_at * extent + col_at)
    return np.array(entries, np.int32)


def border_tables(extent):
    length = 4 * extent - 4
    heading = []
    anchor = []
    for col_at in range(extent):
        heading.append(0)
        anchor.append(extent - 1 + col_at)
    for col_at in range(extent):
        heading.append(1)
        anchor.append((length - col_at) % length)
    for row_at in range(extent):
        heading.append(2)
        anchor.append(3 * extent - 3 - row_at)
    for row_at in range(extent):
        heading.append(3)
        anchor.append(row_at)
    heading += [4, 5, 6, 7]
    anchor += [2 * extent - 2, extent - 1, 3 * extent - 3, 0]
    return (np.array(heading, np.int32), np.array(anchor, np.int32))


def layout_table(extent):
    padded_side = extent + 2
    interior = extent * extent
    entries = []
    for row_at in range(padded_side):
        for col_at in range(padded_side):
            if 1 <= row_at <= extent and 1 <= col_at <= extent:
                entries.append((row_at - 1) * extent + col_at - 1)
            elif row_at == 0 and 1 <= col_at <= extent:
                entries.append(interior + col_at - 1)
            elif row_at == padded_side - 1 and 1 <= col_at <= extent:
                entries.append(interior + extent + col_at - 1)
            elif col_at == 0 and 1 <= row_at <= extent:
                entries.append(interior + 2 * extent + row_at - 1)
            elif col_at == padded_side - 1 and 1 <= row_at <= extent:
                entries.append(interior + 3 * extent + row_at - 1)
            else:
                corner = (0 if row_at == 0 else 2) + (0 if col_at == 0 else 1)
                entries.append(interior + 4 * extent + corner)
    return np.array(entries, np.int32)


def conv_layer(activity, kernel, local_beside, local_turns, gather_rims):
    length = 4 * P_SIZE - 4
    cycle_vals = jnp.take(activity, cycle_table(P_SIZE), axis=2)
    extended = gather_rims(cycle_vals)
    heading, anchor = border_tables(P_SIZE)
    near_tile = jnp.take(local_beside, heading, axis=1)
    near_turn = jnp.take(local_turns, heading, axis=1)
    source = near_tile * length + jnp.remainder(anchor[None, :] - near_turn * (P_SIZE - 1), length)
    flat_cycles = extended.reshape(extended.shape[0], -1)
    border = jnp.take(flat_cycles, source.reshape(-1), axis=1)
    border = border.reshape(activity.shape[0], activity.shape[1], 4 * P_SIZE + 4)
    joined = jnp.concatenate([activity, border], axis=2)
    padded = jnp.take(joined, layout_table(P_SIZE), axis=2)
    padded_side = P_SIZE + 2
    stretch = P_SIZE * padded_side - 2
    summed = None
    for tap_index in range(9):
        offset = padded_side + 1 + (tap_index // 3 - 1) * padded_side + (tap_index % 3 - 1)
        window = padded[:, :, offset : offset + stretch]
        partial_sum = jnp.einsum(
            "oc,ctq->otq", kernel[tap_index], window, preferred_element_type=jnp.float32
        )
        summed = partial_sum if summed is None else summed + partial_sum
    summed = jnp.pad(summed, ((0, 0), (0, 0), (0, 2)))
    summed = summed.reshape(summed.shape[0], summed.shape[1], P_SIZE, padded_side)[:, :, :, :P_SIZE]
    summed = summed.reshape(summed.shape[0], summed.shape[1], P_SIZE * P_SIZE)
    return jax.nn.gelu(summed, approximate=False).astype(jnp.bfloat16)


def on_device(
    analysis,
    send_rows,
    send_count,
    corner_slot,
    corner_weight,
    beside,
    quarter_turns,
    kernel_one,
    kernel_two,
    kernel_three,
):
    shards = lax.axis_size("tile")
    groups = lax.axis_size("chan")
    tiles_here = corner_slot.shape[1]
    near_count = send_rows.shape[1]
    capacity = send_rows.shape[2]
    channels_here = analysis.shape[0]
    total_tiles = tiles_here * shards
    slot_order = jnp.arange(capacity)
    blocks = []
    for offset_index in range(near_count):
        rows_list = send_rows[0, offset_index]
        count_here = send_count[0, offset_index]
        source_block = analysis
        if offset_index != REACH:
            packed = jnp.concatenate([rows_list, count_here[None]])
            packed = from_behind(packed, "tile", offset_index - REACH)
            rows_list = packed[:capacity]
            count_here = packed[capacity]
            source_block = from_behind(analysis, "tile", offset_index - REACH)
        piece = jnp.take(source_block, rows_list, axis=1)
        piece = jnp.where(slot_order[None, :] < count_here, piece, jnp.zeros((), piece.dtype))
        blocks.append(piece)
    arrived = jnp.concatenate(blocks, axis=1)
    values = jnp.take(arrived, corner_slot.reshape(-1), axis=1)
    values = values.reshape(channels_here, 4, tiles_here, corner_slot.shape[2]).astype(jnp.float32)
    regridded = jnp.sum(values * corner_weight[None], axis=1).astype(jnp.bfloat16)
    per_group = tiles_here // groups
    activity = lax.all_to_all(regridded, "chan", split_axis=1, concat_axis=0, tiled=True)
    kernels = (
        lax.all_gather(kernel_one, "chan", axis=1, tiled=True),
        lax.all_gather(kernel_two, "chan", axis=1, tiled=True),
        lax.all_gather(kernel_three, "chan", axis=1, tiled=True),
    )
    first_tile = lax.axis_index(("tile", "chan")) * per_group
    near_beside = lax.dynamic_slice_in_dim(beside, lax.axis_index("chan") * per_group, per_group, 0)
    near_turns = lax.dynamic_slice_in_dim(
        quarter_turns, lax.axis_index("chan") * per_group, per_group, 0
    )
    local_beside = jnp.remainder(near_beside - first_tile + REACH, total_tiles)

    def joined_rims(cycle_vals):
        return extended_2(cycle_vals, ((("tile", "chan"), 1),), REACH)

    for kernel in kernels:
        activity = conv_layer(activity, kernel, local_beside, near_turns, joined_rims)
    result = lax.all_to_all(activity, "chan", split_axis=0, concat_axis=1, tiled=True)
    return result


def solution(mesh):
    return jax.shard_map(
        on_device,
        mesh=mesh,
        in_specs=(
            P("chan", "tile"),
            P("tile", None, None),
            P("tile", None),
            P(None, "tile", None),
            P(None, "tile", None),
            P("tile", None),
            P("tile", None),
            P(None, "chan", None),
            P(None, "chan", None),
            P(None, "chan", None),
        ),
        out_specs=P("chan", "tile", None),
        check_vma=False,
    )
```

profile of v0, /device:TPU:2, one launch (start us, length us, event | category | flops | bytes accessed | tf_op | source)
XLA Modules:
  0.0 374.5 jit_solution(5830040270725615998)
XLA Ops:
  0.0 13.1 %collective-permute-start.1 = (bf16[8,8192]{1,0:T(8,128)(2,1)}, bf16[8,8192]{1,0:T(8,128)(2,1)S(1)}, u32[]{:S(2)}, u32[]{:S(2)}) collective-permute-start(bf16[8,8192]{1,0:T(8,128)(2,1)} %param.32), channel_id=1, source_target_pairs={{0,496},{8,504},{16,0},{24,8},{32,16},{40,24},{48,32},{56,40},{64,... | collective-permute-start | bytes 393224 | tf_op jit(solution)/shard_map/ppermute | solution.py:14
  13.1 2.5 collective-permute-start.3
  15.6 1.9 collective-permute-start.5
  17.5 4.0 %collective-permute-start.7 = (bf16[8,8192]{1,0:T(8,128)(2,1)}, bf16[8,8192]{1,0:T(8,128)(2,1)S(1)}, u32[]{:S(2)}, u32[]{:S(2)}) collective-permute-start(bf16[8,8192]{1,0:T(8,128)(2,1)} %param.32), channel_id=1, source_target_pairs={{0,16},{8,24},{16,32},{24,40},{32,48},{40,56},{48,64},{56,72},{64,... | collective-permute-start | bytes 393224 | tf_op jit(solution)/shard_map/ppermute | solution.py:14
  21.6 1.5 fusion.74
  24.3 5.4 %collective-permute-start = (s32[129]{0:T(256)S(1)}, s32[129]{0:T(256)S(1)}, u32[]{:S(2)}, u32[]{:S(2)}) collective-permute-start(s32[129]{0:T(256)S(1)} %pad_add_fusion), channel_id=1, source_target_pairs={{0,496},{8,504},{16,0},{24,8},{32,16},{40,24},{48,32},{56,40},{64,... | collective-permute-start | bytes 1556 | tf_op jit(solution)/shard_map/ppermute | solution.py:14
  39.0 1.8 copy.262
  41.5 4.6 %collective-permute-start.2 = (s32[129]{0:T(256)S(1)}, s32[129]{0:T(256)S(1)}, u32[]{:S(2)}, u32[]{:S(2)}) collective-permute-start(s32[129]{0:T(256)S(1)} %pad_add_fusion.1), channel_id=1, source_target_pairs={{0,504},{8,0},{16,8},{24,16},{32,24},{40,32},{48,40},{56,48},{64,5... | collective-permute-start | bytes 1556 | tf_op jit(solution)/shard_map/ppermute | solution.py:14
  47.4 4.1 %collective-permute-start.4 = (s32[129]{0:T(256)S(1)}, s32[129]{0:T(256)S(1)}, u32[]{:S(2)}, u32[]{:S(2)}) collective-permute-start(s32[129]{0:T(256)S(1)} %pad_add_fusion.2), channel_id=1, source_target_pairs={{0,8},{8,16},{16,24},{24,32},{32,40},{40,48},{48,56},{56,64},{64,7... | collective-permute-start | bytes 1556 | tf_op jit(solution)/shard_map/ppermute | solution.py:14
  52.7 3.2 collective-permute-done.4
  55.9 1.9 collective-permute-start.6
  59.0 6.0 %collective-permute-done.6 = s32[129]{0:T(256)S(1)} collective-permute-done((s32[129]{0:T(256)S(1)}, s32[129]{0:T(256)S(1)}, u32[]{:S(2)}, u32[]{:S(2)}) %collective-permute-start.6) | collective-permute-done | bytes 548 | tf_op jit(solution)/shard_map/ppermute | solution.py:14
  73.7 114.2 %gather_fusion = bf16[32768,8]{1,0:T(8,128)(2,1)} fusion(bf16[8,640]{0,1:T(8,128)(2,1)S(1)} %fusion.60, s32[32768]{0:T(1024)S(1)} %broadcast_clamp_fusion), kind=kCustom, calls=%fused_computation.13 | custom fusion | bytes 1179648 | tf_op jit(solution)/shard_map/jit(_take)/gather | solution.py:153
  187.9 13.0 %multiply_reduce_fusion = bf16[8,32,256]{0,2,1:T(8,128)(2,1)S(1)} fusion(f32[4,32,256]{2,1,0:T(8,128)S(1)} %copy-done.1, bf16[8,4,32,256]{0,3,2,1:T(8,128)(2,1)} %bitcast.254, pred[4,32,256]{2,1,0:T(8,128)(4,1)S(1)} %compare_and_fusion), kind=kLoop, calls=%fused_computation.17 | loop fusion | flops 983040 | bytes 819200 | tf_op jit(solution)/shard_map/reduce_sum | solution.py:155
  202.5 5.9 %all-to-all-start = ((bf16[8,32,256]{2,0,1:T(8,128)(2,1)}), bf16[8,32,256]{2,0,1:T(8,128)(2,1)S(1)}, u32[]{:S(2)}, u32[]{:S(2)}) async-start(bf16[8,32,256]{2,0,1:T(8,128)(2,1)} %copy.266), calls=%async_computation | async-start | bytes 262144 | tf_op jit(solution)/shard_map/all_to_all | solution.py:157
  208.5 5.2 %all-to-all-done = bf16[8,32,256]{2,0,1:T(8,128)(2,1)S(1)} async-done(((bf16[8,32,256]{2,0,1:T(8,128)(2,1)}), bf16[8,32,256]{2,0,1:T(8,128)(2,1)S(1)}, u32[]{:S(2)}, u32[]{:S(2)}) %all-to-all-start) | async-done | bytes 131104 | tf_op jit(solution)/shard_map/all_to_all | solution.py:157
  214.6 2.6 collective-permute-start.8
  217.3 5.3 %collective-permute-start.9 = (bf16[64,2,60]{0,1,2:T(2,128)(2,1)S(1)}, bf16[64,2,60]{0,1,2:T(2,128)(2,1)S(1)}, u32[]{:S(2)}, u32[]{:S(2)}) collective-permute-start(bf16[64,2,60]{0,1,2:T(2,128)(2,1)S(1)} %get-tuple-element.33), channel_id=1, source_target_pairs={{1,0},{2,1},{3,2},{4,3},{5,4},{6,5},{7,6},{8,7},{9,8},{10,9},{11,1... | collective-permute-start | bytes 46088 | tf_op jit(solution)/shard_map/ppermute | solution.py:25
  222.6 29.0 %all_gather.9 = bf16[9,128,64]{2,1,0:T(8,128)(2,1)S(1)} all-gather(bf16[9,16,64]{2,1,0:T(8,128)(2,1)S(1)} %copy-done.2), channel_id=1, replica_groups=mesh['tile'=64,'chan'=8] {'chan'}, dimensions={1}, use_global_device_ids=true | all-gather | bytes 165888 | tf_op jit(solution)/shard_map/all_gather | solution.py:159
  251.9 1.4 gather_fusion.2
  253.8 2.0 gather_fusion.3
  263.0 1.9 collective-permute-start.10
  264.9 6.0 %collective-permute-start.11 = (bf16[128,2,60]{0,1,2:T(2,128)(2,1)S(1)}, bf16[128,2,60]{0,1,2:T(2,128)(2,1)S(1)}, u32[]{:S(2)}, u32[]{:S(2)}) collective-permute-start(bf16[128,2,60]{0,1,2:T(2,128)(2,1)S(1)} %get-tuple-element.31), channel_id=1, source_target_pairs={{1,0},{2,1},{3,2},{4,3},{5,4},{6,5},{7,6},{8,7},{9,8},{10,9},{11,1... | collective-permute-start | bytes 92168 | tf_op jit(solution)/shard_map/ppermute | solution.py:25
  270.9 31.7 %all_gather.10 = bf16[9,128,128]{2,1,0:T(8,128)(2,1)S(1)} all-gather(bf16[9,16,128]{2,1,0:T(8,128)(2,1)S(1)} %copy-done.3), channel_id=1, replica_groups=mesh['tile'=64,'chan'=8] {'chan'}, dimensions={1}, use_global_device_ids=true | all-gather | bytes 331776 | tf_op jit(solution)/shard_map/all_gather | solution.py:160
  302.8 1.4 gather_fusion.12
  304.8 2.0 gather_fusion.13
  312.4 2.1 collective-permute-start.12
  314.4 5.9 %collective-permute-start.13 = (bf16[128,2,60]{0,1,2:T(2,128)(2,1)S(1)}, bf16[128,2,60]{0,1,2:T(2,128)(2,1)S(1)}, u32[]{:S(2)}, u32[]{:S(2)}) collective-permute-start(bf16[128,2,60]{0,1,2:T(2,128)(2,1)S(1)} %get-tuple-element.29), channel_id=1, source_target_pairs={{1,0},{2,1},{3,2},{4,3},{5,4},{6,5},{7,6},{8,7},{9,8},{10,9},{11,1... | collective-permute-start | bytes 92168 | tf_op jit(solution)/shard_map/ppermute | solution.py:25
  320.3 31.7 %all_gather.11 = bf16[9,128,128]{2,1,0:T(8,128)(2,1)S(1)} all-gather(bf16[9,16,128]{2,1,0:T(8,128)(2,1)S(1)} %copy-done.4), channel_id=1, replica_groups=mesh['tile'=64,'chan'=8] {'chan'}, dimensions={1}, use_global_device_ids=true | all-gather | bytes 331776 | tf_op jit(solution)/shard_map/all_gather | solution.py:161
  352.3 1.4 gather_fusion.15
  354.2 2.0 gather_fusion.16
  361.1 12.5 %all_to_all.36 = bf16[128,4,256]{2,1,0:T(4,128)(2,1)S(1)} all-to-all(bf16[128,4,256]{2,1,0:T(4,128)(2,1)S(1)} %copy.324), channel_id=1, replica_groups=mesh['tile'=64,'chan'=8] {'chan'}, dimensions={0} | all-to-all | bytes 524288 | tf_op jit(solution)/shard_map/all_to_all | solution.py:175
  (173 shorter events, 46.0 us)
Async XLA Ops:
  0.0 34.5 %copy-start = (s32[32,8]{0,1:T(8,128)S(1)}, s32[32,8]{0,1:T(8,128)}, u32[]{:S(2)}) copy-start(s32[32,8]{0,1:T(8,128)} %param.38) | copy-start | bytes 3076
  0.0 66.1 %collective-permute-start.1 = (bf16[8,8192]{1,0:T(8,128)(2,1)}, bf16[8,8192]{1,0:T(8,128)(2,1)S(1)}, u32[]{:S(2)}, u32[]{:S(2)}) collective-permute-start(bf16[8,8192]{1,0:T(8,128)(2,1)} %param.32), channel_id=1, source_target_pairs={{0,496},{8,504},{16,0},{24,8},{32,16},{40,24},{48,32},{56,40},{64,... | collective-permute-start | bytes 393224 | tf_op jit(solution)/shard_map/ppermute | solution.py:14
  13.1 54.8 %collective-permute-start.3 = (bf16[8,8192]{1,0:T(8,128)(2,1)}, bf16[8,8192]{1,0:T(8,128)(2,1)S(1)}, u32[]{:S(2)}, u32[]{:S(2)}) collective-permute-start(bf16[8,8192]{1,0:T(8,128)(2,1)} %param.32), channel_id=1, source_target_pairs={{0,504},{8,0},{16,8},{24,16},{32,24},{40,32},{48,40},{56,48},{64,5... | collective-permute-start | bytes 393224 | tf_op jit(solution)/shard_map/ppermute | solution.py:14
  15.6 54.0 %collective-permute-start.5 = (bf16[8,8192]{1,0:T(8,128)(2,1)}, bf16[8,8192]{1,0:T(8,128)(2,1)S(1)}, u32[]{:S(2)}, u32[]{:S(2)}) collective-permute-start(bf16[8,8192]{1,0:T(8,128)(2,1)} %param.32), channel_id=1, source_target_pairs={{0,8},{8,16},{16,24},{24,32},{32,40},{40,48},{48,56},{56,64},{64,7... | collective-permute-start | bytes 393224 | tf_op jit(solution)/shard_map/ppermute | solution.py:14
  17.5 53.8 %collective-permute-start.7 = (bf16[8,8192]{1,0:T(8,128)(2,1)}, bf16[8,8192]{1,0:T(8,128)(2,1)S(1)}, u32[]{:S(2)}, u32[]{:S(2)}) collective-permute-start(bf16[8,8192]{1,0:T(8,128)(2,1)} %param.32), channel_id=1, source_target_pairs={{0,16},{8,24},{16,32},{24,40},{32,48},{40,56},{48,64},{56,72},{64,... | collective-permute-start | bytes 393224 | tf_op jit(solution)/shard_map/ppermute | solution.py:14
  24.3 17.2 %collective-permute-start = (s32[129]{0:T(256)S(1)}, s32[129]{0:T(256)S(1)}, u32[]{:S(2)}, u32[]{:S(2)}) collective-permute-start(s32[129]{0:T(256)S(1)} %pad_add_fusion), channel_id=1, source_target_pairs={{0,496},{8,504},{16,0},{24,8},{32,16},{40,24},{48,32},{56,40},{64,... | collective-permute-start | bytes 1556 | tf_op jit(solution)/shard_map/ppermute | solution.py:14
  41.5 5.9 %collective-permute-start.2 = (s32[129]{0:T(256)S(1)}, s32[129]{0:T(256)S(1)}, u32[]{:S(2)}, u32[]{:S(2)}) collective-permute-start(s32[129]{0:T(256)S(1)} %pad_add_fusion.1), channel_id=1, source_target_pairs={{0,504},{8,0},{16,8},{24,16},{32,24},{40,32},{48,40},{56,48},{64,5... | collective-permute-start | bytes 1556 | tf_op jit(solution)/shard_map/ppermute | solution.py:14
  47.4 8.5 %collective-permute-start.4 = (s32[129]{0:T(256)S(1)}, s32[129]{0:T(256)S(1)}, u32[]{:S(2)}, u32[]{:S(2)}) collective-permute-start(s32[129]{0:T(256)S(1)} %pad_add_fusion.2), channel_id=1, source_target_pairs={{0,8},{8,16},{16,24},{24,32},{32,40},{40,48},{48,56},{56,64},{64,7... | collective-permute-start | bytes 1556 | tf_op jit(solution)/shard_map/ppermute | solution.py:14
  55.9 9.1 %collective-permute-start.6 = (s32[129]{0:T(256)S(1)}, s32[129]{0:T(256)S(1)}, u32[]{:S(2)}, u32[]{:S(2)}) collective-permute-start(s32[129]{0:T(256)S(1)} %pad_add_fusion.3), channel_id=1, source_target_pairs={{0,16},{8,24},{16,32},{24,40},{32,48},{40,56},{48,64},{56,72},{64,... | collective-permute-start | bytes 1556 | tf_op jit(solution)/shard_map/ppermute | solution.py:14
  73.7 114.3 %copy-start.1 = (f32[4,32,256]{2,1,0:T(8,128)S(1)}, f32[4,32,256]{2,1,0:T(8,128)}, u32[]{:S(2)}) copy-start(f32[4,32,256]{2,1,0:T(8,128)} %param.36) | copy-start | bytes 393220
  200.9 7.6 %copy-start.6 = (s32[60]{0:T(128)S(1)}, s32[60]{0:T(128)}, u32[]{:S(2)}) copy-start(s32[60]{0:T(128)} %constant.232.clone) | copy-start | bytes 724
  200.9 7.6 %copy-start.5 = (s32[324]{0:T(512)S(1)}, s32[324]{0:T(512)}, u32[]{:S(2)}) copy-start(s32[324]{0:T(512)} %constant.235.clone) | copy-start | bytes 3892
  200.9 21.6 %copy-start.2 = (bf16[9,16,64]{2,1,0:T(8,128)(2,1)S(1)}, bf16[9,16,64]{2,1,0:T(8,128)(2,1)}, u32[]{:S(2)}) copy-start(bf16[9,16,64]{2,1,0:T(8,128)(2,1)} %param.39) | copy-start | bytes 55300
  202.5 11.2 %all-to-all-start = ((bf16[8,32,256]{2,0,1:T(8,128)(2,1)}), bf16[8,32,256]{2,0,1:T(8,128)(2,1)S(1)}, u32[]{:S(2)}, u32[]{:S(2)}) async-start(bf16[8,32,256]{2,0,1:T(8,128)(2,1)} %copy.266), calls=%async_computation | async-start | bytes 262144 | tf_op jit(solution)/shard_map/all_to_all | solution.py:157
  214.6 37.1 %collective-permute-start.8 = (bf16[64,2,60]{0,1,2:T(2,128)(2,1)S(1)}, bf16[64,2,60]{0,1,2:T(2,128)(2,1)S(1)}, u32[]{:S(2)}, u32[]{:S(2)}) collective-permute-start(bf16[64,2,60]{0,1,2:T(2,128)(2,1)S(1)} %get-tuple-element.32), channel_id=1, source_target_pairs={{0,1},{1,2},{2,3},{3,4},{4,5},{5,6},{6,7},{7,8},{8,9},{9,10},{10,1... | collective-permute-start | bytes 46088 | tf_op jit(solution)/shard_map/ppermute | solution.py:24
  217.3 34.5 %collective-permute-start.9 = (bf16[64,2,60]{0,1,2:T(2,128)(2,1)S(1)}, bf16[64,2,60]{0,1,2:T(2,128)(2,1)S(1)}, u32[]{:S(2)}, u32[]{:S(2)}) collective-permute-start(bf16[64,2,60]{0,1,2:T(2,128)(2,1)S(1)} %get-tuple-element.33), channel_id=1, source_target_pairs={{1,0},{2,1},{3,2},{4,3},{5,4},{6,5},{7,6},{8,7},{9,8},{10,9},{11,1... | collective-permute-start | bytes 46088 | tf_op jit(solution)/shard_map/ppermute | solution.py:25
  260.5 10.4 %copy-start.3 = (bf16[9,16,128]{2,1,0:T(8,128)(2,1)S(1)}, bf16[9,16,128]{2,1,0:T(8,128)(2,1)}, u32[]{:S(2)}) copy-start(bf16[9,16,128]{2,1,0:T(8,128)(2,1)} %param.40) | copy-start | bytes 110596
  263.0 39.7 %collective-permute-start.10 = (bf16[128,2,60]{0,1,2:T(2,128)(2,1)S(1)}, bf16[128,2,60]{0,1,2:T(2,128)(2,1)S(1)}, u32[]{:S(2)}, u32[]{:S(2)}) collective-permute-start(bf16[128,2,60]{0,1,2:T(2,128)(2,1)S(1)} %get-tuple-element.30), channel_id=1, source_target_pairs={{0,1},{1,2},{2,3},{3,4},{4,5},{5,6},{6,7},{7,8},{8,9},{9,10},{10,1... | collective-permute-start | bytes 92168 | tf_op jit(solution)/shard_map/ppermute | solution.py:24
  264.9 37.8 %collective-permute-start.11 = (bf16[128,2,60]{0,1,2:T(2,128)(2,1)S(1)}, bf16[128,2,60]{0,1,2:T(2,128)(2,1)S(1)}, u32[]{:S(2)}, u32[]{:S(2)}) collective-permute-start(bf16[128,2,60]{0,1,2:T(2,128)(2,1)S(1)} %get-tuple-element.31), channel_id=1, source_target_pairs={{1,0},{2,1},{3,2},{4,3},{5,4},{6,5},{7,6},{8,7},{9,8},{10,9},{11,1... | collective-permute-start | bytes 92168 | tf_op jit(solution)/shard_map/ppermute | solution.py:25
  309.9 10.4 %copy-start.4 = (bf16[9,16,128]{2,1,0:T(8,128)(2,1)S(1)}, bf16[9,16,128]{2,1,0:T(8,128)(2,1)}, u32[]{:S(2)}) copy-start(bf16[9,16,128]{2,1,0:T(8,128)(2,1)} %param.41) | copy-start | bytes 110596
  312.4 39.7 %collective-permute-start.12 = (bf16[128,2,60]{0,1,2:T(2,128)(2,1)S(1)}, bf16[128,2,60]{0,1,2:T(2,128)(2,1)S(1)}, u32[]{:S(2)}, u32[]{:S(2)}) collective-permute-start(bf16[128,2,60]{0,1,2:T(2,128)(2,1)S(1)} %get-tuple-element.28), channel_id=1, source_target_pairs={{0,1},{1,2},{2,3},{3,4},{4,5},{5,6},{6,7},{7,8},{8,9},{9,10},{10,1... | collective-permute-start | bytes 92168 | tf_op jit(solution)/shard_map/ppermute | solution.py:24
  314.4 37.7 %collective-permute-start.13 = (bf16[128,2,60]{0,1,2:T(2,128)(2,1)S(1)}, bf16[128,2,60]{0,1,2:T(2,128)(2,1)S(1)}, u32[]{:S(2)}, u32[]{:S(2)}) collective-permute-start(bf16[128,2,60]{0,1,2:T(2,128)(2,1)S(1)} %get-tuple-element.29), channel_id=1, source_target_pairs={{1,0},{2,1},{3,2},{4,3},{5,4},{6,5},{7,6},{8,7},{9,8},{10,9},{11,1... | collective-permute-start | bytes 92168 | tf_op jit(solution)/shard_map/ppermute | solution.py:25
where the time goes:
time: 375 us
  local copies, waits for them, and re-layouts  150 us (40%)
  blocking collectives  105 us (28%)
  starting transfers between devices  67.3 us (18%)
  other arithmetic  28.4 us (8%)
  waiting for transfers between devices  14.5 us (4%)
  matrix products  7.92 us (2%)
    gather x1, local copies, waits for them, and re-layouts, on_device(): values = jnp.take(arrived, corner_slot.reshape(-1), axis=1)  114 us
    ppermute x8, starting transfers between devices, from_behind(): return lax.ppermute(value, axis, pairs)  37.5 us
    all_gather x1, blocking collectives, on_device(): lax.all_gather(kernel_three, 'chan', axis=1, tiled=True)  31.7 us
    all_gather x1, blocking collectives, on_device(): lax.all_gather(kernel_two, 'chan', axis=1, tiled=True)  31.7 us
    all_gather x1, blocking collectives, on_device(): lax.all_gather(kernel_one, 'chan', axis=1, tiled=True)  29 us
    ppermute x3, starting transfers between devices, extended_2(): after = lax.ppermute(initial, axis, down)  17.2 us
    reduce_sum x1, other arithmetic, on_device(): jnp.sum(values * corner_weight[None], axis=1).astype(jnp.bfloat16)  13 us
    all_to_all x1, blocking collectives, on_device(): lax.all_to_all(activity, 'chan', split_axis=0, concat_axis=1, tiled=True)  12.5 us
  transfers between devices with their start and end apart: 15, of which 4 were waited for; matrix products, arithmetic and copies ran while one was open for 7% of the time, Pallas kernels for 0%

commit v1 on v0

--- a/solution.py
+++ b/solution.py
@@ -133,38 +133,46 @@
     near_count = send_rows.shape[1]
     capacity = send_rows.shape[2]
     channels_here = analysis.shape[0]
+    pixels = corner_slot.shape[2]
     total_tiles = tiles_here * shards
+    per_group = tiles_here // groups
+    widths = [kernel_one.shape[2], kernel_two.shape[2], kernel_three.shape[2]]
+    joined_kernels = jnp.concatenate([kernel_one, kernel_two, kernel_three], axis=2)
+    joined_kernels = lax.all_gather(joined_kernels, "chan", axis=1, tiled=True)
+    kernels = []
+    low = 0
+    for width in widths:
+        kernels.append(joined_kernels[:, :, low : low + width])
+        low += width
     slot_order = jnp.arange(capacity)
+    rows_list = send_rows[0].reshape(-1)
+    piece = jnp.take(analysis, rows_list, axis=1).reshape(channels_here, near_count, capacity)
+    is_live = slot_order[None, :] < send_count[0][:, None]
+    piece = jnp.where(is_live[None], piece, jnp.zeros((), piece.dtype))
     blocks = []
     for offset_index in range(near_count):
-        rows_list = send_rows[0, offset_index]
-        count_here = send_count[0, offset_index]
-        source_block = analysis
+        block = piece[:, offset_index]
         if offset_index != REACH:
-            packed = jnp.concatenate([rows_list, count_here[None]])
-            packed = from_behind(packed, "tile", offset_index - REACH)
-            rows_list = packed[:capacity]
-            count_here = packed[capacity]
-            source_block = from_behind(analysis, "tile", offset_index - REACH)
-        piece = jnp.take(source_block, rows_list, axis=1)
-        piece = jnp.where(slot_order[None, :] < count_here, piece, jnp.zeros((), piece.dtype))
-        blocks.append(piece)
-    arrived = jnp.concatenate(blocks, axis=1)
-    values = jnp.take(arrived, corner_slot.reshape(-1), axis=1)
-    values = values.reshape(channels_here, 4, tiles_here, corner_slot.shape[2]).astype(jnp.float32)
-    regridded = jnp.sum(values * corner_weight[None], axis=1).astype(jnp.bfloat16)
-    per_group = tiles_here // groups
-    activity = lax.all_to_all(regridded, "chan", split_axis=1, concat_axis=0, tiled=True)
-    kernels = (
-        lax.all_gather(kernel_one, "chan", axis=1, tiled=True),
-        lax.all_gather(kernel_two, "chan", axis=1, tiled=True),
-        lax.all_gather(kernel_three, "chan", axis=1, tiled=True),
-    )
+            block = from_behind(block, "tile", offset_index - REACH)
+        blocks.append(block)
+    arrived = jnp.stack(blocks, axis=1).reshape(channels_here, near_count * capacity)
+    arrived = lax.all_gather(arrived, "chan", axis=0, tiled=True)
+    group_index = lax.axis_index("chan")
+    my_slots = lax.dynamic_slice_in_dim(corner_slot, group_index * per_group, per_group, 1)
+    my_weights = lax.dynamic_slice_in_dim(corner_weight, group_index * per_group, per_group, 1)
+    my_slots = my_slots.reshape(my_slots.shape[0], per_group * pixels)
+    my_weights = my_weights.reshape(my_weights.shape[0], per_group * pixels)
+    slot_ids = jnp.arange(near_count * capacity)
+    summed = None
+    for corner in range(my_slots.shape[0]):
+        one_hot = (slot_ids[:, None] == my_slots[corner][None, :]).astype(arrived.dtype)
+        picked = jnp.dot(arrived, one_hot, preferred_element_type=jnp.float32)
+        term = picked * my_weights[corner][None, :]
+        summed = term if summed is None else summed + term
+    activity = summed.astype(jnp.bfloat16).reshape(arrived.shape[0], per_group, pixels)
     first_tile = lax.axis_index(("tile", "chan")) * per_group
-    near_beside = lax.dynamic_slice_in_dim(beside, lax.axis_index("chan") * per_group, per_group, 0)
-    near_turns = lax.dynamic_slice_in_dim(
-        quarter_turns, lax.axis_index("chan") * per_group, per_group, 0
-    )
+    near_beside = lax.dynamic_slice_in_dim(beside, group_index * per_group, per_group, 0)
+    near_turns = lax.dynamic_slice_in_dim(quarter_turns, group_index * per_group, per_group, 0)
     local_beside = jnp.remainder(near_beside - first_tile + REACH, total_tiles)
 
     def joined_rims(cycle_vals):

time: 375 us -> 178 us (0.47)
  local copies, waits for them, and re-layouts: 150 us -> 25.4 us
  blocking collectives: 105 us -> 76 us
  starting transfers between devices: 67.3 us -> 45.7 us
  other arithmetic: 28.4 us -> 6.83 us
  waiting for transfers between devices: 14.5 us -> 9.64 us
  matrix products: 7.92 us -> 12.5 us
    gather x6 -> x2, local copies, waits for them, and re-layouts: 118 us -> 2.09 us  [on_device(): jnp.take(analysis, rows_list, axis=1)]
    all_gather x3 -> x2, blocking collectives: 92.5 us -> 58.1 us  [the longest x1 29.9 us: on_device(): joined_kernels = lax.all_gather(joined_kernels, 'chan', axis=1, tiled=True)]
    ppermute x8 -> x4, starting transfers between devices: 37.5 us -> 20.9 us  [from_behind(): return lax.ppermute(value, axis, pairs)]
    reduce_sum x1 -> x0, other arithmetic: 13 us -> none  [on_device(): jnp.sum(values * corner_weight[None], axis=1).astype(jnp.bfloat16)]
    all_to_all x1 -> x0, starting transfers between devices: 5.93 us -> none  [on_device(): lax.all_to_all(regridded, 'chan', split_axis=1, concat_axis=0, tiled=True)]
    all_to_all x1, blocking collectives: 12.5 us -> 17.9 us  [on_device(): lax.all_to_all(activity, 'chan', split_axis=0, concat_axis=1, tiled=True)]
    all_to_all x1 -> x0, waiting for transfers between devices: 5.2 us -> none  [on_device(): lax.all_to_all(regridded, 'chan', split_axis=1, concat_axis=0, tiled=True)]
    ppermute x3, waiting for transfers between devices: 0.01 us -> 4.07 us  [extended_2(): after = lax.ppermute(initial, axis, down)]
  transfers between devices with their start and end apart: 15 -> 10, of which waited for: 4 -> 5; matrix products, arithmetic and copies ran while one was open for 7% -> 2% of each run, Pallas kernels for 0% -> 0%
where the time goes in v1:
time: 178 us; the launch traced here: 177 us
  blocking collectives  76 us (43%)
  starting transfers between devices  45.7 us (26%)
  local copies, waits for them, and re-layouts  25.4 us (14%)
  matrix products  12.5 us (7%)
  waiting for transfers between devices  9.64 us (5%)
  other arithmetic  6.83 us (4%)
    all_gather x1, blocking collectives, on_device(): joined_kernels = lax.all_gather(joined_kernels, 'chan', axis=1, tiled=True)  29.9 us
    all_gather x1, blocking collectives, on_device(): arrived = lax.all_gather(arrived, 'chan', axis=0, tiled=True)  28.2 us
    ppermute x4, starting transfers between devices, from_behind(): return lax.ppermute(value, axis, pairs)  20.9 us
    all_to_all x1, blocking collectives, on_device(): lax.all_to_all(activity, 'chan', split_axis=0, concat_axis=1, tiled=True)  17.9 us
    ppermute x3, starting transfers between devices, extended_2(): after = lax.ppermute(initial, axis, down)  16.6 us
    dot_general x27, matrix products, conv_layer(): jnp.einsum('oc,ctq->otq', kernel[tap_index], window, preferred_element_ty...  10.1 us
    ppermute x3, starting transfers between devices, extended_2(): before = lax.ppermute(last, axis, up)  8.27 us
    gather x6, local copies, waits for them, and re-layouts, conv_layer(): padded = jnp.take(joined, layout_table(P_SIZE), axis=2)  6.41 us
  transfers between devices with their start and end apart: 10, of which 5 were waited for; matrix products, arithmetic and copies ran while one was open for 2% of the time, Pallas kernels for 0%

profile of v1, /device:TPU:2, one launch (start us, length us, event | category | flops | bytes accessed | tf_op | source)
XLA Modules:
  0.0 177.2 jit_solution(4643471819461875339)
XLA Ops:
  0.1 0.8 fusion.74
  0.8 0.8 iota_compare_fusion.24
  1.6 1.9 %copy.243 = bf16[8,8192]{0,1:T(8,128)(2,1)S(1)} copy(bf16[8,8192]{1,0:T(8,128)(2,1)} %param.30) | data formatting | bytes 262144 | tf_op args[0]
  3.5 2.0 %gather_fusion = bf16[640,8]{1,0:T(8,128)(2,1)S(1)} fusion(bf16[8,8192]{0,1:T(8,128)(2,1)S(1)} %copy.243, s32[1024]{0:T(1024)S(1)} %pad_clamp_fusion.5), kind=kCustom, calls=%fused_computation.8 | custom fusion | bytes 23040 | tf_op jit(solution)/shard_map/jit(_take)/gather | solution.py:149
  5.6 13.0 %collective-permute-start = (bf16[8,128]{1,0:T(8,128)(2,1)S(1)}, bf16[8,128]{1,0:T(8,128)(2,1)S(1)}, u32[]{:S(2)}, u32[]{:S(2)}) collective-permute-start(bf16[8,128]{1,0:T(8,128)(2,1)S(1)} %get-tuple-element.35), channel_id=1, source_target_pairs={{0,496},{8,504},{16,0},{24,8},{32,16},{40,24},{48,32},{56,40},{64,... | collective-permute-start | bytes 6152 | tf_op jit(solution)/shard_map/ppermute | solution.py:14
  18.6 2.5 %collective-permute-start.1 = (bf16[8,128]{1,0:T(8,128)(2,1)S(1)}, bf16[8,128]{1,0:T(8,128)(2,1)S(1)}, u32[]{:S(2)}, u32[]{:S(2)}) collective-permute-start(bf16[8,128]{1,0:T(8,128)(2,1)S(1)} %get-tuple-element.34), channel_id=1, source_target_pairs={{0,504},{8,0},{16,8},{24,16},{32,24},{40,32},{48,40},{56,48},{64,5... | collective-permute-start | bytes 6152 | tf_op jit(solution)/shard_map/ppermute | solution.py:14
  24.5 29.9 %all_gather.6 = bf16[9,128,320]{2,1,0:T(8,128)(2,1)S(1)} all-gather(bf16[9,16,320]{2,1,0:T(8,128)(2,1)S(1)} %pad_maximum_fusion.6), channel_id=1, replica_groups=mesh['tile'=64,'chan'=8] {'chan'}, dimensions={1}, use_global_device_ids=true | all-gather | bytes 829440 | tf_op jit(solution)/shard_map/all_gather | solution.py:141
  54.5 1.9 %collective-permute-start.2 = (bf16[8,128]{1,0:T(8,128)(2,1)S(1)}, bf16[8,128]{1,0:T(8,128)(2,1)S(1)}, u32[]{:S(2)}, u32[]{:S(2)}) collective-permute-start(bf16[8,128]{1,0:T(8,128)(2,1)S(1)} %get-tuple-element.32), channel_id=1, source_target_pairs={{0,8},{8,16},{16,24},{24,32},{32,40},{40,48},{48,56},{56,64},{64,7... | collective-permute-start | bytes 6152 | tf_op jit(solution)/shard_map/ppermute | solution.py:14
  56.6 3.5 %collective-permute-start.3 = (bf16[8,128]{1,0:T(8,128)(2,1)S(1)}, bf16[8,128]{1,0:T(8,128)(2,1)S(1)}, u32[]{:S(2)}, u32[]{:S(2)}) collective-permute-start(bf16[8,128]{1,0:T(8,128)(2,1)S(1)} %get-tuple-element.31), channel_id=1, source_target_pairs={{0,16},{8,24},{16,32},{24,40},{32,48},{40,56},{48,64},{56,72},{64,... | collective-permute-start | bytes 6152 | tf_op jit(solution)/shard_map/ppermute | solution.py:14
  60.1 2.9 %collective-permute-done.2 = bf16[8,128]{1,0:T(8,128)(2,1)S(1)} collective-permute-done((bf16[8,128]{1,0:T(8,128)(2,1)S(1)}, bf16[8,128]{1,0:T(8,128)(2,1)S(1)}, u32[]{:S(2)}, u32[]{:S(2)}) %collective-permute-start.2) | collective-permute-done | bytes 2080 | tf_op jit(solution)/shard_map/ppermute | solution.py:14
  63.1 2.6 %collective-permute-done.3 = bf16[8,128]{1,0:T(8,128)(2,1)S(1)} collective-permute-done((bf16[8,128]{1,0:T(8,128)(2,1)S(1)}, bf16[8,128]{1,0:T(8,128)(2,1)S(1)}, u32[]{:S(2)}, u32[]{:S(2)}) %collective-permute-start.3) | collective-permute-done | bytes 2080 | tf_op jit(solution)/shard_map/ppermute | solution.py:14
  65.7 28.2 %all_gather.7 = bf16[64,640]{1,0:T(8,128)(2,1)S(1)} all-gather(bf16[8,640]{1,0:T(8,128)(2,1)S(1)} %bitcast.272), channel_id=1, replica_groups=mesh['tile'=64,'chan'=8] {'chan'}, dimensions={0}, use_global_device_ids=true | all-gather | bytes 92160 | tf_op jit(solution)/shard_map/all_gather | solution.py:159
  97.3 3.2 %collective-permute-start.4 = (bf16[64,2,60]{0,1,2:T(2,128)(2,1)S(1)}, bf16[64,2,60]{0,1,2:T(2,128)(2,1)S(1)}, u32[]{:S(2)}, u32[]{:S(2)}) collective-permute-start(bf16[64,2,60]{0,1,2:T(2,128)(2,1)S(1)} %get-tuple-element.29), channel_id=1, source_target_pairs={{0,1},{1,2},{2,3},{3,4},{4,5},{5,6},{6,7},{7,8},{8,9},{9,10},{10,1... | collective-permute-start | bytes 46088 | tf_op jit(solution)/shard_map/ppermute | solution.py:24
  100.6 4.9 %collective-permute-start.5 = (bf16[64,2,60]{0,1,2:T(2,128)(2,1)S(1)}, bf16[64,2,60]{0,1,2:T(2,128)(2,1)S(1)}, u32[]{:S(2)}, u32[]{:S(2)}) collective-permute-start(bf16[64,2,60]{0,1,2:T(2,128)(2,1)S(1)} %get-tuple-element.30), channel_id=1, source_target_pairs={{1,0},{2,1},{3,2},{4,3},{5,4},{6,5},{7,6},{8,7},{9,8},{10,9},{11,1... | collective-permute-start | bytes 46088 | tf_op jit(solution)/shard_map/ppermute | solution.py:25
  105.7 1.2 collective-permute-done.5
  107.1 1.4 gather_fusion.2
  108.9 2.0 %gather_fusion.3 = bf16[324,64,4]{1,2,0:T(4,128)(2,1)S(1)} fusion(bf16[64,4,324]{0,1,2:T(4,128)(2,1)S(1)} %pad_maximum_fusion.2, s32[1024]{0:T(1024)S(1)} %get-tuple-element.37), kind=kCustom, calls=%fused_computation.11 | custom fusion | bytes 333072 | tf_op jit(solution)/shard_map/jit(_take)/gather | solution.py:101
  116.9 1.1 fusion.18
  118.9 2.6 %collective-permute-start.6 = (bf16[128,2,60]{0,1,2:T(2,128)(2,1)S(1)}, bf16[128,2,60]{0,1,2:T(2,128)(2,1)S(1)}, u32[]{:S(2)}, u32[]{:S(2)}) collective-permute-start(bf16[128,2,60]{0,1,2:T(2,128)(2,1)S(1)} %get-tuple-element.27), channel_id=1, source_target_pairs={{0,1},{1,2},{2,3},{3,4},{4,5},{5,6},{6,7},{7,8},{8,9},{9,10},{10,1... | collective-permute-start | bytes 92168 | tf_op jit(solution)/shard_map/ppermute | solution.py:24
  121.5 5.9 %collective-permute-start.7 = (bf16[128,2,60]{0,1,2:T(2,128)(2,1)S(1)}, bf16[128,2,60]{0,1,2:T(2,128)(2,1)S(1)}, u32[]{:S(2)}, u32[]{:S(2)}) collective-permute-start(bf16[128,2,60]{0,1,2:T(2,128)(2,1)S(1)} %get-tuple-element.28), channel_id=1, source_target_pairs={{1,0},{2,1},{3,2},{4,3},{5,4},{6,5},{7,6},{8,7},{9,8},{10,9},{11,1... | collective-permute-start | bytes 92168 | tf_op jit(solution)/shard_map/ppermute | solution.py:25
  127.4 1.3 collective-permute-done.7
  128.9 1.4 gather_fusion.7
  130.9 2.0 %gather_fusion.8 = bf16[324,128,4]{1,2,0:T(4,128)(2,1)S(1)} fusion(bf16[128,4,324]{0,1,2:T(4,128)(2,1)S(1)} %copy.275, s32[1024]{0:T(1024)S(1)} %get-tuple-element.37), kind=kCustom, calls=%fused_computation.3.clone | custom fusion | bytes 664848 | tf_op jit(solution)/shard_map/jit(_take)/gather | solution.py:101
  137.0 1.1 fusion.21
  139.0 2.5 %collective-permute-start.8 = (bf16[128,2,60]{0,1,2:T(2,128)(2,1)S(1)}, bf16[128,2,60]{0,1,2:T(2,128)(2,1)S(1)}, u32[]{:S(2)}, u32[]{:S(2)}) collective-permute-start(bf16[128,2,60]{0,1,2:T(2,128)(2,1)S(1)} %get-tuple-element.25), channel_id=1, source_target_pairs={{0,1},{1,2},{2,3},{3,4},{4,5},{5,6},{6,7},{7,8},{8,9},{9,10},{10,1... | collective-permute-start | bytes 92168 | tf_op jit(solution)/shard_map/ppermute | solution.py:24
  141.5 5.8 %collective-permute-start.9 = (bf16[128,2,60]{0,1,2:T(2,128)(2,1)S(1)}, bf16[128,2,60]{0,1,2:T(2,128)(2,1)S(1)}, u32[]{:S(2)}, u32[]{:S(2)}) collective-permute-start(bf16[128,2,60]{0,1,2:T(2,128)(2,1)S(1)} %get-tuple-element.26), channel_id=1, source_target_pairs={{1,0},{2,1},{3,2},{4,3},{5,4},{6,5},{7,6},{8,7},{9,8},{10,9},{11,1... | collective-permute-start | bytes 92168 | tf_op jit(solution)/shard_map/ppermute | solution.py:25
  147.3 1.5 collective-permute-done.9
  149.0 1.4 gather_fusion.10
  151.0 2.0 %gather_fusion.11 = bf16[324,128,4]{1,2,0:T(4,128)(2,1)S(1)} fusion(bf16[128,4,324]{0,1,2:T(4,128)(2,1)S(1)} %copy.289, s32[1024]{0:T(1024)S(1)} %get-tuple-element.37), kind=kCustom, calls=%fused_computation.7.clone | custom fusion | bytes 664848 | tf_op jit(solution)/shard_map/jit(_take)/gather | solution.py:101
  157.2 1.1 fusion.24
  158.5 17.9 %all_to_all.18 = bf16[128,4,256]{2,1,0:T(4,128)(2,1)S(1)} all-to-all(bf16[128,4,256]{2,1,0:T(4,128)(2,1)S(1)} %copy.300), channel_id=1, replica_groups=mesh['tile'=64,'chan'=8] {'chan'}, dimensions={0} | all-to-all | bytes 524288 | tf_op jit(solution)/shard_map/all_to_all | solution.py:183
  176.4 0.8 copy.303
  (146 shorter events, 25.2 us)
Async XLA Ops:
  0.0 21.9 %copy-start = (s32[32,8]{0,1:T(8,128)S(1)}, s32[32,8]{0,1:T(8,128)}, u32[]{:S(2)}) copy-start(s32[32,8]{0,1:T(8,128)} %param.36) | copy-start | bytes 3076
  0.0 21.1 %copy-start.7 = (s32[68]{0:T(128)S(1)}, s32[68]{0:T(128)}, u32[]{:S(2)}) copy-start(s32[68]{0:T(128)} %constant.310) | copy-start | bytes 820
  0.0 22.7 %copy-start.6 = (s32[68]{0:T(128)S(1)}, s32[68]{0:T(128)}, u32[]{:S(2)}) copy-start(s32[68]{0:T(128)} %constant.243) | copy-start | bytes 820
  0.0 56.5 %copy-start.8 = (s32[60]{0:T(128)S(1)}, s32[60]{0:T(128)}, u32[]{:S(2)}) copy-start(s32[60]{0:T(128)} %constant.221.clone) | copy-start | bytes 724
  0.0 21.1 %copy-start.4 = (s32[32,8]{0,1:T(8,128)S(1)}, s32[32,8]{0,1:T(8,128)}, u32[]{:S(2)}) copy-start(s32[32,8]{0,1:T(8,128)} %param.35) | copy-start | bytes 3076
  0.0 24.3 %copy-start.3 = (bf16[9,16,64]{2,1,0:T(8,128)(2,1)S(1)}, bf16[9,16,64]{2,1,0:T(8,128)(2,1)}, u32[]{:S(2)}) copy-start(bf16[9,16,64]{2,1,0:T(8,128)(2,1)} %param.37) | copy-start | bytes 55300
  0.0 24.3 %copy-start.2 = (bf16[9,16,128]{2,1,0:T(8,128)(2,1)S(1)}, bf16[9,16,128]{2,1,0:T(8,128)(2,1)}, u32[]{:S(2)}) copy-start(bf16[9,16,128]{2,1,0:T(8,128)(2,1)} %param.38) | copy-start | bytes 110596
  0.1 24.3 %copy-start.1 = (bf16[9,16,128]{2,1,0:T(8,128)(2,1)S(1)}, bf16[9,16,128]{2,1,0:T(8,128)(2,1)}, u32[]{:S(2)}) copy-start(bf16[9,16,128]{2,1,0:T(8,128)(2,1)} %param.39) | copy-start | bytes 110596
  5.6 48.8 %collective-permute-start = (bf16[8,128]{1,0:T(8,128)(2,1)S(1)}, bf16[8,128]{1,0:T(8,128)(2,1)S(1)}, u32[]{:S(2)}, u32[]{:S(2)}) collective-permute-start(bf16[8,128]{1,0:T(8,128)(2,1)S(1)} %get-tuple-element.35), channel_id=1, source_target_pairs={{0,496},{8,504},{16,0},{24,8},{32,16},{40,24},{48,32},{56,40},{64,... | collective-permute-start | bytes 6152 | tf_op jit(solution)/shard_map/ppermute | solution.py:14
  18.6 35.9 %collective-permute-start.1 = (bf16[8,128]{1,0:T(8,128)(2,1)S(1)}, bf16[8,128]{1,0:T(8,128)(2,1)S(1)}, u32[]{:S(2)}, u32[]{:S(2)}) collective-permute-start(bf16[8,128]{1,0:T(8,128)(2,1)S(1)} %get-tuple-element.34), channel_id=1, source_target_pairs={{0,504},{8,0},{16,8},{24,16},{32,24},{40,32},{48,40},{56,48},{64,5... | collective-permute-start | bytes 6152 | tf_op jit(solution)/shard_map/ppermute | solution.py:14
  54.5 8.5 %collective-permute-start.2 = (bf16[8,128]{1,0:T(8,128)(2,1)S(1)}, bf16[8,128]{1,0:T(8,128)(2,1)S(1)}, u32[]{:S(2)}, u32[]{:S(2)}) collective-permute-start(bf16[8,128]{1,0:T(8,128)(2,1)S(1)} %get-tuple-element.32), channel_id=1, source_target_pairs={{0,8},{8,16},{16,24},{24,32},{32,40},{40,48},{48,56},{56,64},{64,7... | collective-permute-start | bytes 6152 | tf_op jit(solution)/shard_map/ppermute | solution.py:14
  56.6 9.1 %collective-permute-start.3 = (bf16[8,128]{1,0:T(8,128)(2,1)S(1)}, bf16[8,128]{1,0:T(8,128)(2,1)S(1)}, u32[]{:S(2)}, u32[]{:S(2)}) collective-permute-start(bf16[8,128]{1,0:T(8,128)(2,1)S(1)} %get-tuple-element.31), channel_id=1, source_target_pairs={{0,16},{8,24},{16,32},{24,40},{32,48},{40,56},{48,64},{56,72},{64,... | collective-permute-start | bytes 6152 | tf_op jit(solution)/shard_map/ppermute | solution.py:14
  94.5 11.0 %copy-start.5 = (s32[324]{0:T(512)S(1)}, s32[324]{0:T(512)}, u32[]{:S(2)}) copy-start(s32[324]{0:T(512)} %constant.224.clone) | copy-start | bytes 3892
  97.3 8.3 %collective-permute-start.4 = (bf16[64,2,60]{0,1,2:T(2,128)(2,1)S(1)}, bf16[64,2,60]{0,1,2:T(2,128)(2,1)S(1)}, u32[]{:S(2)}, u32[]{:S(2)}) collective-permute-start(bf16[64,2,60]{0,1,2:T(2,128)(2,1)S(1)} %get-tuple-element.29), channel_id=1, source_target_pairs={{0,1},{1,2},{2,3},{3,4},{4,5},{5,6},{6,7},{7,8},{8,9},{9,10},{10,1... | collective-permute-start | bytes 46088 | tf_op jit(solution)/shard_map/ppermute | solution.py:24
  100.6 6.3 %collective-permute-start.5 = (bf16[64,2,60]{0,1,2:T(2,128)(2,1)S(1)}, bf16[64,2,60]{0,1,2:T(2,128)(2,1)S(1)}, u32[]{:S(2)}, u32[]{:S(2)}) collective-permute-start(bf16[64,2,60]{0,1,2:T(2,128)(2,1)S(1)} %get-tuple-element.30), channel_id=1, source_target_pairs={{1,0},{2,1},{3,2},{4,3},{5,4},{6,5},{7,6},{8,7},{9,8},{10,9},{11,1... | collective-permute-start | bytes 46088 | tf_op jit(solution)/shard_map/ppermute | solution.py:25
  118.9 8.5 %collective-permute-start.6 = (bf16[128,2,60]{0,1,2:T(2,128)(2,1)S(1)}, bf16[128,2,60]{0,1,2:T(2,128)(2,1)S(1)}, u32[]{:S(2)}, u32[]{:S(2)}) collective-permute-start(bf16[128,2,60]{0,1,2:T(2,128)(2,1)S(1)} %get-tuple-element.27), channel_id=1, source_target_pairs={{0,1},{1,2},{2,3},{3,4},{4,5},{5,6},{6,7},{7,8},{8,9},{9,10},{10,1... | collective-permute-start | bytes 92168 | tf_op jit(solution)/shard_map/ppermute | solution.py:24
  121.5 7.3 %collective-permute-start.7 = (bf16[128,2,60]{0,1,2:T(2,128)(2,1)S(1)}, bf16[128,2,60]{0,1,2:T(2,128)(2,1)S(1)}, u32[]{:S(2)}, u32[]{:S(2)}) collective-permute-start(bf16[128,2,60]{0,1,2:T(2,128)(2,1)S(1)} %get-tuple-element.28), channel_id=1, source_target_pairs={{1,0},{2,1},{3,2},{4,3},{5,4},{6,5},{7,6},{8,7},{9,8},{10,9},{11,1... | collective-permute-start | bytes 92168 | tf_op jit(solution)/shard_map/ppermute | solution.py:25
  139.0 8.3 %collective-permute-start.8 = (bf16[128,2,60]{0,1,2:T(2,128)(2,1)S(1)}, bf16[128,2,60]{0,1,2:T(2,128)(2,1)S(1)}, u32[]{:S(2)}, u32[]{:S(2)}) collective-permute-start(bf16[128,2,60]{0,1,2:T(2,128)(2,1)S(1)} %get-tuple-element.25), channel_id=1, source_target_pairs={{0,1},{1,2},{2,3},{3,4},{4,5},{5,6},{6,7},{7,8},{8,9},{9,10},{10,1... | collective-permute-start | bytes 92168 | tf_op jit(solution)/shard_map/ppermute | solution.py:24
  141.5 7.4 %collective-permute-start.9 = (bf16[128,2,60]{0,1,2:T(2,128)(2,1)S(1)}, bf16[128,2,60]{0,1,2:T(2,128)(2,1)S(1)}, u32[]{:S(2)}, u32[]{:S(2)}) collective-permute-start(bf16[128,2,60]{0,1,2:T(2,128)(2,1)S(1)} %get-tuple-element.26), channel_id=1, source_target_pairs={{1,0},{2,1},{3,2},{4,3},{5,4},{6,5},{7,6},{8,7},{9,8},{10,9},{11,1... | collective-permute-start | bytes 92168 | tf_op jit(solution)/shard_map/ppermute | solution.py:25

commit v2 on v1

--- a/solution.py
+++ b/solution.py
@@ -12,6 +12,12 @@
     count = lax.axis_size(axis)
     pairs = [(source, (source + steps) % count) for source in range(count)]
     return lax.ppermute(value, axis, pairs)
+
+
+def gather_by_exchange(value, axis, dim):
+    count = lax.axis_size(axis)
+    copies = jnp.concatenate([value] * count, axis=dim)
+    return lax.all_to_all(copies, axis, split_axis=dim, concat_axis=dim, tiled=True)
 
 
 def extended_2(x, sides, width):
@@ -138,7 +144,7 @@
     per_group = tiles_here // groups
     widths = [kernel_one.shape[2], kernel_two.shape[2], kernel_three.shape[2]]
     joined_kernels = jnp.concatenate([kernel_one, kernel_two, kernel_three], axis=2)
-    joined_kernels = lax.all_gather(joined_kernels, "chan", axis=1, tiled=True)
+    joined_kernels = gather_by_exchange(joined_kernels, "chan", 1)
     kernels = []
     low = 0
     for width in widths:
@@ -156,7 +162,7 @@
             block = from_behind(block, "tile", offset_index - REACH)
         blocks.append(block)
     arrived = jnp.stack(blocks, axis=1).reshape(channels_here, near_count * capacity)
-    arrived = lax.all_gather(arrived, "chan", axis=0, tiled=True)
+    arrived = gather_by_exchange(arrived, "chan", 0)
     group_index = lax.axis_index("chan")
     my_slots = lax.dynamic_slice_in_dim(corner_slot, group_index * per_group, per_group, 1)
     my_weights = lax.dynamic_slice_in_dim(corner_weight, group_index * per_group, per_group, 1)

time: 178 us -> 143 us (0.80)
  blocking collectives: 76 us -> 17.1 us
  local copies, waits for them, and re-layouts: 25.4 us -> 36.8 us
  starting transfers between devices: 45.7 us -> 57 us
  waiting for transfers between devices: 9.64 us -> 12.8 us
    all_gather x2 -> x0, blocking collectives: 58.1 us -> none  [the longest x1 29.9 us: on_device(): joined_kernels = lax.all_gather(joined_kernels, 'chan', axis=1, tiled=True)]
    all_to_all x0 -> x2, starting transfers between devices: none -> 10.8 us  [gather_by_exchange(): lax.all_to_all(copies, axis, split_axis=dim, concat_axis=dim, tiled=True)]
    unnamed x35 -> x64, local copies, waits for them, and re-layouts: 4.62 us -> 13.2 us
    all_to_all x0 -> x2, waiting for transfers between devices: none -> 5.24 us  [gather_by_exchange(): lax.all_to_all(copies, axis, split_axis=dim, concat_axis=dim, tiled=True)]
    slice x0 -> x2, local copies, waits for them, and re-layouts: none -> 2.27 us  [conv_layer(): kernel[tap_index]]
  transfers between devices with their start and end apart: 10 -> 12, of which waited for: 5 -> 5; matrix products, arithmetic and copies ran while one was open for 2% -> 11% of each run, Pallas kernels for 0% -> 0%
where the time goes in v2:
time: 143 us
  starting transfers between devices  57 us (40%)
  local copies, waits for them, and re-layouts  36.8 us (26%)
  blocking collectives  17.1 us (12%)
  waiting for transfers between devices  12.8 us (9%)
  matrix products  11.3 us (8%)
  other arithmetic  6.31 us (4%)
    ppermute x4, starting transfers between devices, from_behind(): return lax.ppermute(value, axis, pairs)  21.4 us
    all_to_all x1, blocking collectives, on_device(): lax.all_to_all(activity, 'chan', split_axis=0, concat_axis=1, tiled=True)  17.1 us
    ppermute x3, starting transfers between devices, extended_2(): after = lax.ppermute(initial, axis, down)  16.5 us
    unnamed x64, local copies, waits for them, and re-layouts  13.2 us
    all_to_all x2, starting transfers between devices, gather_by_exchange(): lax.all_to_all(copies, axis, split_axis=dim, concat_axis=dim, tiled=True)  10.8 us
    dot_general x27, matrix products, conv_layer(): jnp.einsum('oc,ctq->otq', kernel[tap_index], window, preferred_element_ty...  8.83 us
    ppermute x3, starting transfers between devices, extended_2(): before = lax.ppermute(last, axis, up)  8.32 us
    gather x6, local copies, waits for them, and re-layouts, conv_layer(): padded = jnp.take(joined, layout_table(P_SIZE), axis=2)  6.41 us
  transfers between devices with their start and end apart: 12, of which 5 were waited for; matrix products, arithmetic and copies ran while one was open for 11% of the time, Pallas kernels for 0%

profile of v2, /device:TPU:2, one launch (start us, length us, event | category | flops | bytes accessed | tf_op | source)
XLA Modules:
  0.0 142.5 jit_solution(846386293449990085)
XLA Ops:
  0.8 1.8 %copy.393 = bf16[8,8192]{0,1:T(8,128)(2,1)S(1)} copy(bf16[8,8192]{1,0:T(8,128)(2,1)} %param.30) | data formatting | bytes 262144 | tf_op args[0]
  2.7 2.0 %gather_fusion = bf16[640,8]{1,0:T(8,128)(2,1)S(1)} fusion(bf16[8,8192]{0,1:T(8,128)(2,1)S(1)} %copy.393, s32[1024]{0:T(1024)S(1)} %get-tuple-element.68), kind=kCustom, calls=%fused_computation.8 | custom fusion | bytes 23040 | tf_op jit(solution)/shard_map/jit(_take)/gather | solution.py:155
  4.9 13.0 %collective-permute-start = (bf16[8,128]{1,0:T(8,128)(2,1)S(1)}, bf16[8,128]{1,0:T(8,128)(2,1)S(1)}, u32[]{:S(2)}, u32[]{:S(2)}) collective-permute-start(bf16[8,128]{1,0:T(8,128)(2,1)S(1)} %get-tuple-element.62), channel_id=1, source_target_pairs={{0,496},{8,504},{16,0},{24,8},{32,16},{40,24},{48,32},{56,40},{64,... | collective-permute-start | bytes 6152 | tf_op jit(solution)/shard_map/ppermute | solution.py:14
  17.9 2.5 %collective-permute-start.1 = (bf16[8,128]{1,0:T(8,128)(2,1)S(1)}, bf16[8,128]{1,0:T(8,128)(2,1)S(1)}, u32[]{:S(2)}, u32[]{:S(2)}) collective-permute-start(bf16[8,128]{1,0:T(8,128)(2,1)S(1)} %get-tuple-element.61), channel_id=1, source_target_pairs={{0,504},{8,0},{16,8},{24,16},{32,24},{40,32},{48,40},{56,48},{64,5... | collective-permute-start | bytes 6152 | tf_op jit(solution)/shard_map/ppermute | solution.py:14
  24.2 1.9 %collective-permute-start.2 = (bf16[8,128]{1,0:T(8,128)(2,1)S(1)}, bf16[8,128]{1,0:T(8,128)(2,1)S(1)}, u32[]{:S(2)}, u32[]{:S(2)}) collective-permute-start(bf16[8,128]{1,0:T(8,128)(2,1)S(1)} %get-tuple-element.59), channel_id=1, source_target_pairs={{0,8},{8,16},{16,24},{24,32},{32,40},{40,48},{48,56},{56,64},{64,7... | collective-permute-start | bytes 6152 | tf_op jit(solution)/shard_map/ppermute | solution.py:14
  26.3 1.9 %reshape.366 = bf16[8,2,23040]{2,1,0:T(2,128)(2,1)} reshape(bf16[128,9,320]{2,1,0:T(8,128)(2,1)S(1)} %bitcast.271) | data formatting | bytes 1474560
  28.2 4.0 %collective-permute-start.3 = (bf16[8,128]{1,0:T(8,128)(2,1)S(1)}, bf16[8,128]{1,0:T(8,128)(2,1)S(1)}, u32[]{:S(2)}, u32[]{:S(2)}) collective-permute-start(bf16[8,128]{1,0:T(8,128)(2,1)S(1)} %get-tuple-element.58), channel_id=1, source_target_pairs={{0,16},{8,24},{16,32},{24,40},{32,48},{40,56},{48,64},{56,72},{64,... | collective-permute-start | bytes 6152 | tf_op jit(solution)/shard_map/ppermute | solution.py:14
  32.7 4.5 %collective-permute-done.3 = bf16[8,128]{1,0:T(8,128)(2,1)S(1)} collective-permute-done((bf16[8,128]{1,0:T(8,128)(2,1)S(1)}, bf16[8,128]{1,0:T(8,128)(2,1)S(1)}, u32[]{:S(2)}, u32[]{:S(2)}) %collective-permute-start.3) | collective-permute-done | bytes 2080 | tf_op jit(solution)/shard_map/ppermute | solution.py:14
  42.1 5.9 %all-to-all-start.1 = ((bf16[8,8,640]{2,1,0:T(8,128)(2,1)}), bf16[8,8,640]{2,1,0:T(8,128)(2,1)S(1)}, u32[]{:S(2)}, u32[]{:S(2)}) async-start(bf16[8,8,640]{2,1,0:T(8,128)(2,1)} %bitcast.19), calls=%async_computation.1 | async-start | bytes 163840 | tf_op jit(solution)/shard_map/all_to_all | solution.py:20
  48.0 5.2 %all-to-all-done.1 = bf16[8,8,640]{2,1,0:T(8,128)(2,1)S(1)} async-done(((bf16[8,8,640]{2,1,0:T(8,128)(2,1)}), bf16[8,8,640]{2,1,0:T(8,128)(2,1)S(1)}, u32[]{:S(2)}, u32[]{:S(2)}) %all-to-all-start.1) | async-done | bytes 81952 | tf_op jit(solution)/shard_map/all_to_all | solution.py:20
  53.2 4.8 %all-to-all-start = ((bf16[8,2,23040]{2,1,0:T(2,128)(2,1)}), bf16[8,2,23040]{2,1,0:T(2,128)(2,1)S(1)}, u32[]{:S(2)}, u32[]{:S(2)}) async-start(bf16[8,2,23040]{2,1,0:T(2,128)(2,1)} %reshape.366), calls=%async_computation | async-start | bytes 1474560 | tf_op jit(solution)/shard_map/all_to_all | solution.py:20
  61.5 3.4 %collective-permute-start.4 = (bf16[64,2,60]{0,1,2:T(2,128)(2,1)S(1)}, bf16[64,2,60]{0,1,2:T(2,128)(2,1)S(1)}, u32[]{:S(2)}, u32[]{:S(2)}) collective-permute-start(bf16[64,2,60]{0,1,2:T(2,128)(2,1)S(1)} %get-tuple-element.56), channel_id=1, source_target_pairs={{0,1},{1,2},{2,3},{3,4},{4,5},{5,6},{6,7},{7,8},{8,9},{9,10},{10,1... | collective-permute-start | bytes 46088 | tf_op jit(solution)/shard_map/ppermute | solution.py:30
  64.9 4.8 %collective-permute-start.5 = (bf16[64,2,60]{0,1,2:T(2,128)(2,1)S(1)}, bf16[64,2,60]{0,1,2:T(2,128)(2,1)S(1)}, u32[]{:S(2)}, u32[]{:S(2)}) collective-permute-start(bf16[64,2,60]{0,1,2:T(2,128)(2,1)S(1)} %get-tuple-element.57), channel_id=1, source_target_pairs={{1,0},{2,1},{3,2},{4,3},{5,4},{6,5},{7,6},{8,7},{9,8},{10,9},{11,1... | collective-permute-start | bytes 46088 | tf_op jit(solution)/shard_map/ppermute | solution.py:31
  69.8 1.2 collective-permute-done.5
  71.3 1.4 gather_fusion.2
  73.1 2.0 %gather_fusion.3 = bf16[324,64,4]{1,2,0:T(4,128)(2,1)S(1)} fusion(bf16[64,4,324]{0,1,2:T(4,128)(2,1)S(1)} %pad_maximum_fusion.2, s32[1024]{0:T(1024)S(1)} %get-tuple-element.65), kind=kCustom, calls=%fused_computation.11 | custom fusion | bytes 333072 | tf_op jit(solution)/shard_map/jit(_take)/gather | solution.py:107
  75.4 1.4 reshape.367
  83.9 1.1 fusion.18
  85.9 3.0 %collective-permute-start.6 = (bf16[128,2,60]{0,1,2:T(2,128)(2,1)S(1)}, bf16[128,2,60]{0,1,2:T(2,128)(2,1)S(1)}, u32[]{:S(2)}, u32[]{:S(2)}) collective-permute-start(bf16[128,2,60]{0,1,2:T(2,128)(2,1)S(1)} %get-tuple-element.54), channel_id=1, source_target_pairs={{0,1},{1,2},{2,3},{3,4},{4,5},{5,6},{6,7},{7,8},{8,9},{9,10},{10,1... | collective-permute-start | bytes 92168 | tf_op jit(solution)/shard_map/ppermute | solution.py:30
  88.9 5.4 %collective-permute-start.7 = (bf16[128,2,60]{0,1,2:T(2,128)(2,1)S(1)}, bf16[128,2,60]{0,1,2:T(2,128)(2,1)S(1)}, u32[]{:S(2)}, u32[]{:S(2)}) collective-permute-start(bf16[128,2,60]{0,1,2:T(2,128)(2,1)S(1)} %get-tuple-element.55), channel_id=1, source_target_pairs={{1,0},{2,1},{3,2},{4,3},{5,4},{6,5},{7,6},{8,7},{9,8},{10,9},{11,1... | collective-permute-start | bytes 92168 | tf_op jit(solution)/shard_map/ppermute | solution.py:31
  94.4 1.8 %fusion.93 = (bf16[1,128,128]{2,0,1:T(2,128)(2,1)S(1)}, bf16[1,128,128]{2,0,1:T(2,128)(2,1)S(1)}, bf16[1,128,128]{2,0,1:T(2,128)(2,1)S(1)}, bf16[1,128,128]{2,0,...) fusion(bf16[9,128,320]{2,0,1:T(8,128)(2,1)S(1)} %bitcast.261), kind=kLoop, calls=%fused_computation.248 | loop fusion | bytes 1179648 | tf_op jit(solution)/shard_map/slice | solution.py:115
  96.4 1.4 gather_fusion.7
  98.4 2.0 %gather_fusion.8 = bf16[324,128,4]{1,2,0:T(4,128)(2,1)S(1)} fusion(bf16[128,4,324]{0,1,2:T(4,128)(2,1)S(1)} %copy.425, s32[1024]{0:T(1024)S(1)} %get-tuple-element.65), kind=kCustom, calls=%fused_computation.3.clone | custom fusion | bytes 664848 | tf_op jit(solution)/shard_map/jit(_take)/gather | solution.py:107
  104.0 1.1 fusion.21
  106.0 1.9 %collective-permute-start.8 = (bf16[128,2,60]{0,1,2:T(2,128)(2,1)S(1)}, bf16[128,2,60]{0,1,2:T(2,128)(2,1)S(1)}, u32[]{:S(2)}, u32[]{:S(2)}) collective-permute-start(bf16[128,2,60]{0,1,2:T(2,128)(2,1)S(1)} %get-tuple-element.52), channel_id=1, source_target_pairs={{0,1},{1,2},{2,3},{3,4},{4,5},{5,6},{6,7},{7,8},{8,9},{9,10},{10,1... | collective-permute-start | bytes 92168 | tf_op jit(solution)/shard_map/ppermute | solution.py:30
  107.9 6.3 %collective-permute-start.9 = (bf16[128,2,60]{0,1,2:T(2,128)(2,1)S(1)}, bf16[128,2,60]{0,1,2:T(2,128)(2,1)S(1)}, u32[]{:S(2)}, u32[]{:S(2)}) collective-permute-start(bf16[128,2,60]{0,1,2:T(2,128)(2,1)S(1)} %get-tuple-element.53), channel_id=1, source_target_pairs={{1,0},{2,1},{3,2},{4,3},{5,4},{6,5},{7,6},{8,7},{9,8},{10,9},{11,1... | collective-permute-start | bytes 92168 | tf_op jit(solution)/shard_map/ppermute | solution.py:31
  114.2 1.3 collective-permute-done.9
  115.7 1.4 gather_fusion.10
  117.6 2.0 %gather_fusion.11 = bf16[324,128,4]{1,2,0:T(4,128)(2,1)S(1)} fusion(bf16[128,4,324]{0,1,2:T(4,128)(2,1)S(1)} %copy.447, s32[1024]{0:T(1024)S(1)} %get-tuple-element.65), kind=kCustom, calls=%fused_computation.7.clone | custom fusion | bytes 664848 | tf_op jit(solution)/shard_map/jit(_take)/gather | solution.py:107
  123.2 1.1 fusion.24
  124.6 17.1 %all_to_all.35 = bf16[128,4,256]{2,1,0:T(4,128)(2,1)S(1)} all-to-all(bf16[128,4,256]{2,1,0:T(4,128)(2,1)S(1)} %copy.466), channel_id=1, replica_groups=mesh['tile'=64,'chan'=8] {'chan'}, dimensions={0} | all-to-all | bytes 524288 | tf_op jit(solution)/shard_map/all_to_all | solution.py:189
  141.8 0.8 copy.469
  (180 shorter events, 31.9 us)
Async XLA Ops:
  0.0 2.7 %copy-start.9 = (s32[68]{0:T(128)S(1)}, s32[68]{0:T(128)}, u32[]{:S(2)}) copy-start(s32[68]{0:T(128)} %constant.310) | copy-start | bytes 820
  0.0 21.9 %copy-start.7 = (s32[68]{0:T(128)S(1)}, s32[68]{0:T(128)}, u32[]{:S(2)}) copy-start(s32[68]{0:T(128)} %constant.243) | copy-start | bytes 820
  0.0 4.8 %copy-start.3 = (s32[1,5,128]{2,0,1:T(1,128)S(1)}, s32[1,5,128]{2,0,1:T(1,128)}, u32[]{:S(2)}) copy-start(s32[1,5,128]{2,0,1:T(1,128)} %param.31) | copy-start | bytes 7684
  0.0 4.8 %copy-start.8 = (s32[1,5]{1,0:T(1,128)S(1)}, s32[1,5]{1,0:T(1,128)}, u32[]{:S(2)}) copy-start(s32[1,5]{1,0:T(1,128)} %param.32) | copy-start | bytes 64
  0.0 20.4 %copy-start.4 = (s32[32,8]{0,1:T(8,128)S(1)}, s32[32,8]{0,1:T(8,128)}, u32[]{:S(2)}) copy-start(s32[32,8]{0,1:T(8,128)} %param.35) | copy-start | bytes 3076
  0.0 20.4 %copy-start.5 = (s32[32,8]{0,1:T(8,128)S(1)}, s32[32,8]{0,1:T(8,128)}, u32[]{:S(2)}) copy-start(s32[32,8]{0,1:T(8,128)} %param.36) | copy-start | bytes 3076
  0.0 23.6 %copy-start.2 = (bf16[9,16,64]{2,1,0:T(8,128)(2,1)S(1)}, bf16[9,16,64]{2,1,0:T(8,128)(2,1)}, u32[]{:S(2)}) copy-start(bf16[9,16,64]{2,1,0:T(8,128)(2,1)} %param.37) | copy-start | bytes 55300
  0.0 23.6 %copy-start.1 = (bf16[9,16,128]{2,1,0:T(8,128)(2,1)S(1)}, bf16[9,16,128]{2,1,0:T(8,128)(2,1)}, u32[]{:S(2)}) copy-start(bf16[9,16,128]{2,1,0:T(8,128)(2,1)} %param.38) | copy-start | bytes 110596
  0.1 23.6 %copy-start = (bf16[9,16,128]{2,1,0:T(8,128)(2,1)S(1)}, bf16[9,16,128]{2,1,0:T(8,128)(2,1)}, u32[]{:S(2)}) copy-start(bf16[9,16,128]{2,1,0:T(8,128)(2,1)} %param.39) | copy-start | bytes 110596
  4.7 21.5 %copy-start.6 = (s32[324]{0:T(512)S(1)}, s32[324]{0:T(512)}, u32[]{:S(2)}) copy-start(s32[324]{0:T(512)} %constant.224.clone) | copy-start | bytes 3892
  4.7 21.5 %copy-start.10 = (s32[60]{0:T(128)S(1)}, s32[60]{0:T(128)}, u32[]{:S(2)}) copy-start(s32[60]{0:T(128)} %constant.221.clone) | copy-start | bytes 724
  4.9 19.2 %collective-permute-start = (bf16[8,128]{1,0:T(8,128)(2,1)S(1)}, bf16[8,128]{1,0:T(8,128)(2,1)S(1)}, u32[]{:S(2)}, u32[]{:S(2)}) collective-permute-start(bf16[8,128]{1,0:T(8,128)(2,1)S(1)} %get-tuple-element.62), channel_id=1, source_target_pairs={{0,496},{8,504},{16,0},{24,8},{32,16},{40,24},{48,32},{56,40},{64,... | collective-permute-start | bytes 6152 | tf_op jit(solution)/shard_map/ppermute | solution.py:14
  17.9 6.3 %collective-permute-start.1 = (bf16[8,128]{1,0:T(8,128)(2,1)S(1)}, bf16[8,128]{1,0:T(8,128)(2,1)S(1)}, u32[]{:S(2)}, u32[]{:S(2)}) collective-permute-start(bf16[8,128]{1,0:T(8,128)(2,1)S(1)} %get-tuple-element.61), channel_id=1, source_target_pairs={{0,504},{8,0},{16,8},{24,16},{32,24},{40,32},{48,40},{56,48},{64,5... | collective-permute-start | bytes 6152 | tf_op jit(solution)/shard_map/ppermute | solution.py:14
  24.2 8.5 %collective-permute-start.2 = (bf16[8,128]{1,0:T(8,128)(2,1)S(1)}, bf16[8,128]{1,0:T(8,128)(2,1)S(1)}, u32[]{:S(2)}, u32[]{:S(2)}) collective-permute-start(bf16[8,128]{1,0:T(8,128)(2,1)S(1)} %get-tuple-element.59), channel_id=1, source_target_pairs={{0,8},{8,16},{16,24},{24,32},{32,40},{40,48},{48,56},{56,64},{64,7... | collective-permute-start | bytes 6152 | tf_op jit(solution)/shard_map/ppermute | solution.py:14
  28.2 9.1 %collective-permute-start.3 = (bf16[8,128]{1,0:T(8,128)(2,1)S(1)}, bf16[8,128]{1,0:T(8,128)(2,1)S(1)}, u32[]{:S(2)}, u32[]{:S(2)}) collective-permute-start(bf16[8,128]{1,0:T(8,128)(2,1)S(1)} %get-tuple-element.58), channel_id=1, source_target_pairs={{0,16},{8,24},{16,32},{24,40},{32,48},{40,56},{48,64},{56,72},{64,... | collective-permute-start | bytes 6152 | tf_op jit(solution)/shard_map/ppermute | solution.py:14
  42.1 11.2 %all-to-all-start.1 = ((bf16[8,8,640]{2,1,0:T(8,128)(2,1)}), bf16[8,8,640]{2,1,0:T(8,128)(2,1)S(1)}, u32[]{:S(2)}, u32[]{:S(2)}) async-start(bf16[8,8,640]{2,1,0:T(8,128)(2,1)} %bitcast.19), calls=%async_computation.1 | async-start | bytes 163840 | tf_op jit(solution)/shard_map/all_to_all | solution.py:20
  53.2 22.2 %all-to-all-start = ((bf16[8,2,23040]{2,1,0:T(2,128)(2,1)}), bf16[8,2,23040]{2,1,0:T(2,128)(2,1)S(1)}, u32[]{:S(2)}, u32[]{:S(2)}) async-start(bf16[8,2,23040]{2,1,0:T(2,128)(2,1)} %reshape.366), calls=%async_computation | async-start | bytes 1474560 | tf_op jit(solution)/shard_map/all_to_all | solution.py:20
  61.5 8.3 %collective-permute-start.4 = (bf16[64,2,60]{0,1,2:T(2,128)(2,1)S(1)}, bf16[64,2,60]{0,1,2:T(2,128)(2,1)S(1)}, u32[]{:S(2)}, u32[]{:S(2)}) collective-permute-start(bf16[64,2,60]{0,1,2:T(2,128)(2,1)S(1)} %get-tuple-element.56), channel_id=1, source_target_pairs={{0,1},{1,2},{2,3},{3,4},{4,5},{5,6},{6,7},{7,8},{8,9},{9,10},{10,1... | collective-permute-start | bytes 46088 | tf_op jit(solution)/shard_map/ppermute | solution.py:30
  64.9 6.1 %collective-permute-start.5 = (bf16[64,2,60]{0,1,2:T(2,128)(2,1)S(1)}, bf16[64,2,60]{0,1,2:T(2,128)(2,1)S(1)}, u32[]{:S(2)}, u32[]{:S(2)}) collective-permute-start(bf16[64,2,60]{0,1,2:T(2,128)(2,1)S(1)} %get-tuple-element.57), channel_id=1, source_target_pairs={{1,0},{2,1},{3,2},{4,3},{5,4},{6,5},{7,6},{8,7},{9,8},{10,9},{11,1... | collective-permute-start | bytes 46088 | tf_op jit(solution)/shard_map/ppermute | solution.py:31
  85.9 10.3 %collective-permute-start.6 = (bf16[128,2,60]{0,1,2:T(2,128)(2,1)S(1)}, bf16[128,2,60]{0,1,2:T(2,128)(2,1)S(1)}, u32[]{:S(2)}, u32[]{:S(2)}) collective-permute-start(bf16[128,2,60]{0,1,2:T(2,128)(2,1)S(1)} %get-tuple-element.54), channel_id=1, source_target_pairs={{0,1},{1,2},{2,3},{3,4},{4,5},{5,6},{6,7},{7,8},{8,9},{9,10},{10,1... | collective-permute-start | bytes 92168 | tf_op jit(solution)/shard_map/ppermute | solution.py:30
  88.9 7.3 %collective-permute-start.7 = (bf16[128,2,60]{0,1,2:T(2,128)(2,1)S(1)}, bf16[128,2,60]{0,1,2:T(2,128)(2,1)S(1)}, u32[]{:S(2)}, u32[]{:S(2)}) collective-permute-start(bf16[128,2,60]{0,1,2:T(2,128)(2,1)S(1)} %get-tuple-element.55), channel_id=1, source_target_pairs={{1,0},{2,1},{3,2},{4,3},{5,4},{6,5},{7,6},{8,7},{9,8},{10,9},{11,1... | collective-permute-start | bytes 92168 | tf_op jit(solution)/shard_map/ppermute | solution.py:31
  106.0 8.2 %collective-permute-start.8 = (bf16[128,2,60]{0,1,2:T(2,128)(2,1)S(1)}, bf16[128,2,60]{0,1,2:T(2,128)(2,1)S(1)}, u32[]{:S(2)}, u32[]{:S(2)}) collective-permute-start(bf16[128,2,60]{0,1,2:T(2,128)(2,1)S(1)} %get-tuple-element.52), channel_id=1, source_target_pairs={{0,1},{1,2},{2,3},{3,4},{4,5},{5,6},{6,7},{7,8},{8,9},{9,10},{10,1... | collective-permute-start | bytes 92168 | tf_op jit(solution)/shard_map/ppermute | solution.py:30
  107.9 7.6 %collective-permute-start.9 = (bf16[128,2,60]{0,1,2:T(2,128)(2,1)S(1)}, bf16[128,2,60]{0,1,2:T(2,128)(2,1)S(1)}, u32[]{:S(2)}, u32[]{:S(2)}) collective-permute-start(bf16[128,2,60]{0,1,2:T(2,128)(2,1)S(1)} %get-tuple-element.53), channel_id=1, source_target_pairs={{1,0},{2,1},{3,2},{4,3},{5,4},{6,5},{7,6},{8,7},{9,8},{10,9},{11,1... | collective-permute-start | bytes 92168 | tf_op jit(solution)/shard_map/ppermute | solution.py:31

commit v3 on v2

--- a/solution.py
+++ b/solution.py
@@ -151,13 +151,11 @@
         kernels.append(joined_kernels[:, :, low : low + width])
         low += width
     slot_order = jnp.arange(capacity)
-    rows_list = send_rows[0].reshape(-1)
-    piece = jnp.take(analysis, rows_list, axis=1).reshape(channels_here, near_count, capacity)
-    is_live = slot_order[None, :] < send_count[0][:, None]
-    piece = jnp.where(is_live[None], piece, jnp.zeros((), piece.dtype))
     blocks = []
     for offset_index in range(near_count):
-        block = piece[:, offset_index]
+        block = jnp.take(analysis, send_rows[0, offset_index], axis=1)
+        is_live = slot_order < send_count[0, offset_index]
+        block = jnp.where(is_live[None, :], block, jnp.zeros((), block.dtype))
         if offset_index != REACH:
             block = from_behind(block, "tile", offset_index - REACH)
         blocks.append(block)
@@ -191,7 +189,7 @@
 
 
 def solution(mesh):
-    return jax.shard_map(
+    step = jax.shard_map(
         on_device,
         mesh=mesh,
         in_specs=(
@@ -209,3 +207,4 @@
         out_specs=P("chan", "tile", None),
         check_vma=False,
     )
+    return step

time: 143 us -> 145 us (1.014)
  waiting for transfers between devices: 12.8 us -> 7.56 us
  other arithmetic: 6.31 us -> 9.84 us
  local copies, waits for them, and re-layouts: 36.8 us -> 40.2 us
    ppermute x4, waiting for transfers between devices: 5.05 us -> 0.01 us  [from_behind(): return lax.ppermute(value, axis, pairs)]
    lt x1 -> x4, other arithmetic: 0.09 us -> 2.46 us  [on_device(): is_live = slot_order < send_count[0, offset_index]]
    slice x0 -> x1, local copies, waits for them, and re-layouts: none -> 1.49 us  [on_device(): is_live = slot_order < send_count[0, offset_index]]
    gather x2 -> x5, local copies, waits for them, and re-layouts: 2.09 us -> 3.56 us  [on_device(): block = jnp.take(analysis, send_rows[0, offset_index], axis=1)]
    unnamed x64 -> x61, local copies, waits for them, and re-layouts: 13.2 us -> 13.2 us
  transfers between devices with their start and end apart: 12 -> 12, of which waited for: 5 -> 3; matrix products, arithmetic and copies ran while one was open for 11% -> 15% of each run, Pallas kernels for 0% -> 0%
where the time goes in v3:
time: 145 us; the launch traced here: 144 us
  starting transfers between devices  57 us (39%)
  local copies, waits for them, and re-layouts  40.2 us (28%)
  blocking collectives  17.1 us (12%)
  matrix products  11.3 us (8%)
  other arithmetic  9.84 us (7%)
  waiting for transfers between devices  7.56 us (5%)
    ppermute x4, starting transfers between devices, from_behind(): return lax.ppermute(value, axis, pairs)  21.4 us
    all_to_all x1, blocking collectives, on_device(): lax.all_to_all(activity, 'chan', split_axis=0, concat_axis=1, tiled=True)  17.1 us
    ppermute x3, starting transfers between devices, extended_2(): after = lax.ppermute(initial, axis, down)  16.5 us
    unnamed x61, local copies, waits for them, and re-layouts  13.2 us
    all_to_all x2, starting transfers between devices, gather_by_exchange(): lax.all_to_all(copies, axis, split_axis=dim, concat_axis=dim, tiled=True)  10.8 us
    dot_general x27, matrix products, conv_layer(): jnp.einsum('oc,ctq->otq', kernel[tap_index], window, preferred_element_ty...  8.81 us
    ppermute x3, starting transfers between devices, extended_2(): before = lax.ppermute(last, axis, up)  8.32 us
    gather x6, local copies, waits for them, and re-layouts, conv_layer(): padded = jnp.take(joined, layout_table(P_SIZE), axis=2)  6.41 us
  transfers between devices with their start and end apart: 12, of which 3 were waited for; matrix products, arithmetic and copies ran while one was open for 15% of the time, Pallas kernels for 0%

profile of v3, /device:TPU:2, one launch (start us, length us, event | category | flops | bytes accessed | tf_op | source)
XLA Modules:
  0.0 144.2 jit_solution(14884596726137399985)
XLA Ops:
  0.0 1.5 %fusion.98 = (s32[1,1]{1,0:T(1,128)}, s32[1,1]{1,0:T(1,128)}, s32[1,1]{1,0:T(1,128)}, s32[1,1]{1,0:T(1,128)}, s32[1,1]{1,0:T(1,128)}) fusion(s32[1,5]{1,0:T(1,128)} %param.34), kind=kLoop, calls=%fused_computation.272 | loop fusion | bytes 40 | tf_op jit(solution)/shard_map/slice | solution.py:157
  1.5 1.4 compare_and_fusion.1
  3.0 1.8 %copy.451 = bf16[8,8192]{0,1:T(8,128)(2,1)S(1)} copy(bf16[8,8192]{1,0:T(8,128)(2,1)} %param.32) | data formatting | bytes 262144 | tf_op args[0]
  5.6 13.0 %collective-permute-start = (bf16[8,128]{0,1:T(8,128)(2,1)S(1)}, bf16[8,128]{0,1:T(8,128)(2,1)S(1)}, u32[]{:S(2)}, u32[]{:S(2)}) collective-permute-start(bf16[8,128]{0,1:T(8,128)(2,1)S(1)} %bitcast_select_fusion.4), channel_id=1, source_target_pairs={{0,496},{8,504},{16,0},{24,8},{32,16},{40,24},{48,32},{56,40},{64,... | collective-permute-start | bytes 6152 | tf_op jit(solution)/shard_map/ppermute | solution.py:14
  20.1 2.5 %collective-permute-start.1 = (bf16[8,128]{0,1:T(8,128)(2,1)S(1)}, bf16[8,128]{0,1:T(8,128)(2,1)S(1)}, u32[]{:S(2)}, u32[]{:S(2)}) collective-permute-start(bf16[8,128]{0,1:T(8,128)(2,1)S(1)} %bitcast_select_fusion.3), channel_id=1, source_target_pairs={{0,504},{8,0},{16,8},{24,16},{32,24},{40,32},{48,40},{56,48},{64,5... | collective-permute-start | bytes 6152 | tf_op jit(solution)/shard_map/ppermute | solution.py:14
  24.0 1.9 %collective-permute-start.2 = (bf16[8,128]{0,1:T(8,128)(2,1)S(1)}, bf16[8,128]{0,1:T(8,128)(2,1)S(1)}, u32[]{:S(2)}, u32[]{:S(2)}) collective-permute-start(bf16[8,128]{0,1:T(8,128)(2,1)S(1)} %bitcast_select_fusion.1), channel_id=1, source_target_pairs={{0,8},{8,16},{16,24},{24,32},{32,40},{40,48},{48,56},{56,64},{64,7... | collective-permute-start | bytes 6152 | tf_op jit(solution)/shard_map/ppermute | solution.py:14
  27.4 4.0 %collective-permute-start.3 = (bf16[8,128]{0,1:T(8,128)(2,1)S(1)}, bf16[8,128]{0,1:T(8,128)(2,1)S(1)}, u32[]{:S(2)}, u32[]{:S(2)}) collective-permute-start(bf16[8,128]{0,1:T(8,128)(2,1)S(1)} %bitcast_select_fusion), channel_id=1, source_target_pairs={{0,16},{8,24},{16,32},{24,40},{32,48},{40,56},{48,64},{56,72},{64,... | collective-permute-start | bytes 6152 | tf_op jit(solution)/shard_map/ppermute | solution.py:14
  36.9 1.9 %reshape.376 = bf16[8,2,23040]{2,1,0:T(2,128)(2,1)} reshape(bf16[128,9,320]{2,1,0:T(8,128)(2,1)S(1)} %bitcast.283) | data formatting | bytes 1474560
  44.0 5.9 %all-to-all-start.1 = ((bf16[8,8,640]{2,1,0:T(8,128)(2,1)}), bf16[8,8,640]{2,1,0:T(8,128)(2,1)S(1)}, u32[]{:S(2)}, u32[]{:S(2)}) async-start(bf16[8,8,640]{2,1,0:T(8,128)(2,1)} %bitcast.27), calls=%async_computation.1 | async-start | bytes 163840 | tf_op jit(solution)/shard_map/all_to_all | solution.py:20
  49.9 5.0 %all-to-all-done.1 = bf16[8,8,640]{2,1,0:T(8,128)(2,1)S(1)} async-done(((bf16[8,8,640]{2,1,0:T(8,128)(2,1)}), bf16[8,8,640]{2,1,0:T(8,128)(2,1)S(1)}, u32[]{:S(2)}, u32[]{:S(2)}) %all-to-all-start.1) | async-done | bytes 81952 | tf_op jit(solution)/shard_map/all_to_all | solution.py:20
  54.9 4.8 %all-to-all-start = ((bf16[8,2,23040]{2,1,0:T(2,128)(2,1)}), bf16[8,2,23040]{2,1,0:T(2,128)(2,1)S(1)}, u32[]{:S(2)}, u32[]{:S(2)}) async-start(bf16[8,2,23040]{2,1,0:T(2,128)(2,1)} %reshape.376), calls=%async_computation | async-start | bytes 1474560 | tf_op jit(solution)/shard_map/all_to_all | solution.py:20
  63.2 3.4 %collective-permute-start.4 = (bf16[64,2,60]{0,1,2:T(2,128)(2,1)S(1)}, bf16[64,2,60]{0,1,2:T(2,128)(2,1)S(1)}, u32[]{:S(2)}, u32[]{:S(2)}) collective-permute-start(bf16[64,2,60]{0,1,2:T(2,128)(2,1)S(1)} %get-tuple-element.67), channel_id=1, source_target_pairs={{0,1},{1,2},{2,3},{3,4},{4,5},{5,6},{6,7},{7,8},{8,9},{9,10},{10,1... | collective-permute-start | bytes 46088 | tf_op jit(solution)/shard_map/ppermute | solution.py:30
  66.6 4.8 %collective-permute-start.5 = (bf16[64,2,60]{0,1,2:T(2,128)(2,1)S(1)}, bf16[64,2,60]{0,1,2:T(2,128)(2,1)S(1)}, u32[]{:S(2)}, u32[]{:S(2)}) collective-permute-start(bf16[64,2,60]{0,1,2:T(2,128)(2,1)S(1)} %get-tuple-element.68), channel_id=1, source_target_pairs={{1,0},{2,1},{3,2},{4,3},{5,4},{6,5},{7,6},{8,7},{9,8},{10,9},{11,1... | collective-permute-start | bytes 46088 | tf_op jit(solution)/shard_map/ppermute | solution.py:31
  71.5 1.2 collective-permute-done.5
  72.9 1.4 gather_fusion.1
  74.8 2.0 %gather_fusion.2 = bf16[324,64,4]{1,2,0:T(4,128)(2,1)S(1)} fusion(bf16[64,4,324]{0,1,2:T(4,128)(2,1)S(1)} %pad_maximum_fusion.2, s32[1024]{0:T(1024)S(1)} %get-tuple-element.84), kind=kCustom, calls=%fused_computation.15 | custom fusion | bytes 333072 | tf_op jit(solution)/shard_map/jit(_take)/gather | solution.py:107
  77.1 1.4 reshape.377
  85.6 1.1 fusion.18
  87.6 3.0 %collective-permute-start.6 = (bf16[128,2,60]{0,1,2:T(2,128)(2,1)S(1)}, bf16[128,2,60]{0,1,2:T(2,128)(2,1)S(1)}, u32[]{:S(2)}, u32[]{:S(2)}) collective-permute-start(bf16[128,2,60]{0,1,2:T(2,128)(2,1)S(1)} %get-tuple-element.65), channel_id=1, source_target_pairs={{0,1},{1,2},{2,3},{3,4},{4,5},{5,6},{6,7},{7,8},{8,9},{9,10},{10,1... | collective-permute-start | bytes 92168 | tf_op jit(solution)/shard_map/ppermute | solution.py:30
  90.6 5.5 %collective-permute-start.7 = (bf16[128,2,60]{0,1,2:T(2,128)(2,1)S(1)}, bf16[128,2,60]{0,1,2:T(2,128)(2,1)S(1)}, u32[]{:S(2)}, u32[]{:S(2)}) collective-permute-start(bf16[128,2,60]{0,1,2:T(2,128)(2,1)S(1)} %get-tuple-element.66), channel_id=1, source_target_pairs={{1,0},{2,1},{3,2},{4,3},{5,4},{6,5},{7,6},{8,7},{9,8},{10,9},{11,1... | collective-permute-start | bytes 92168 | tf_op jit(solution)/shard_map/ppermute | solution.py:31
  96.1 1.8 %fusion.93 = (bf16[1,128,128]{2,0,1:T(2,128)(2,1)S(1)}, bf16[1,128,128]{2,0,1:T(2,128)(2,1)S(1)}, bf16[1,128,128]{2,0,1:T(2,128)(2,1)S(1)}, bf16[1,128,128]{2,0,...) fusion(bf16[9,128,320]{2,0,1:T(8,128)(2,1)S(1)} %bitcast.273), kind=kLoop, calls=%fused_computation.267 | loop fusion | bytes 1179648 | tf_op jit(solution)/shard_map/slice | solution.py:115
  98.1 1.4 gather_fusion.11
  100.1 2.0 %gather_fusion.12 = bf16[324,128,4]{1,2,0:T(4,128)(2,1)S(1)} fusion(bf16[128,4,324]{0,1,2:T(4,128)(2,1)S(1)} %copy.491, s32[1024]{0:T(1024)S(1)} %get-tuple-element.84), kind=kCustom, calls=%fused_computation.4.clone | custom fusion | bytes 664848 | tf_op jit(solution)/shard_map/jit(_take)/gather | solution.py:107
  105.7 1.1 fusion.21
  107.6 1.9 %collective-permute-start.8 = (bf16[128,2,60]{0,1,2:T(2,128)(2,1)S(1)}, bf16[128,2,60]{0,1,2:T(2,128)(2,1)S(1)}, u32[]{:S(2)}, u32[]{:S(2)}) collective-permute-start(bf16[128,2,60]{0,1,2:T(2,128)(2,1)S(1)} %get-tuple-element.63), channel_id=1, source_target_pairs={{0,1},{1,2},{2,3},{3,4},{4,5},{5,6},{6,7},{7,8},{8,9},{9,10},{10,1... | collective-permute-start | bytes 92168 | tf_op jit(solution)/shard_map/ppermute | solution.py:30
  109.6 6.3 %collective-permute-start.9 = (bf16[128,2,60]{0,1,2:T(2,128)(2,1)S(1)}, bf16[128,2,60]{0,1,2:T(2,128)(2,1)S(1)}, u32[]{:S(2)}, u32[]{:S(2)}) collective-permute-start(bf16[128,2,60]{0,1,2:T(2,128)(2,1)S(1)} %get-tuple-element.64), channel_id=1, source_target_pairs={{1,0},{2,1},{3,2},{4,3},{5,4},{6,5},{7,6},{8,7},{9,8},{10,9},{11,1... | collective-permute-start | bytes 92168 | tf_op jit(solution)/shard_map/ppermute | solution.py:31
  115.9 1.3 collective-permute-done.9
  117.3 1.4 gather_fusion.14
  119.3 2.0 %gather_fusion.15 = bf16[324,128,4]{1,2,0:T(4,128)(2,1)S(1)} fusion(bf16[128,4,324]{0,1,2:T(4,128)(2,1)S(1)} %copy.513, s32[1024]{0:T(1024)S(1)} %get-tuple-element.84), kind=kCustom, calls=%fused_computation.12.clone | custom fusion | bytes 664848 | tf_op jit(solution)/shard_map/jit(_take)/gather | solution.py:107
  124.9 1.1 fusion.24
  126.2 17.1 %all_to_all.35 = bf16[128,4,256]{2,1,0:T(4,128)(2,1)S(1)} all-to-all(bf16[128,4,256]{2,1,0:T(4,128)(2,1)S(1)} %copy.532), channel_id=1, replica_groups=mesh['tile'=64,'chan'=8] {'chan'}, dimensions={0} | all-to-all | bytes 524288 | tf_op jit(solution)/shard_map/all_to_all | solution.py:187
  143.4 0.8 copy.535
  (196 shorter events, 37.3 us)
Async XLA Ops:
  0.0 31.5 %copy-start.7 = (s32[68]{0:T(128)S(1)}, s32[68]{0:T(128)}, u32[]{:S(2)}) copy-start(s32[68]{0:T(128)} %constant.306) | copy-start | bytes 820
  0.0 33.0 %copy-start.6 = (s32[68]{0:T(128)S(1)}, s32[68]{0:T(128)}, u32[]{:S(2)}) copy-start(s32[68]{0:T(128)} %constant.239) | copy-start | bytes 820
  0.0 31.5 %copy-start.3 = (s32[32,8]{0,1:T(8,128)S(1)}, s32[32,8]{0,1:T(8,128)}, u32[]{:S(2)}) copy-start(s32[32,8]{0,1:T(8,128)} %param.37) | copy-start | bytes 3076
  0.0 31.5 %copy-start.4 = (s32[32,8]{0,1:T(8,128)S(1)}, s32[32,8]{0,1:T(8,128)}, u32[]{:S(2)}) copy-start(s32[32,8]{0,1:T(8,128)} %param.38) | copy-start | bytes 3076
  0.0 36.0 %copy-start.2 = (bf16[9,16,64]{2,1,0:T(8,128)(2,1)S(1)}, bf16[9,16,64]{2,1,0:T(8,128)(2,1)}, u32[]{:S(2)}) copy-start(bf16[9,16,64]{2,1,0:T(8,128)(2,1)} %param.39) | copy-start | bytes 55300
  0.0 36.0 %copy-start.1 = (bf16[9,16,128]{2,1,0:T(8,128)(2,1)S(1)}, bf16[9,16,128]{2,1,0:T(8,128)(2,1)}, u32[]{:S(2)}) copy-start(bf16[9,16,128]{2,1,0:T(8,128)(2,1)} %param.40) | copy-start | bytes 110596
  0.0 36.0 %copy-start = (bf16[9,16,128]{2,1,0:T(8,128)(2,1)S(1)}, bf16[9,16,128]{2,1,0:T(8,128)(2,1)}, u32[]{:S(2)}) copy-start(bf16[9,16,128]{2,1,0:T(8,128)(2,1)} %param.41) | copy-start | bytes 110596
  5.6 33.1 %collective-permute-start = (bf16[8,128]{0,1:T(8,128)(2,1)S(1)}, bf16[8,128]{0,1:T(8,128)(2,1)S(1)}, u32[]{:S(2)}, u32[]{:S(2)}) collective-permute-start(bf16[8,128]{0,1:T(8,128)(2,1)S(1)} %bitcast_select_fusion.4), channel_id=1, source_target_pairs={{0,496},{8,504},{16,0},{24,8},{32,16},{40,24},{48,32},{56,40},{64,... | collective-permute-start | bytes 6152 | tf_op jit(solution)/shard_map/ppermute | solution.py:14
  20.1 18.7 %collective-permute-start.1 = (bf16[8,128]{0,1:T(8,128)(2,1)S(1)}, bf16[8,128]{0,1:T(8,128)(2,1)S(1)}, u32[]{:S(2)}, u32[]{:S(2)}) collective-permute-start(bf16[8,128]{0,1:T(8,128)(2,1)S(1)} %bitcast_select_fusion.3), channel_id=1, source_target_pairs={{0,504},{8,0},{16,8},{24,16},{32,24},{40,32},{48,40},{56,48},{64,5... | collective-permute-start | bytes 6152 | tf_op jit(solution)/shard_map/ppermute | solution.py:14
  24.0 14.9 %collective-permute-start.2 = (bf16[8,128]{0,1:T(8,128)(2,1)S(1)}, bf16[8,128]{0,1:T(8,128)(2,1)S(1)}, u32[]{:S(2)}, u32[]{:S(2)}) collective-permute-start(bf16[8,128]{0,1:T(8,128)(2,1)S(1)} %bitcast_select_fusion.1), channel_id=1, source_target_pairs={{0,8},{8,16},{16,24},{24,32},{32,40},{40,48},{48,56},{56,64},{64,7... | collective-permute-start | bytes 6152 | tf_op jit(solution)/shard_map/ppermute | solution.py:14
  25.9 10.7 %copy-start.5 = (s32[324]{0:T(512)S(1)}, s32[324]{0:T(512)}, u32[]{:S(2)}) copy-start(s32[324]{0:T(512)} %constant.220.clone) | copy-start | bytes 3892
  26.0 10.7 %copy-start.8 = (s32[60]{0:T(128)S(1)}, s32[60]{0:T(128)}, u32[]{:S(2)}) copy-start(s32[60]{0:T(128)} %constant.217.clone) | copy-start | bytes 724
  27.4 11.6 %collective-permute-start.3 = (bf16[8,128]{0,1:T(8,128)(2,1)S(1)}, bf16[8,128]{0,1:T(8,128)(2,1)S(1)}, u32[]{:S(2)}, u32[]{:S(2)}) collective-permute-start(bf16[8,128]{0,1:T(8,128)(2,1)S(1)} %bitcast_select_fusion), channel_id=1, source_target_pairs={{0,16},{8,24},{16,32},{24,40},{32,48},{40,56},{48,64},{56,72},{64,... | collective-permute-start | bytes 6152 | tf_op jit(solution)/shard_map/ppermute | solution.py:14
  44.0 11.0 %all-to-all-start.1 = ((bf16[8,8,640]{2,1,0:T(8,128)(2,1)}), bf16[8,8,640]{2,1,0:T(8,128)(2,1)S(1)}, u32[]{:S(2)}, u32[]{:S(2)}) async-start(bf16[8,8,640]{2,1,0:T(8,128)(2,1)} %bitcast.27), calls=%async_computation.1 | async-start | bytes 163840 | tf_op jit(solution)/shard_map/all_to_all | solution.py:20
  54.9 22.1 %all-to-all-start = ((bf16[8,2,23040]{2,1,0:T(2,128)(2,1)}), bf16[8,2,23040]{2,1,0:T(2,128)(2,1)S(1)}, u32[]{:S(2)}, u32[]{:S(2)}) async-start(bf16[8,2,23040]{2,1,0:T(2,128)(2,1)} %reshape.376), calls=%async_computation | async-start | bytes 1474560 | tf_op jit(solution)/shard_map/all_to_all | solution.py:20
  63.2 8.3 %collective-permute-start.4 = (bf16[64,2,60]{0,1,2:T(2,128)(2,1)S(1)}, bf16[64,2,60]{0,1,2:T(2,128)(2,1)S(1)}, u32[]{:S(2)}, u32[]{:S(2)}) collective-permute-start(bf16[64,2,60]{0,1,2:T(2,128)(2,1)S(1)} %get-tuple-element.67), channel_id=1, source_target_pairs={{0,1},{1,2},{2,3},{3,4},{4,5},{5,6},{6,7},{7,8},{8,9},{9,10},{10,1... | collective-permute-start | bytes 46088 | tf_op jit(solution)/shard_map/ppermute | solution.py:30
  66.6 6.1 %collective-permute-start.5 = (bf16[64,2,60]{0,1,2:T(2,128)(2,1)S(1)}, bf16[64,2,60]{0,1,2:T(2,128)(2,1)S(1)}, u32[]{:S(2)}, u32[]{:S(2)}) collective-permute-start(bf16[64,2,60]{0,1,2:T(2,128)(2,1)S(1)} %get-tuple-element.68), channel_id=1, source_target_pairs={{1,0},{2,1},{3,2},{4,3},{5,4},{6,5},{7,6},{8,7},{9,8},{10,9},{11,1... | collective-permute-start | bytes 46088 | tf_op jit(solution)/shard_map/ppermute | solution.py:31
  87.6 10.3 %collective-permute-start.6 = (bf16[128,2,60]{0,1,2:T(2,128)(2,1)S(1)}, bf16[128,2,60]{0,1,2:T(2,128)(2,1)S(1)}, u32[]{:S(2)}, u32[]{:S(2)}) collective-permute-start(bf16[128,2,60]{0,1,2:T(2,128)(2,1)S(1)} %get-tuple-element.65), channel_id=1, source_target_pairs={{0,1},{1,2},{2,3},{3,4},{4,5},{5,6},{6,7},{7,8},{8,9},{9,10},{10,1... | collective-permute-start | bytes 92168 | tf_op jit(solution)/shard_map/ppermute | solution.py:30
  90.6 7.3 %collective-permute-start.7 = (bf16[128,2,60]{0,1,2:T(2,128)(2,1)S(1)}, bf16[128,2,60]{0,1,2:T(2,128)(2,1)S(1)}, u32[]{:S(2)}, u32[]{:S(2)}) collective-permute-start(bf16[128,2,60]{0,1,2:T(2,128)(2,1)S(1)} %get-tuple-element.66), channel_id=1, source_target_pairs={{1,0},{2,1},{3,2},{4,3},{5,4},{6,5},{7,6},{8,7},{9,8},{10,9},{11,1... | collective-permute-start | bytes 92168 | tf_op jit(solution)/shard_map/ppermute | solution.py:31
  107.6 8.2 %collective-permute-start.8 = (bf16[128,2,60]{0,1,2:T(2,128)(2,1)S(1)}, bf16[128,2,60]{0,1,2:T(2,128)(2,1)S(1)}, u32[]{:S(2)}, u32[]{:S(2)}) collective-permute-start(bf16[128,2,60]{0,1,2:T(2,128)(2,1)S(1)} %get-tuple-element.63), channel_id=1, source_target_pairs={{0,1},{1,2},{2,3},{3,4},{4,5},{5,6},{6,7},{7,8},{8,9},{9,10},{10,1... | collective-permute-start | bytes 92168 | tf_op jit(solution)/shard_map/ppermute | solution.py:30
  109.6 7.6 %collective-permute-start.9 = (bf16[128,2,60]{0,1,2:T(2,128)(2,1)S(1)}, bf16[128,2,60]{0,1,2:T(2,128)(2,1)S(1)}, u32[]{:S(2)}, u32[]{:S(2)}) collective-permute-start(bf16[128,2,60]{0,1,2:T(2,128)(2,1)S(1)} %get-tuple-element.64), channel_id=1, source_target_pairs={{1,0},{2,1},{3,2},{4,3},{5,4},{6,5},{7,6},{8,7},{9,8},{10,9},{11,1... | collective-permute-start | bytes 92168 | tf_op jit(solution)/shard_map/ppermute | solution.py:31

commit v4 on v3

--- a/solution.py
+++ b/solution.py
@@ -16,7 +16,11 @@
 
 def gather_by_exchange(value, axis, dim):
     count = lax.axis_size(axis)
-    copies = jnp.concatenate([value] * count, axis=dim)
+    shape = value.shape
+    copies = jnp.broadcast_to(
+        jnp.expand_dims(value, dim), shape[:dim] + (count,) + shape[dim:]
+    )
+    copies = copies.reshape(shape[:dim] + (count * shape[dim],) + shape[dim + 1 :])
     return lax.all_to_all(copies, axis, split_axis=dim, concat_axis=dim, tiled=True)
 
 
@@ -159,7 +163,7 @@
         if offset_index != REACH:
             block = from_behind(block, "tile", offset_index - REACH)
         blocks.append(block)
-    arrived = jnp.stack(blocks, axis=1).reshape(channels_here, near_count * capacity)
+    arrived = jnp.concatenate(blocks, axis=1)
     arrived = gather_by_exchange(arrived, "chan", 0)
     group_index = lax.axis_index("chan")
     my_slots = lax.dynamic_slice_in_dim(corner_slot, group_index * per_group, per_group, 1)

time: 145 us -> 141 us (0.972)
  local copies, waits for them, and re-layouts: 40.2 us -> 36.3 us
    unnamed x61 -> x47, local copies, waits for them, and re-layouts: 13.2 us -> 8.7 us
where the time goes in v4:
time: 141 us; the launch traced here: 140 us
  starting transfers between devices  57 us (40%)
  local copies, waits for them, and re-layouts  36.3 us (26%)
  blocking collectives  17.1 us (12%)
  matrix products  11.3 us (8%)
  other arithmetic  9.83 us (7%)
  waiting for transfers between devices  7.57 us (5%)
    ppermute x4, starting transfers between devices, from_behind(): return lax.ppermute(value, axis, pairs)  21.4 us
    all_to_all x1, blocking collectives, on_device(): lax.all_to_all(activity, 'chan', split_axis=0, concat_axis=1, tiled=True)  17.1 us
    ppermute x3, starting transfers between devices, extended_2(): after = lax.ppermute(initial, axis, down)  16.5 us
    all_to_all x2, starting transfers between devices, gather_by_exchange(): lax.all_to_all(copies, axis, split_axis=dim, concat_axis=dim, tiled=True)  10.8 us
    dot_general x27, matrix products, conv_layer(): jnp.einsum('oc,ctq->otq', kernel[tap_index], window, preferred_element_ty...  8.83 us
    unnamed x47, local copies, waits for them, and re-layouts  8.7 us
    ppermute x3, starting transfers between devices, extended_2(): before = lax.ppermute(last, axis, up)  8.32 us
    gather x6, local copies, waits for them, and re-layouts, conv_layer(): padded = jnp.take(joined, layout_table(P_SIZE), axis=2)  6.41 us
  transfers between devices with their start and end apart: 12, of which 3 were waited for; matrix products, arithmetic and copies ran while one was open for 15% of the time, Pallas kernels for 0%

profile of v4, /device:TPU:2, one launch (start us, length us, event | category | flops | bytes accessed | tf_op | source)
XLA Modules:
  0.0 140.3 jit_solution(9293134772552719352)
XLA Ops:
  0.1 1.5 %fusion.97 = (s32[1,1]{1,0:T(1,128)}, s32[1,1]{1,0:T(1,128)}, s32[1,1]{1,0:T(1,128)}, s32[1,1]{1,0:T(1,128)}, s32[1,1]{1,0:T(1,128)}) fusion(s32[1,5]{1,0:T(1,128)} %param.34), kind=kLoop, calls=%fused_computation.255 | loop fusion | bytes 40 | tf_op jit(solution)/shard_map/slice | solution.py:161
  1.6 1.4 %compare_and_fusion.1 = (pred[128]{0:T(512)(128)(4,1)S(1)}, s32[128]{0:T(128)S(1)}, pred[128]{0:T(512)(128)(4,1)S(1)}, s32[128]{0:T(128)S(1)}, pred[128]{0:T(512...) fusion(s32[1,5,128]{2,0,1:T(1,128)} %param.33, ...), kind=kLoop, calls=%fused_computation.238 | loop fusion | flops 3968 | bytes 5892 | tf_op jit(solution)/shard_map/jit(_take)/and | solution.py:160
  3.0 1.8 %copy.336 = bf16[8,8192]{0,1:T(8,128)(2,1)S(1)} copy(bf16[8,8192]{1,0:T(8,128)(2,1)} %param.32) | data formatting | bytes 262144 | tf_op args[0]
  5.6 13.0 %collective-permute-start = (bf16[8,128]{0,1:T(8,128)(2,1)S(1)}, bf16[8,128]{0,1:T(8,128)(2,1)S(1)}, u32[]{:S(2)}, u32[]{:S(2)}) collective-permute-start(bf16[8,128]{0,1:T(8,128)(2,1)S(1)} %bitcast_select_fusion.4), channel_id=1, source_target_pairs={{0,496},{8,504},{16,0},{24,8},{32,16},{40,24},{48,32},{56,40},{64,... | collective-permute-start | bytes 6152 | tf_op jit(solution)/shard_map/ppermute | solution.py:14
  20.1 2.5 %collective-permute-start.1 = (bf16[8,128]{0,1:T(8,128)(2,1)S(1)}, bf16[8,128]{0,1:T(8,128)(2,1)S(1)}, u32[]{:S(2)}, u32[]{:S(2)}) collective-permute-start(bf16[8,128]{0,1:T(8,128)(2,1)S(1)} %bitcast_select_fusion.3), channel_id=1, source_target_pairs={{0,504},{8,0},{16,8},{24,16},{32,24},{40,32},{48,40},{56,48},{64,5... | collective-permute-start | bytes 6152 | tf_op jit(solution)/shard_map/ppermute | solution.py:14
  24.0 1.9 %collective-permute-start.2 = (bf16[8,128]{0,1:T(8,128)(2,1)S(1)}, bf16[8,128]{0,1:T(8,128)(2,1)S(1)}, u32[]{:S(2)}, u32[]{:S(2)}) collective-permute-start(bf16[8,128]{0,1:T(8,128)(2,1)S(1)} %bitcast_select_fusion.1), channel_id=1, source_target_pairs={{0,8},{8,16},{16,24},{24,32},{32,40},{40,48},{48,56},{56,64},{64,7... | collective-permute-start | bytes 6152 | tf_op jit(solution)/shard_map/ppermute | solution.py:14
  27.4 4.0 %collective-permute-start.3 = (bf16[8,128]{0,1:T(8,128)(2,1)S(1)}, bf16[8,128]{0,1:T(8,128)(2,1)S(1)}, u32[]{:S(2)}, u32[]{:S(2)}) collective-permute-start(bf16[8,128]{0,1:T(8,128)(2,1)S(1)} %bitcast_select_fusion), channel_id=1, source_target_pairs={{0,16},{8,24},{16,32},{24,40},{32,48},{40,56},{48,64},{56,72},{64,... | collective-permute-start | bytes 6152 | tf_op jit(solution)/shard_map/ppermute | solution.py:14
  37.1 1.9 %reshape.380 = bf16[8,2,23040]{2,1,0:T(2,128)(2,1)} reshape(bf16[128,9,320]{2,1,0:T(8,128)(2,1)S(1)} %bitcast.259) | data formatting | bytes 1474560
  40.1 5.9 %all-to-all-start.1 = ((bf16[8,8,640]{2,1,0:T(8,128)(2,1)}), bf16[8,8,640]{2,1,0:T(8,128)(2,1)S(1)}, u32[]{:S(2)}, u32[]{:S(2)}) async-start(bf16[8,8,640]{2,1,0:T(8,128)(2,1)} %broadcast_in_dim.144), calls=%async_computation.1 | async-start | bytes 163840 | tf_op jit(solution)/shard_map/all_to_all | solution.py:24
  46.0 5.0 %all-to-all-done.1 = bf16[8,8,640]{2,1,0:T(8,128)(2,1)S(1)} async-done(((bf16[8,8,640]{2,1,0:T(8,128)(2,1)}), bf16[8,8,640]{2,1,0:T(8,128)(2,1)S(1)}, u32[]{:S(2)}, u32[]{:S(2)}) %all-to-all-start.1) | async-done | bytes 81952 | tf_op jit(solution)/shard_map/all_to_all | solution.py:24
  51.0 4.8 %all-to-all-start = ((bf16[8,2,23040]{2,1,0:T(2,128)(2,1)}), bf16[8,2,23040]{2,1,0:T(2,128)(2,1)S(1)}, u32[]{:S(2)}, u32[]{:S(2)}) async-start(bf16[8,2,23040]{2,1,0:T(2,128)(2,1)} %reshape.380), calls=%async_computation | async-start | bytes 1474560 | tf_op jit(solution)/shard_map/all_to_all | solution.py:24
  59.3 3.4 %collective-permute-start.4 = (bf16[64,2,60]{0,1,2:T(2,128)(2,1)S(1)}, bf16[64,2,60]{0,1,2:T(2,128)(2,1)S(1)}, u32[]{:S(2)}, u32[]{:S(2)}) collective-permute-start(bf16[64,2,60]{0,1,2:T(2,128)(2,1)S(1)} %get-tuple-element.67), channel_id=1, source_target_pairs={{0,1},{1,2},{2,3},{3,4},{4,5},{5,6},{6,7},{7,8},{8,9},{9,10},{10,1... | collective-permute-start | bytes 46088 | tf_op jit(solution)/shard_map/ppermute | solution.py:34
  62.7 4.8 %collective-permute-start.5 = (bf16[64,2,60]{0,1,2:T(2,128)(2,1)S(1)}, bf16[64,2,60]{0,1,2:T(2,128)(2,1)S(1)}, u32[]{:S(2)}, u32[]{:S(2)}) collective-permute-start(bf16[64,2,60]{0,1,2:T(2,128)(2,1)S(1)} %get-tuple-element.68), channel_id=1, source_target_pairs={{1,0},{2,1},{3,2},{4,3},{5,4},{6,5},{7,6},{8,7},{9,8},{10,9},{11,1... | collective-permute-start | bytes 46088 | tf_op jit(solution)/shard_map/ppermute | solution.py:35
  67.6 1.2 collective-permute-done.5
  69.1 1.4 gather_fusion.1
  70.9 2.0 %gather_fusion.2 = bf16[324,64,4]{1,2,0:T(4,128)(2,1)S(1)} fusion(bf16[64,4,324]{0,1,2:T(4,128)(2,1)S(1)} %pad_maximum_fusion.2, s32[1024]{0:T(1024)S(1)} %get-tuple-element.84), kind=kCustom, calls=%fused_computation.15 | custom fusion | bytes 333072 | tf_op jit(solution)/shard_map/jit(_take)/gather | solution.py:111
  73.2 1.4 reshape.381
  81.7 1.1 fusion.18
  83.7 3.0 %collective-permute-start.6 = (bf16[128,2,60]{0,1,2:T(2,128)(2,1)S(1)}, bf16[128,2,60]{0,1,2:T(2,128)(2,1)S(1)}, u32[]{:S(2)}, u32[]{:S(2)}) collective-permute-start(bf16[128,2,60]{0,1,2:T(2,128)(2,1)S(1)} %get-tuple-element.65), channel_id=1, source_target_pairs={{0,1},{1,2},{2,3},{3,4},{4,5},{5,6},{6,7},{7,8},{8,9},{9,10},{10,1... | collective-permute-start | bytes 92168 | tf_op jit(solution)/shard_map/ppermute | solution.py:34
  86.7 5.4 %collective-permute-start.7 = (bf16[128,2,60]{0,1,2:T(2,128)(2,1)S(1)}, bf16[128,2,60]{0,1,2:T(2,128)(2,1)S(1)}, u32[]{:S(2)}, u32[]{:S(2)}) collective-permute-start(bf16[128,2,60]{0,1,2:T(2,128)(2,1)S(1)} %get-tuple-element.66), channel_id=1, source_target_pairs={{1,0},{2,1},{3,2},{4,3},{5,4},{6,5},{7,6},{8,7},{9,8},{10,9},{11,1... | collective-permute-start | bytes 92168 | tf_op jit(solution)/shard_map/ppermute | solution.py:35
  92.2 1.8 %fusion.92 = (bf16[1,128,128]{2,0,1:T(2,128)(2,1)S(1)}, bf16[1,128,128]{2,0,1:T(2,128)(2,1)S(1)}, bf16[1,128,128]{2,0,1:T(2,128)(2,1)S(1)}, bf16[1,128,128]{2,0,...) fusion(bf16[9,128,320]{2,0,1:T(8,128)(2,1)S(1)} %bitcast.258), kind=kLoop, calls=%fused_computation.250 | loop fusion | bytes 1179648 | tf_op jit(solution)/shard_map/slice | solution.py:119
  94.2 1.4 gather_fusion.11
  96.2 2.0 %gather_fusion.12 = bf16[324,128,4]{1,2,0:T(4,128)(2,1)S(1)} fusion(bf16[128,4,324]{0,1,2:T(4,128)(2,1)S(1)} %copy.376, s32[1024]{0:T(1024)S(1)} %get-tuple-element.84), kind=kCustom, calls=%fused_computation.4.clone | custom fusion | bytes 664848 | tf_op jit(solution)/shard_map/jit(_take)/gather | solution.py:111
  101.8 1.1 fusion.21
  103.8 1.9 %collective-permute-start.8 = (bf16[128,2,60]{0,1,2:T(2,128)(2,1)S(1)}, bf16[128,2,60]{0,1,2:T(2,128)(2,1)S(1)}, u32[]{:S(2)}, u32[]{:S(2)}) collective-permute-start(bf16[128,2,60]{0,1,2:T(2,128)(2,1)S(1)} %get-tuple-element.63), channel_id=1, source_target_pairs={{0,1},{1,2},{2,3},{3,4},{4,5},{5,6},{6,7},{7,8},{8,9},{9,10},{10,1... | collective-permute-start | bytes 92168 | tf_op jit(solution)/shard_map/ppermute | solution.py:34
  105.7 6.3 %collective-permute-start.9 = (bf16[128,2,60]{0,1,2:T(2,128)(2,1)S(1)}, bf16[128,2,60]{0,1,2:T(2,128)(2,1)S(1)}, u32[]{:S(2)}, u32[]{:S(2)}) collective-permute-start(bf16[128,2,60]{0,1,2:T(2,128)(2,1)S(1)} %get-tuple-element.64), channel_id=1, source_target_pairs={{1,0},{2,1},{3,2},{4,3},{5,4},{6,5},{7,6},{8,7},{9,8},{10,9},{11,1... | collective-permute-start | bytes 92168 | tf_op jit(solution)/shard_map/ppermute | solution.py:35
  112.0 1.3 collective-permute-done.9
  113.5 1.4 gather_fusion.14
  115.4 2.0 %gather_fusion.15 = bf16[324,128,4]{1,2,0:T(4,128)(2,1)S(1)} fusion(bf16[128,4,324]{0,1,2:T(4,128)(2,1)S(1)} %copy.398, s32[1024]{0:T(1024)S(1)} %get-tuple-element.84), kind=kCustom, calls=%fused_computation.12.clone | custom fusion | bytes 664848 | tf_op jit(solution)/shard_map/jit(_take)/gather | solution.py:111
  121.0 1.1 fusion.24
  122.3 17.1 %all_to_all.32 = bf16[128,4,256]{2,1,0:T(4,128)(2,1)S(1)} all-to-all(bf16[128,4,256]{2,1,0:T(4,128)(2,1)S(1)} %copy.417), channel_id=1, replica_groups=mesh['tile'=64,'chan'=8] {'chan'}, dimensions={0} | all-to-all | bytes 524288 | tf_op jit(solution)/shard_map/all_to_all | solution.py:191
  139.5 0.8 copy.420
  (183 shorter events, 33.5 us)
Async XLA Ops:
  0.0 31.5 %copy-start.7 = (s32[68]{0:T(128)S(1)}, s32[68]{0:T(128)}, u32[]{:S(2)}) copy-start(s32[68]{0:T(128)} %constant.306) | copy-start | bytes 820
  0.0 33.0 %copy-start.6 = (s32[68]{0:T(128)S(1)}, s32[68]{0:T(128)}, u32[]{:S(2)}) copy-start(s32[68]{0:T(128)} %constant.239) | copy-start | bytes 820
  0.0 36.3 %copy-start.8 = (s32[60]{0:T(128)S(1)}, s32[60]{0:T(128)}, u32[]{:S(2)}) copy-start(s32[60]{0:T(128)} %constant.217.clone) | copy-start | bytes 724
  0.0 36.3 %copy-start.5 = (s32[324]{0:T(512)S(1)}, s32[324]{0:T(512)}, u32[]{:S(2)}) copy-start(s32[324]{0:T(512)} %constant.220.clone) | copy-start | bytes 3892
  0.0 31.5 %copy-start.3 = (s32[32,8]{0,1:T(8,128)S(1)}, s32[32,8]{0,1:T(8,128)}, u32[]{:S(2)}) copy-start(s32[32,8]{0,1:T(8,128)} %param.37) | copy-start | bytes 3076
  0.0 31.5 %copy-start.4 = (s32[32,8]{0,1:T(8,128)S(1)}, s32[32,8]{0,1:T(8,128)}, u32[]{:S(2)}) copy-start(s32[32,8]{0,1:T(8,128)} %param.38) | copy-start | bytes 3076
  0.0 36.1 %copy-start.2 = (bf16[9,16,64]{2,1,0:T(8,128)(2,1)S(1)}, bf16[9,16,64]{2,1,0:T(8,128)(2,1)}, u32[]{:S(2)}) copy-start(bf16[9,16,64]{2,1,0:T(8,128)(2,1)} %param.39) | copy-start | bytes 55300
  0.1 36.1 %copy-start.1 = (bf16[9,16,128]{2,1,0:T(8,128)(2,1)S(1)}, bf16[9,16,128]{2,1,0:T(8,128)(2,1)}, u32[]{:S(2)}) copy-start(bf16[9,16,128]{2,1,0:T(8,128)(2,1)} %param.40) | copy-start | bytes 110596
  0.1 36.1 %copy-start = (bf16[9,16,128]{2,1,0:T(8,128)(2,1)S(1)}, bf16[9,16,128]{2,1,0:T(8,128)(2,1)}, u32[]{:S(2)}) copy-start(bf16[9,16,128]{2,1,0:T(8,128)(2,1)} %param.41) | copy-start | bytes 110596
  5.6 33.4 %collective-permute-start = (bf16[8,128]{0,1:T(8,128)(2,1)S(1)}, bf16[8,128]{0,1:T(8,128)(2,1)S(1)}, u32[]{:S(2)}, u32[]{:S(2)}) collective-permute-start(bf16[8,128]{0,1:T(8,128)(2,1)S(1)} %bitcast_select_fusion.4), channel_id=1, source_target_pairs={{0,496},{8,504},{16,0},{24,8},{32,16},{40,24},{48,32},{56,40},{64,... | collective-permute-start | bytes 6152 | tf_op jit(solution)/shard_map/ppermute | solution.py:14
  20.1 19.0 %collective-permute-start.1 = (bf16[8,128]{0,1:T(8,128)(2,1)S(1)}, bf16[8,128]{0,1:T(8,128)(2,1)S(1)}, u32[]{:S(2)}, u32[]{:S(2)}) collective-permute-start(bf16[8,128]{0,1:T(8,128)(2,1)S(1)} %bitcast_select_fusion.3), channel_id=1, source_target_pairs={{0,504},{8,0},{16,8},{24,16},{32,24},{40,32},{48,40},{56,48},{64,5... | collective-permute-start | bytes 6152 | tf_op jit(solution)/shard_map/ppermute | solution.py:14
  24.0 15.2 %collective-permute-start.2 = (bf16[8,128]{0,1:T(8,128)(2,1)S(1)}, bf16[8,128]{0,1:T(8,128)(2,1)S(1)}, u32[]{:S(2)}, u32[]{:S(2)}) collective-permute-start(bf16[8,128]{0,1:T(8,128)(2,1)S(1)} %bitcast_select_fusion.1), channel_id=1, source_target_pairs={{0,8},{8,16},{16,24},{24,32},{32,40},{40,48},{48,56},{56,64},{64,7... | collective-permute-start | bytes 6152 | tf_op jit(solution)/shard_map/ppermute | solution.py:14
  27.4 11.9 %collective-permute-start.3 = (bf16[8,128]{0,1:T(8,128)(2,1)S(1)}, bf16[8,128]{0,1:T(8,128)(2,1)S(1)}, u32[]{:S(2)}, u32[]{:S(2)}) collective-permute-start(bf16[8,128]{0,1:T(8,128)(2,1)S(1)} %bitcast_select_fusion), channel_id=1, source_target_pairs={{0,16},{8,24},{16,32},{24,40},{32,48},{40,56},{48,64},{56,72},{64,... | collective-permute-start | bytes 6152 | tf_op jit(solution)/shard_map/ppermute | solution.py:14
  40.1 11.0 %all-to-all-start.1 = ((bf16[8,8,640]{2,1,0:T(8,128)(2,1)}), bf16[8,8,640]{2,1,0:T(8,128)(2,1)S(1)}, u32[]{:S(2)}, u32[]{:S(2)}) async-start(bf16[8,8,640]{2,1,0:T(8,128)(2,1)} %broadcast_in_dim.144), calls=%async_computation.1 | async-start | bytes 163840 | tf_op jit(solution)/shard_map/all_to_all | solution.py:24
  51.0 22.1 %all-to-all-start = ((bf16[8,2,23040]{2,1,0:T(2,128)(2,1)}), bf16[8,2,23040]{2,1,0:T(2,128)(2,1)S(1)}, u32[]{:S(2)}, u32[]{:S(2)}) async-start(bf16[8,2,23040]{2,1,0:T(2,128)(2,1)} %reshape.380), calls=%async_computation | async-start | bytes 1474560 | tf_op jit(solution)/shard_map/all_to_all | solution.py:24
  59.3 8.3 %collective-permute-start.4 = (bf16[64,2,60]{0,1,2:T(2,128)(2,1)S(1)}, bf16[64,2,60]{0,1,2:T(2,128)(2,1)S(1)}, u32[]{:S(2)}, u32[]{:S(2)}) collective-permute-start(bf16[64,2,60]{0,1,2:T(2,128)(2,1)S(1)} %get-tuple-element.67), channel_id=1, source_target_pairs={{0,1},{1,2},{2,3},{3,4},{4,5},{5,6},{6,7},{7,8},{8,9},{9,10},{10,1... | collective-permute-start | bytes 46088 | tf_op jit(solution)/shard_map/ppermute | solution.py:34
  62.7 6.1 %collective-permute-start.5 = (bf16[64,2,60]{0,1,2:T(2,128)(2,1)S(1)}, bf16[64,2,60]{0,1,2:T(2,128)(2,1)S(1)}, u32[]{:S(2)}, u32[]{:S(2)}) collective-permute-start(bf16[64,2,60]{0,1,2:T(2,128)(2,1)S(1)} %get-tuple-element.68), channel_id=1, source_target_pairs={{1,0},{2,1},{3,2},{4,3},{5,4},{6,5},{7,6},{8,7},{9,8},{10,9},{11,1... | collective-permute-start | bytes 46088 | tf_op jit(solution)/shard_map/ppermute | solution.py:35
  83.7 10.3 %collective-permute-start.6 = (bf16[128,2,60]{0,1,2:T(2,128)(2,1)S(1)}, bf16[128,2,60]{0,1,2:T(2,128)(2,1)S(1)}, u32[]{:S(2)}, u32[]{:S(2)}) collective-permute-start(bf16[128,2,60]{0,1,2:T(2,128)(2,1)S(1)} %get-tuple-element.65), channel_id=1, source_target_pairs={{0,1},{1,2},{2,3},{3,4},{4,5},{5,6},{6,7},{7,8},{8,9},{9,10},{10,1... | collective-permute-start | bytes 92168 | tf_op jit(solution)/shard_map/ppermute | solution.py:34
  86.7 7.3 %collective-permute-start.7 = (bf16[128,2,60]{0,1,2:T(2,128)(2,1)S(1)}, bf16[128,2,60]{0,1,2:T(2,128)(2,1)S(1)}, u32[]{:S(2)}, u32[]{:S(2)}) collective-permute-start(bf16[128,2,60]{0,1,2:T(2,128)(2,1)S(1)} %get-tuple-element.66), channel_id=1, source_target_pairs={{1,0},{2,1},{3,2},{4,3},{5,4},{6,5},{7,6},{8,7},{9,8},{10,9},{11,1... | collective-permute-start | bytes 92168 | tf_op jit(solution)/shard_map/ppermute | solution.py:35
  103.8 8.2 %collective-permute-start.8 = (bf16[128,2,60]{0,1,2:T(2,128)(2,1)S(1)}, bf16[128,2,60]{0,1,2:T(2,128)(2,1)S(1)}, u32[]{:S(2)}, u32[]{:S(2)}) collective-permute-start(bf16[128,2,60]{0,1,2:T(2,128)(2,1)S(1)} %get-tuple-element.63), channel_id=1, source_target_pairs={{0,1},{1,2},{2,3},{3,4},{4,5},{5,6},{6,7},{7,8},{8,9},{9,10},{10,1... | collective-permute-start | bytes 92168 | tf_op jit(solution)/shard_map/ppermute | solution.py:34
  105.7 7.6 %collective-permute-start.9 = (bf16[128,2,60]{0,1,2:T(2,128)(2,1)S(1)}, bf16[128,2,60]{0,1,2:T(2,128)(2,1)S(1)}, u32[]{:S(2)}, u32[]{:S(2)}) collective-permute-start(bf16[128,2,60]{0,1,2:T(2,128)(2,1)S(1)} %get-tuple-element.64), channel_id=1, source_target_pairs={{1,0},{2,1},{3,2},{4,3},{5,4},{6,5},{7,6},{8,7},{9,8},{10,9},{11,1... | collective-permute-start | bytes 92168 | tf_op jit(solution)/shard_map/ppermute | solution.py:35

commit v5 on v4

--- a/solution.py
+++ b/solution.py
@@ -148,23 +148,34 @@
     per_group = tiles_here // groups
     widths = [kernel_one.shape[2], kernel_two.shape[2], kernel_three.shape[2]]
     joined_kernels = jnp.concatenate([kernel_one, kernel_two, kernel_three], axis=2)
-    joined_kernels = gather_by_exchange(joined_kernels, "chan", 1)
+    slot_order = jnp.arange(capacity)
+    picked = []
+    for offset_index in range(near_count):
+        block = jnp.take(analysis, send_rows[0, offset_index], axis=1)
+        is_live = slot_order < send_count[0, offset_index]
+        picked.append(jnp.where(is_live[None, :], block, jnp.zeros((), block.dtype)))
+    pieces = jnp.concatenate(picked, axis=1)
+    piece_size = pieces.size
+    payload = jnp.concatenate([pieces.reshape(-1), joined_kernels.reshape(-1)])
+    received = gather_by_exchange(payload[None], "chan", 0)
+    pieces = received[:, :piece_size].reshape(groups * channels_here, near_count * capacity)
+    joined_kernels = received[:, piece_size:].reshape((groups,) + joined_kernels.shape)
+    joined_kernels = jnp.transpose(joined_kernels, (1, 0, 2, 3))
+    joined_kernels = joined_kernels.reshape(
+        joined_kernels.shape[0], groups * joined_kernels.shape[2], joined_kernels.shape[3]
+    )
     kernels = []
     low = 0
     for width in widths:
         kernels.append(joined_kernels[:, :, low : low + width])
         low += width
-    slot_order = jnp.arange(capacity)
     blocks = []
     for offset_index in range(near_count):
-        block = jnp.take(analysis, send_rows[0, offset_index], axis=1)
-        is_live = slot_order < send_count[0, offset_index]
-        block = jnp.where(is_live[None, :], block, jnp.zeros((), block.dtype))
+        block = pieces[:, offset_index * capacity : (offset_index + 1) * capacity]
         if offset_index != REACH:
             block = from_behind(block, "tile", offset_index - REACH)
         blocks.append(block)
     arrived = jnp.concatenate(blocks, axis=1)
-    arrived = gather_by_exchange(arrived, "chan", 0)
     group_index = lax.axis_index("chan")
     my_slots = lax.dynamic_slice_in_dim(corner_slot, group_index * per_group, per_group, 1)
     my_weights = lax.dynamic_slice_in_dim(corner_weight, group_index * per_group, per_group, 1)

time: 141 us -> 155 us (1.099)
  waiting for transfers between devices: 7.57 us -> 17.5 us
  other arithmetic: 9.83 us -> 16.2 us
  local copies, waits for them, and re-layouts: 36.3 us -> 34 us
  starting transfers between devices: 57 us -> 55.1 us
    ppermute x4, waiting for transfers between devices: 0.02 us -> 8.53 us  [from_behind(): return lax.ppermute(value, axis, pairs)]
    reshape x0 -> x1, other arithmetic: none -> 5.82 us  [gather_by_exchange(): copies.reshape(shape[:dim] + (count * shape[dim],) + shape[dim + 1:])]
    slice x2 -> x4, local copies, waits for them, and re-layouts: 2.27 us -> 0.08 us  [the longest x1 0.05 us: on_device(): received[:, piece_size:].reshape((groups,) + joined_kernels.shape)]
    all_to_all x2 -> x1, starting transfers between devices: 10.8 us -> 9.35 us  [gather_by_exchange(): lax.all_to_all(copies, axis, split_axis=dim, concat_axis=dim, tiled=True)]
    unnamed x47 -> x36, local copies, waits for them, and re-layouts: 8.7 us -> 7.42 us
    lt x4 -> x5, other arithmetic: 2.46 us -> 3.17 us  [on_device(): is_live = slot_order < send_count[0, offset_index]]
    all_to_all x2 -> x1, waiting for transfers between devices: 5.03 us -> 5.57 us  [gather_by_exchange(): lax.all_to_all(copies, axis, split_axis=dim, concat_axis=dim, tiled=True)]
  transfers between devices with their start and end apart: 12 -> 11, of which waited for: 3 -> 7; matrix products, arithmetic and copies ran while one was open for 15% -> 3% of each run, Pallas kernels for 0% -> 0%
where the time goes in v5:
time: 155 us; the launch traced here: 154 us
  starting transfers between devices  55.1 us (36%)
  local copies, waits for them, and re-layouts  34 us (22%)
  waiting for transfers between devices  17.5 us (11%)
  blocking collectives  17.4 us (11%)
  other arithmetic  16.2 us (10%)
  matrix products  12.5 us (8%)
    ppermute x4, starting transfers between devices, from_behind(): return lax.ppermute(value, axis, pairs)  21.1 us
    ppermute x3, starting transfers between devices, extended_2(): after = lax.ppermute(initial, axis, down)  17.8 us
    all_to_all x1, blocking collectives, on_device(): lax.all_to_all(activity, 'chan', split_axis=0, concat_axis=1, tiled=True)  17.4 us
    dot_general x27, matrix products, conv_layer(): jnp.einsum('oc,ctq->otq', kernel[tap_index], window, preferred_element_ty...  10.1 us
    all_to_all x1, starting transfers between devices, gather_by_exchange(): lax.all_to_all(copies, axis, split_axis=dim, concat_axis=dim, tiled=True)  9.35 us
    ppermute x4, waiting for transfers between devices, from_behind(): return lax.ppermute(value, axis, pairs)  8.53 us
    unnamed x36, local copies, waits for them, and re-layouts  7.42 us
    ppermute x3, starting transfers between devices, extended_2(): before = lax.ppermute(last, axis, up)  6.9 us
  transfers between devices with their start and end apart: 11, of which 7 were waited for; matrix products, arithmetic and copies ran while one was open for 3% of the time, Pallas kernels for 0%

profile of v5, /device:TPU:2, one launch (start us, length us, event | category | flops | bytes accessed | tf_op | source)
XLA Modules:
  0.0 153.9 jit_solution(13693389602400568374)
XLA Ops:
  0.0 1.5 fusion.84
  5.5 0.9 pad_maximum_fusion.6
  6.6 1.9 %copy.258 = bf16[8,8192]{0,1:T(8,128)(2,1)S(1)} copy(bf16[8,8192]{1,0:T(8,128)(2,1)} %param.32) | data formatting | bytes 262144 | tf_op args[0]
  14.3 5.8 %reduce.2 = bf16[8,51200]{1,0:T(8,128)(2,1)S(1)} reduce(bf16[8,1,51200]{2,1,0:T(2,128)(2,1)S(1)} %reshape.195, bf16[]{:T(256)} %broadcast.443), dimensions={1}, to_apply=%reshape.195.reduce_sub_computation | reduce | bytes 1638402 | tf_op jit(solution)/shard_map/reshape | solution.py:23
  20.1 1.6 %reshape.402 = bf16[8,2,25600]{2,1,0:T(2,128)(2,1)} reshape(bf16[8,51200]{1,0:T(8,128)(2,1)S(1)} %reduce.2) | data formatting | bytes 1638400
  21.7 9.3 %all-to-all-start = ((bf16[8,2,25600]{2,1,0:T(2,128)(2,1)}), bf16[8,2,25600]{2,1,0:T(2,128)(2,1)S(1)}, u32[]{:S(2)}, u32[]{:S(2)}) async-start(bf16[8,2,25600]{2,1,0:T(2,128)(2,1)} %reshape.402), calls=%async_computation | async-start | bytes 1638400 | tf_op jit(solution)/shard_map/all_to_all | solution.py:24
  34.3 5.6 %all-to-all-done = bf16[8,2,25600]{2,1,0:T(2,128)(2,1)S(1)} async-done(((bf16[8,2,25600]{2,1,0:T(2,128)(2,1)}), bf16[8,2,25600]{2,1,0:T(2,128)(2,1)S(1)}, u32[]{:S(2)}, u32[]{:S(2)}) %all-to-all-start) | async-done | bytes 819232 | tf_op jit(solution)/shard_map/all_to_all | solution.py:24
  41.2 12.5 %collective-permute-start = (bf16[64,128]{1,0:T(8,128)(2,1)S(1)}, bf16[64,128]{1,0:T(8,128)(2,1)S(1)}, u32[]{:S(2)}, u32[]{:S(2)}) collective-permute-start(bf16[64,128]{1,0:T(8,128)(2,1)S(1)} %get-tuple-element.40), channel_id=1, source_target_pairs={{0,496},{8,504},{16,0},{24,8},{32,16},{40,24},{48,32},{56,40},{64,... | collective-permute-start | bytes 49160 | tf_op jit(solution)/shard_map/ppermute | solution.py:14
  53.7 2.4 %collective-permute-start.1 = (bf16[64,128]{1,0:T(8,128)(2,1)S(1)}, bf16[64,128]{1,0:T(8,128)(2,1)S(1)}, u32[]{:S(2)}, u32[]{:S(2)}) collective-permute-start(bf16[64,128]{1,0:T(8,128)(2,1)S(1)} %get-tuple-element.39), channel_id=1, source_target_pairs={{0,504},{8,0},{16,8},{24,16},{32,24},{40,32},{48,40},{56,48},{64,5... | collective-permute-start | bytes 49160 | tf_op jit(solution)/shard_map/ppermute | solution.py:14
  56.1 1.4 collective-permute-done.1
  57.5 4.1 %collective-permute-start.2 = (bf16[64,128]{1,0:T(8,128)(2,1)S(1)}, bf16[64,128]{1,0:T(8,128)(2,1)S(1)}, u32[]{:S(2)}, u32[]{:S(2)}) collective-permute-start(bf16[64,128]{1,0:T(8,128)(2,1)S(1)} %get-tuple-element.37), channel_id=1, source_target_pairs={{0,8},{8,16},{16,24},{24,32},{32,40},{40,48},{48,56},{56,64},{64,7... | collective-permute-start | bytes 49160 | tf_op jit(solution)/shard_map/ppermute | solution.py:14
  61.8 2.1 %collective-permute-start.3 = (bf16[64,128]{1,0:T(8,128)(2,1)S(1)}, bf16[64,128]{1,0:T(8,128)(2,1)S(1)}, u32[]{:S(2)}, u32[]{:S(2)}) collective-permute-start(bf16[64,128]{1,0:T(8,128)(2,1)S(1)} %get-tuple-element.36), channel_id=1, source_target_pairs={{0,16},{8,24},{16,32},{24,40},{32,48},{40,56},{48,64},{56,72},{64,... | collective-permute-start | bytes 49160 | tf_op jit(solution)/shard_map/ppermute | solution.py:14
  63.9 2.3 %collective-permute-done.2 = bf16[64,128]{1,0:T(8,128)(2,1)S(1)} collective-permute-done((bf16[64,128]{1,0:T(8,128)(2,1)S(1)}, bf16[64,128]{1,0:T(8,128)(2,1)S(1)}, u32[]{:S(2)}, u32[]{:S(2)}) %collective-permute-start.2) | collective-permute-done | bytes 16416 | tf_op jit(solution)/shard_map/ppermute | solution.py:14
  66.2 4.8 %collective-permute-done.3 = bf16[64,128]{1,0:T(8,128)(2,1)S(1)} collective-permute-done((bf16[64,128]{1,0:T(8,128)(2,1)S(1)}, bf16[64,128]{1,0:T(8,128)(2,1)S(1)}, u32[]{:S(2)}, u32[]{:S(2)}) %collective-permute-start.3) | collective-permute-done | bytes 16416 | tf_op jit(solution)/shard_map/ppermute | solution.py:14
  74.5 3.1 %collective-permute-start.4 = (bf16[64,2,60]{0,1,2:T(2,128)(2,1)S(1)}, bf16[64,2,60]{0,1,2:T(2,128)(2,1)S(1)}, u32[]{:S(2)}, u32[]{:S(2)}) collective-permute-start(bf16[64,2,60]{0,1,2:T(2,128)(2,1)S(1)} %get-tuple-element.45), channel_id=1, source_target_pairs={{0,1},{1,2},{2,3},{3,4},{4,5},{5,6},{6,7},{7,8},{8,9},{9,10},{10,1... | collective-permute-start | bytes 46088 | tf_op jit(solution)/shard_map/ppermute | solution.py:34
  77.6 4.9 %collective-permute-start.5 = (bf16[64,2,60]{0,1,2:T(2,128)(2,1)S(1)}, bf16[64,2,60]{0,1,2:T(2,128)(2,1)S(1)}, u32[]{:S(2)}, u32[]{:S(2)}) collective-permute-start(bf16[64,2,60]{0,1,2:T(2,128)(2,1)S(1)} %get-tuple-element.46), channel_id=1, source_target_pairs={{1,0},{2,1},{3,2},{4,3},{5,4},{6,5},{7,6},{8,7},{9,8},{10,9},{11,1... | collective-permute-start | bytes 46088 | tf_op jit(solution)/shard_map/ppermute | solution.py:35
  84.2 1.4 gather_fusion.1
  86.0 2.0 %gather_fusion.2 = bf16[324,64,4]{1,2,0:T(4,128)(2,1)S(1)} fusion(bf16[64,4,324]{0,1,2:T(4,128)(2,1)S(1)} %pad_maximum_fusion.2, s32[1024]{0:T(1024)S(1)} %get-tuple-element.65), kind=kCustom, calls=%fused_computation.15 | custom fusion | bytes 333072 | tf_op jit(solution)/shard_map/jit(_take)/gather | solution.py:111
  94.0 1.1 fusion.18
  96.0 1.9 %collective-permute-start.6 = (bf16[128,2,60]{0,1,2:T(2,128)(2,1)S(1)}, bf16[128,2,60]{0,1,2:T(2,128)(2,1)S(1)}, u32[]{:S(2)}, u32[]{:S(2)}) collective-permute-start(bf16[128,2,60]{0,1,2:T(2,128)(2,1)S(1)} %get-tuple-element.43), channel_id=1, source_target_pairs={{0,1},{1,2},{2,3},{3,4},{4,5},{5,6},{6,7},{7,8},{8,9},{9,10},{10,1... | collective-permute-start | bytes 92168 | tf_op jit(solution)/shard_map/ppermute | solution.py:34
  98.0 6.6 %collective-permute-start.7 = (bf16[128,2,60]{0,1,2:T(2,128)(2,1)S(1)}, bf16[128,2,60]{0,1,2:T(2,128)(2,1)S(1)}, u32[]{:S(2)}, u32[]{:S(2)}) collective-permute-start(bf16[128,2,60]{0,1,2:T(2,128)(2,1)S(1)} %get-tuple-element.44), channel_id=1, source_target_pairs={{1,0},{2,1},{3,2},{4,3},{5,4},{6,5},{7,6},{8,7},{9,8},{10,9},{11,1... | collective-permute-start | bytes 92168 | tf_op jit(solution)/shard_map/ppermute | solution.py:35
  104.5 1.3 collective-permute-done.7
  106.0 1.4 gather_fusion.11
  108.0 2.0 %gather_fusion.12 = bf16[324,128,4]{1,2,0:T(4,128)(2,1)S(1)} fusion(bf16[128,4,324]{0,1,2:T(4,128)(2,1)S(1)} %copy.300, s32[1024]{0:T(1024)S(1)} %get-tuple-element.65), kind=kCustom, calls=%fused_computation.4.clone | custom fusion | bytes 664848 | tf_op jit(solution)/shard_map/jit(_take)/gather | solution.py:111
  114.2 1.1 fusion.21
  116.2 1.9 %collective-permute-start.8 = (bf16[128,2,60]{0,1,2:T(2,128)(2,1)S(1)}, bf16[128,2,60]{0,1,2:T(2,128)(2,1)S(1)}, u32[]{:S(2)}, u32[]{:S(2)}) collective-permute-start(bf16[128,2,60]{0,1,2:T(2,128)(2,1)S(1)} %get-tuple-element.41), channel_id=1, source_target_pairs={{0,1},{1,2},{2,3},{3,4},{4,5},{5,6},{6,7},{7,8},{8,9},{9,10},{10,1... | collective-permute-start | bytes 92168 | tf_op jit(solution)/shard_map/ppermute | solution.py:34
  118.1 6.3 %collective-permute-start.9 = (bf16[128,2,60]{0,1,2:T(2,128)(2,1)S(1)}, bf16[128,2,60]{0,1,2:T(2,128)(2,1)S(1)}, u32[]{:S(2)}, u32[]{:S(2)}) collective-permute-start(bf16[128,2,60]{0,1,2:T(2,128)(2,1)S(1)} %get-tuple-element.42), channel_id=1, source_target_pairs={{1,0},{2,1},{3,2},{4,3},{5,4},{6,5},{7,6},{8,7},{9,8},{10,9},{11,1... | collective-permute-start | bytes 92168 | tf_op jit(solution)/shard_map/ppermute | solution.py:35
  124.4 1.5 %collective-permute-done.9 = bf16[128,2,60]{0,1,2:T(2,128)(2,1)S(1)} collective-permute-done((bf16[128,2,60]{0,1,2:T(2,128)(2,1)S(1)}, bf16[128,2,60]{0,1,2:T(2,128)(2,1)S(1)}, u32[]{:S(2)}, u32[]{:S(2)}) %collective-permute-start.9) | collective-permute-done | bytes 30752 | tf_op jit(solution)/shard_map/ppermute | solution.py:35
  126.2 1.4 gather_fusion.14
  128.1 2.0 %gather_fusion.15 = bf16[324,128,4]{1,2,0:T(4,128)(2,1)S(1)} fusion(bf16[128,4,324]{0,1,2:T(4,128)(2,1)S(1)} %copy.314, s32[1024]{0:T(1024)S(1)} %get-tuple-element.65), kind=kCustom, calls=%fused_computation.12.clone | custom fusion | bytes 664848 | tf_op jit(solution)/shard_map/jit(_take)/gather | solution.py:111
  134.3 1.1 fusion.24
  135.6 17.4 %all_to_all.27 = bf16[128,4,256]{2,1,0:T(4,128)(2,1)S(1)} all-to-all(bf16[128,4,256]{2,1,0:T(4,128)(2,1)S(1)} %copy.325), channel_id=1, replica_groups=mesh['tile'=64,'chan'=8] {'chan'}, dimensions={0} | all-to-all | bytes 524288 | tf_op jit(solution)/shard_map/all_to_all | solution.py:202
  (178 shorter events, 38.2 us)
Async XLA Ops:
  0.0 31.1 %copy-start = (s32[32,8]{0,1:T(8,128)S(1)}, s32[32,8]{0,1:T(8,128)}, u32[]{:S(2)}) copy-start(s32[32,8]{0,1:T(8,128)} %param.38) | copy-start | bytes 3076
  20.1 11.0 %copy-start.4 = (s32[68]{0:T(128)S(1)}, s32[68]{0:T(128)}, u32[]{:S(2)}) copy-start(s32[68]{0:T(128)} %constant.306) | copy-start | bytes 820
  20.1 11.0 %copy-start.1 = (s32[32,8]{0,1:T(8,128)S(1)}, s32[32,8]{0,1:T(8,128)}, u32[]{:S(2)}) copy-start(s32[32,8]{0,1:T(8,128)} %param.37) | copy-start | bytes 3076
  20.1 12.5 %copy-start.3 = (s32[68]{0:T(128)S(1)}, s32[68]{0:T(128)}, u32[]{:S(2)}) copy-start(s32[68]{0:T(128)} %constant.239) | copy-start | bytes 820
  21.7 18.2 %all-to-all-start = ((bf16[8,2,25600]{2,1,0:T(2,128)(2,1)}), bf16[8,2,25600]{2,1,0:T(2,128)(2,1)S(1)}, u32[]{:S(2)}, u32[]{:S(2)}) async-start(bf16[8,2,25600]{2,1,0:T(2,128)(2,1)} %reshape.402), calls=%async_computation | async-start | bytes 1638400 | tf_op jit(solution)/shard_map/all_to_all | solution.py:24
  40.6 21.1 %copy-start.5 = (s32[60]{0:T(128)S(1)}, s32[60]{0:T(128)}, u32[]{:S(2)}) copy-start(s32[60]{0:T(128)} %constant.217.clone) | copy-start | bytes 724
  41.2 14.9 %collective-permute-start = (bf16[64,128]{1,0:T(8,128)(2,1)S(1)}, bf16[64,128]{1,0:T(8,128)(2,1)S(1)}, u32[]{:S(2)}, u32[]{:S(2)}) collective-permute-start(bf16[64,128]{1,0:T(8,128)(2,1)S(1)} %get-tuple-element.40), channel_id=1, source_target_pairs={{0,496},{8,504},{16,0},{24,8},{32,16},{40,24},{48,32},{56,40},{64,... | collective-permute-start | bytes 49160 | tf_op jit(solution)/shard_map/ppermute | solution.py:14
  53.7 3.8 %collective-permute-start.1 = (bf16[64,128]{1,0:T(8,128)(2,1)S(1)}, bf16[64,128]{1,0:T(8,128)(2,1)S(1)}, u32[]{:S(2)}, u32[]{:S(2)}) collective-permute-start(bf16[64,128]{1,0:T(8,128)(2,1)S(1)} %get-tuple-element.39), channel_id=1, source_target_pairs={{0,504},{8,0},{16,8},{24,16},{32,24},{40,32},{48,40},{56,48},{64,5... | collective-permute-start | bytes 49160 | tf_op jit(solution)/shard_map/ppermute | solution.py:14
  57.5 8.7 %collective-permute-start.2 = (bf16[64,128]{1,0:T(8,128)(2,1)S(1)}, bf16[64,128]{1,0:T(8,128)(2,1)S(1)}, u32[]{:S(2)}, u32[]{:S(2)}) collective-permute-start(bf16[64,128]{1,0:T(8,128)(2,1)S(1)} %get-tuple-element.37), channel_id=1, source_target_pairs={{0,8},{8,16},{16,24},{24,32},{32,40},{40,48},{48,56},{56,64},{64,7... | collective-permute-start | bytes 49160 | tf_op jit(solution)/shard_map/ppermute | solution.py:14
  61.8 9.2 %collective-permute-start.3 = (bf16[64,128]{1,0:T(8,128)(2,1)S(1)}, bf16[64,128]{1,0:T(8,128)(2,1)S(1)}, u32[]{:S(2)}, u32[]{:S(2)}) collective-permute-start(bf16[64,128]{1,0:T(8,128)(2,1)S(1)} %get-tuple-element.36), channel_id=1, source_target_pairs={{0,16},{8,24},{16,32},{24,40},{32,48},{40,56},{48,64},{56,72},{64,... | collective-permute-start | bytes 49160 | tf_op jit(solution)/shard_map/ppermute | solution.py:14
  71.6 10.8 %copy-start.2 = (s32[324]{0:T(512)S(1)}, s32[324]{0:T(512)}, u32[]{:S(2)}) copy-start(s32[324]{0:T(512)} %constant.220.clone) | copy-start | bytes 3892
  74.5 9.0 %collective-permute-start.4 = (bf16[64,2,60]{0,1,2:T(2,128)(2,1)S(1)}, bf16[64,2,60]{0,1,2:T(2,128)(2,1)S(1)}, u32[]{:S(2)}, u32[]{:S(2)}) collective-permute-start(bf16[64,2,60]{0,1,2:T(2,128)(2,1)S(1)} %get-tuple-element.45), channel_id=1, source_target_pairs={{0,1},{1,2},{2,3},{3,4},{4,5},{5,6},{6,7},{7,8},{8,9},{9,10},{10,1... | collective-permute-start | bytes 46088 | tf_op jit(solution)/shard_map/ppermute | solution.py:34
  77.6 6.5 %collective-permute-start.5 = (bf16[64,2,60]{0,1,2:T(2,128)(2,1)S(1)}, bf16[64,2,60]{0,1,2:T(2,128)(2,1)S(1)}, u32[]{:S(2)}, u32[]{:S(2)}) collective-permute-start(bf16[64,2,60]{0,1,2:T(2,128)(2,1)S(1)} %get-tuple-element.46), channel_id=1, source_target_pairs={{1,0},{2,1},{3,2},{4,3},{5,4},{6,5},{7,6},{8,7},{9,8},{10,9},{11,1... | collective-permute-start | bytes 46088 | tf_op jit(solution)/shard_map/ppermute | solution.py:35
  96.0 8.5 %collective-permute-start.6 = (bf16[128,2,60]{0,1,2:T(2,128)(2,1)S(1)}, bf16[128,2,60]{0,1,2:T(2,128)(2,1)S(1)}, u32[]{:S(2)}, u32[]{:S(2)}) collective-permute-start(bf16[128,2,60]{0,1,2:T(2,128)(2,1)S(1)} %get-tuple-element.43), channel_id=1, source_target_pairs={{0,1},{1,2},{2,3},{3,4},{4,5},{5,6},{6,7},{7,8},{8,9},{9,10},{10,1... | collective-permute-start | bytes 92168 | tf_op jit(solution)/shard_map/ppermute | solution.py:34
  98.0 7.9 %collective-permute-start.7 = (bf16[128,2,60]{0,1,2:T(2,128)(2,1)S(1)}, bf16[128,2,60]{0,1,2:T(2,128)(2,1)S(1)}, u32[]{:S(2)}, u32[]{:S(2)}) collective-permute-start(bf16[128,2,60]{0,1,2:T(2,128)(2,1)S(1)} %get-tuple-element.44), channel_id=1, source_target_pairs={{1,0},{2,1},{3,2},{4,3},{5,4},{6,5},{7,6},{8,7},{9,8},{10,9},{11,1... | collective-permute-start | bytes 92168 | tf_op jit(solution)/shard_map/ppermute | solution.py:35
  116.2 8.3 %collective-permute-start.8 = (bf16[128,2,60]{0,1,2:T(2,128)(2,1)S(1)}, bf16[128,2,60]{0,1,2:T(2,128)(2,1)S(1)}, u32[]{:S(2)}, u32[]{:S(2)}) collective-permute-start(bf16[128,2,60]{0,1,2:T(2,128)(2,1)S(1)} %get-tuple-element.41), channel_id=1, source_target_pairs={{0,1},{1,2},{2,3},{3,4},{4,5},{5,6},{6,7},{7,8},{8,9},{9,10},{10,1... | collective-permute-start | bytes 92168 | tf_op jit(solution)/shard_map/ppermute | solution.py:34
  118.1 7.9 %collective-permute-start.9 = (bf16[128,2,60]{0,1,2:T(2,128)(2,1)S(1)}, bf16[128,2,60]{0,1,2:T(2,128)(2,1)S(1)}, u32[]{:S(2)}, u32[]{:S(2)}) collective-permute-start(bf16[128,2,60]{0,1,2:T(2,128)(2,1)S(1)} %get-tuple-element.42), channel_id=1, source_target_pairs={{1,0},{2,1},{3,2},{4,3},{5,4},{6,5},{7,6},{8,7},{9,8},{10,9},{11,1... | collective-permute-start | bytes 92168 | tf_op jit(solution)/shard_map/ppermute | solution.py:35

commit v6 on v4

--- a/solution.py
+++ b/solution.py
@@ -96,19 +96,29 @@
     return np.array(entries, np.int32)
 
 
-def conv_layer(activity, kernel, local_beside, local_turns, gather_rims):
+def padded_index(tiles, local_beside, local_turns):
     length = 4 * P_SIZE - 4
-    cycle_vals = jnp.take(activity, cycle_table(P_SIZE), axis=2)
-    extended = gather_rims(cycle_vals)
+    interior = P_SIZE * P_SIZE
     heading, anchor = border_tables(P_SIZE)
     near_tile = jnp.take(local_beside, heading, axis=1)
     near_turn = jnp.take(local_turns, heading, axis=1)
     source = near_tile * length + jnp.remainder(anchor[None, :] - near_turn * (P_SIZE - 1), length)
-    flat_cycles = extended.reshape(extended.shape[0], -1)
-    border = jnp.take(flat_cycles, source.reshape(-1), axis=1)
-    border = border.reshape(activity.shape[0], activity.shape[1], 4 * P_SIZE + 4)
-    joined = jnp.concatenate([activity, border], axis=2)
-    padded = jnp.take(joined, layout_table(P_SIZE), axis=2)
+    layout = layout_table(P_SIZE)
+    tile_ids = jnp.arange(tiles)[:, None]
+    from_interior = tile_ids * interior + jnp.minimum(layout, interior - 1)[None, :]
+    border_at = np.maximum(layout - interior, 0)
+    from_border = tiles * interior + jnp.take(source, border_at, axis=1)
+    return jnp.where((layout < interior)[None, :], from_interior, from_border)
+
+
+def conv_layer(activity, kernel, where_from, gather_rims):
+    cycle_vals = jnp.take(activity, cycle_table(P_SIZE), axis=2)
+    extended = gather_rims(cycle_vals)
+    channels, tiles = activity.shape[0], activity.shape[1]
+    joined = jnp.concatenate(
+        [activity.reshape(channels, -1), extended.reshape(channels, -1)], axis=1
+    )
+    padded = jnp.take(joined, where_from.reshape(-1), axis=1).reshape(channels, tiles, -1)
     padded_side = P_SIZE + 2
     stretch = P_SIZE * padded_side - 2
     summed = None
@@ -155,11 +165,13 @@
         kernels.append(joined_kernels[:, :, low : low + width])
         low += width
     slot_order = jnp.arange(capacity)
+    rows_list = send_rows[0].reshape(-1)
+    piece = jnp.take(analysis, rows_list, axis=1)
+    is_live = (slot_order[None, :] < send_count[0][:, None]).reshape(-1)
+    piece = jnp.where(is_live[None, :], piece, jnp.zeros((), piece.dtype))
     blocks = []
     for offset_index in range(near_count):
-        block = jnp.take(analysis, send_rows[0, offset_index], axis=1)
-        is_live = slot_order < send_count[0, offset_index]
-        block = jnp.where(is_live[None, :], block, jnp.zeros((), block.dtype))
+        block = piece[:, offset_index * capacity : (offset_index + 1) * capacity]
         if offset_index != REACH:
             block = from_behind(block, "tile", offset_index - REACH)
         blocks.append(block)
@@ -186,8 +198,9 @@
     def joined_rims(cycle_vals):
         return extended_2(cycle_vals, ((("tile", "chan"), 1),), REACH)
 
+    where_from = padded_index(per_group, local_beside, near_turns)
     for kernel in kernels:
-        activity = conv_layer(activity, kernel, local_beside, near_turns, joined_rims)
+        activity = conv_layer(activity, kernel, where_from, joined_rims)
     result = lax.all_to_all(activity, "chan", split_axis=0, concat_axis=1, tiled=True)
     return result
 

time: 141 us -> 140 us (level)
  local copies, waits for them, and re-layouts: 36.3 us -> 34.5 us
  other arithmetic: 9.83 us -> 11.3 us
    convert_element_type x3 -> x5, other arithmetic: 3.26 us -> 6.5 us  [conv_layer(): return jax.nn.gelu(summed, approximate=False).astype(jnp.bfloat16)]
    lt x4 -> x1, other arithmetic: 2.46 us -> 0.81 us  [on_device(): is_live = (slot_order[None, :] < send_count[0][:, None]).reshape(-1)]
    slice x1 -> x2, local copies, waits for them, and re-layouts: 1.49 us -> 0.07 us  [on_device(): block = piece[:, offset_index * capacity:(offset_index + 1) * capacity]]
    gather x19 -> x9, local copies, waits for them, and re-layouts: 15.5 us -> 14.3 us  [the longest x5 10.1 us: conv_layer(): jnp.take(joined, where_from.reshape(-1), axis=1)]
    unnamed x47 -> x51, local copies, waits for them, and re-layouts: 8.7 us -> 8.69 us
  transfers between devices with their start and end apart: 12 -> 12, of which waited for: 3 -> 3; matrix products, arithmetic and copies ran while one was open for 15% -> 14% of each run, Pallas kernels for 0% -> 0%
where the time goes in v6:
time: 140 us; the launch traced here: 139 us
  starting transfers between devices  57.5 us (41%)
  local copies, waits for them, and re-layouts  34.5 us (25%)
  blocking collectives  17.1 us (12%)
  other arithmetic  11.3 us (8%)
  matrix products  11.3 us (8%)
  waiting for transfers between devices  6.49 us (5%)
    ppermute x4, starting transfers between devices, from_behind(): return lax.ppermute(value, axis, pairs)  22 us
    all_to_all x1, blocking collectives, on_device(): lax.all_to_all(activity, 'chan', split_axis=0, concat_axis=1, tiled=True)  17.1 us
    ppermute x3, starting transfers between devices, extended_2(): after = lax.ppermute(initial, axis, down)  16.5 us
    all_to_all x2, starting transfers between devices, gather_by_exchange(): lax.all_to_all(copies, axis, split_axis=dim, concat_axis=dim, tiled=True)  10.8 us
    gather x5, local copies, waits for them, and re-layouts, conv_layer(): jnp.take(joined, where_from.reshape(-1), axis=1)  10.1 us
    dot_general x27, matrix products, conv_layer(): jnp.einsum('oc,ctq->otq', kernel[tap_index], window, preferred_element_ty...  8.83 us
    unnamed x51, local copies, waits for them, and re-layouts  8.69 us
    ppermute x3, starting transfers between devices, extended_2(): before = lax.ppermute(last, axis, up)  8.33 us
  transfers between devices with their start and end apart: 12, of which 3 were waited for; matrix products, arithmetic and copies ran while one was open for 14% of the time, Pallas kernels for 0%

profile of v6, /device:TPU:2, one launch (start us, length us, event | category | flops | bytes accessed | tf_op | source)
XLA Modules:
  0.0 139.4 jit_solution(2295127965922315638)
XLA Ops:
  0.1 0.8 fusion.125
  2.3 1.8 %copy.301 = bf16[8,8192]{0,1:T(8,128)(2,1)S(1)} copy(bf16[8,8192]{1,0:T(8,128)(2,1)} %param.24) | data formatting | bytes 262144 | tf_op args[0]
  4.2 2.0 %gather_fusion.1 = bf16[640,8]{1,0:T(8,128)(2,1)S(1)} fusion(bf16[8,8192]{0,1:T(8,128)(2,1)S(1)} %copy.301, s32[1024]{0:T(1024)S(1)} %get-tuple-element.65), kind=kCustom, calls=%fused_computation.7 | custom fusion | bytes 23040 | tf_op jit(solution)/shard_map/jit(_take)/gather | solution.py:169
  6.4 4.0 %collective-permute-start.3 = (bf16[8,128]{0,1:T(8,128)(2,1)S(1)}, bf16[8,128]{0,1:T(8,128)(2,1)S(1)}, u32[]{:S(2)}, u32[]{:S(2)}) collective-permute-start(bf16[8,128]{0,1:T(8,128)(2,1)S(1)} %get-tuple-element.43), channel_id=1, source_target_pairs={{0,16},{8,24},{16,32},{24,40},{32,48},{40,56},{48,64},{56,72},{64,... | collective-permute-start | bytes 6152 | tf_op jit(solution)/shard_map/ppermute | solution.py:14
  10.5 1.9 %collective-permute-start.2 = (bf16[8,128]{0,1:T(8,128)(2,1)S(1)}, bf16[8,128]{0,1:T(8,128)(2,1)S(1)}, u32[]{:S(2)}, u32[]{:S(2)}) collective-permute-start(bf16[8,128]{0,1:T(8,128)(2,1)S(1)} %get-tuple-element.44), channel_id=1, source_target_pairs={{0,8},{8,16},{16,24},{24,32},{32,40},{40,48},{48,56},{56,64},{64,7... | collective-permute-start | bytes 6152 | tf_op jit(solution)/shard_map/ppermute | solution.py:14
  12.4 10.3 %collective-permute-start.1 = (bf16[8,128]{0,1:T(8,128)(2,1)S(1)}, bf16[8,128]{0,1:T(8,128)(2,1)S(1)}, u32[]{:S(2)}, u32[]{:S(2)}) collective-permute-start(bf16[8,128]{0,1:T(8,128)(2,1)S(1)} %get-tuple-element.46), channel_id=1, source_target_pairs={{0,504},{8,0},{16,8},{24,16},{32,24},{40,32},{48,40},{56,48},{64,5... | collective-permute-start | bytes 6152 | tf_op jit(solution)/shard_map/ppermute | solution.py:14
  22.7 5.7 %collective-permute-start = (bf16[8,128]{0,1:T(8,128)(2,1)S(1)}, bf16[8,128]{0,1:T(8,128)(2,1)S(1)}, u32[]{:S(2)}, u32[]{:S(2)}) collective-permute-start(bf16[8,128]{0,1:T(8,128)(2,1)S(1)} %get-tuple-element.47), channel_id=1, source_target_pairs={{0,496},{8,504},{16,0},{24,8},{32,16},{40,24},{48,32},{56,40},{64,... | collective-permute-start | bytes 6152 | tf_op jit(solution)/shard_map/ppermute | solution.py:14
  29.9 1.1 gather_fusion
  33.9 1.9 %reshape.397 = bf16[8,2,23040]{2,1,0:T(2,128)(2,1)} reshape(bf16[128,9,320]{2,1,0:T(8,128)(2,1)S(1)} %bitcast.323) | data formatting | bytes 1474560
  36.9 5.9 %all-to-all-start.1 = ((bf16[8,8,640]{2,1,0:T(8,128)(2,1)}), bf16[8,8,640]{2,1,0:T(8,128)(2,1)S(1)}, u32[]{:S(2)}, u32[]{:S(2)}) async-start(bf16[8,8,640]{2,1,0:T(8,128)(2,1)} %broadcast_in_dim.123), calls=%async_computation.1 | async-start | bytes 163840 | tf_op jit(solution)/shard_map/all_to_all | solution.py:24
  42.9 5.0 %all-to-all-done.1 = bf16[8,8,640]{2,1,0:T(8,128)(2,1)S(1)} async-done(((bf16[8,8,640]{2,1,0:T(8,128)(2,1)}), bf16[8,8,640]{2,1,0:T(8,128)(2,1)S(1)}, u32[]{:S(2)}, u32[]{:S(2)}) %all-to-all-start.1) | async-done | bytes 81952 | tf_op jit(solution)/shard_map/all_to_all | solution.py:24
  47.9 4.8 %all-to-all-start = ((bf16[8,2,23040]{2,1,0:T(2,128)(2,1)}), bf16[8,2,23040]{2,1,0:T(2,128)(2,1)S(1)}, u32[]{:S(2)}, u32[]{:S(2)}) async-start(bf16[8,2,23040]{2,1,0:T(2,128)(2,1)} %reshape.397), calls=%async_computation | async-start | bytes 1474560 | tf_op jit(solution)/shard_map/all_to_all | solution.py:24
  56.2 3.4 %collective-permute-start.4 = (bf16[64,2,60]{0,1,2:T(2,128)(2,1)S(1)}, bf16[64,2,60]{0,1,2:T(2,128)(2,1)S(1)}, u32[]{:S(2)}, u32[]{:S(2)}) collective-permute-start(bf16[64,2,60]{0,1,2:T(2,128)(2,1)S(1)} %get-tuple-element.60), channel_id=1, source_target_pairs={{0,1},{1,2},{2,3},{3,4},{4,5},{5,6},{6,7},{7,8},{8,9},{9,10},{10,1... | collective-permute-start | bytes 46088 | tf_op jit(solution)/shard_map/ppermute | solution.py:34
  59.6 4.8 %collective-permute-start.5 = (bf16[64,2,60]{0,1,2:T(2,128)(2,1)S(1)}, bf16[64,2,60]{0,1,2:T(2,128)(2,1)S(1)}, u32[]{:S(2)}, u32[]{:S(2)}) collective-permute-start(bf16[64,2,60]{0,1,2:T(2,128)(2,1)S(1)} %get-tuple-element.61), channel_id=1, source_target_pairs={{1,0},{2,1},{3,2},{4,3},{5,4},{6,5},{7,6},{8,7},{9,8},{10,9},{11,1... | collective-permute-start | bytes 46088 | tf_op jit(solution)/shard_map/ppermute | solution.py:35
  64.5 1.3 collective-permute-done.5
  66.5 3.3 %gather_fusion.3 = bf16[1296,64]{1,0:T(8,128)(2,1)S(1)} fusion(bf16[64,1504]{0,1:T(8,128)(2,1)S(1)} %copy.310, s32[2048]{0:T(1024)S(1)} %pad_clamp_fusion.1), kind=kCustom, calls=%fused_computation.9 | custom fusion | bytes 336960 | tf_op jit(solution)/shard_map/jit(_take)/gather | solution.py:121
  70.1 1.4 reshape.398
  78.2 1.0 copy.331
  79.4 2.1 %fusion.21 = bf16[128,4,256]{2,0,1:T(8,128)(2,1)S(1)} fusion(f32[128,4,256]{2,0,1:T(8,128)} %copy.331, f32[128,4,256]{2,0,1:T(8,128)S(1)} %copy.326), kind=kLoop, calls=%fused_computation.64 | loop fusion | flops 8126464 | bytes 1310720 | tf_op jit(solution)/shard_map/convert_element_type | solution.py:135
  82.5 3.0 %collective-permute-start.6 = (bf16[128,2,60]{0,1,2:T(2,128)(2,1)S(1)}, bf16[128,2,60]{0,1,2:T(2,128)(2,1)S(1)}, u32[]{:S(2)}, u32[]{:S(2)}) collective-permute-start(bf16[128,2,60]{0,1,2:T(2,128)(2,1)S(1)} %get-tuple-element.58), channel_id=1, source_target_pairs={{0,1},{1,2},{2,3},{3,4},{4,5},{5,6},{6,7},{7,8},{8,9},{9,10},{10,1... | collective-permute-start | bytes 92168 | tf_op jit(solution)/shard_map/ppermute | solution.py:34
  85.5 5.4 %collective-permute-start.7 = (bf16[128,2,60]{0,1,2:T(2,128)(2,1)S(1)}, bf16[128,2,60]{0,1,2:T(2,128)(2,1)S(1)}, u32[]{:S(2)}, u32[]{:S(2)}) collective-permute-start(bf16[128,2,60]{0,1,2:T(2,128)(2,1)S(1)} %get-tuple-element.59), channel_id=1, source_target_pairs={{1,0},{2,1},{3,2},{4,3},{5,4},{6,5},{7,6},{8,7},{9,8},{10,9},{11,1... | collective-permute-start | bytes 92168 | tf_op jit(solution)/shard_map/ppermute | solution.py:35
  91.0 1.1 fusion.18
  92.1 1.8 %fusion.127 = (bf16[1,128,128]{2,0,1:T(2,128)(2,1)S(1)}, bf16[1,128,128]{2,0,1:T(2,128)(2,1)S(1)}, bf16[1,128,128]{2,0,1:T(2,128)(2,1)S(1)}, bf16[1,128,128]{2,0...) fusion(bf16[9,128,320]{2,0,1:T(8,128)(2,1)S(1)} %bitcast.322), kind=kLoop, calls=%fused_computation.271 | loop fusion | bytes 1179648 | tf_op jit(solution)/shard_map/slice | solution.py:129
  94.1 3.3 %gather_fusion.7 = bf16[1296,128]{1,0:T(8,128)(2,1)S(1)} fusion(bf16[128,1504]{0,1:T(8,128)(2,1)S(1)} %pad_maximum_fusion, s32[2048]{0:T(1024)S(1)} %pad_clamp_fusion), kind=kCustom, calls=%fused_computation.2.clone | custom fusion | bytes 668736 | tf_op jit(solution)/shard_map/jit(_take)/gather | solution.py:121
  101.3 1.1 fusion.27
  103.3 1.9 %collective-permute-start.8 = (bf16[128,2,60]{0,1,2:T(2,128)(2,1)S(1)}, bf16[128,2,60]{0,1,2:T(2,128)(2,1)S(1)}, u32[]{:S(2)}, u32[]{:S(2)}) collective-permute-start(bf16[128,2,60]{0,1,2:T(2,128)(2,1)S(1)} %get-tuple-element.56), channel_id=1, source_target_pairs={{0,1},{1,2},{2,3},{3,4},{4,5},{5,6},{6,7},{7,8},{8,9},{9,10},{10,1... | collective-permute-start | bytes 92168 | tf_op jit(solution)/shard_map/ppermute | solution.py:34
  105.2 6.3 %collective-permute-start.9 = (bf16[128,2,60]{0,1,2:T(2,128)(2,1)S(1)}, bf16[128,2,60]{0,1,2:T(2,128)(2,1)S(1)}, u32[]{:S(2)}, u32[]{:S(2)}) collective-permute-start(bf16[128,2,60]{0,1,2:T(2,128)(2,1)S(1)} %get-tuple-element.57), channel_id=1, source_target_pairs={{1,0},{2,1},{3,2},{4,3},{5,4},{6,5},{7,6},{8,7},{9,8},{10,9},{11,1... | collective-permute-start | bytes 92168 | tf_op jit(solution)/shard_map/ppermute | solution.py:35
  111.5 1.1 fusion.24
  113.0 3.3 %gather_fusion.9 = bf16[1296,128]{1,0:T(8,128)(2,1)S(1)} fusion(bf16[128,1504]{0,1:T(8,128)(2,1)S(1)} %pad_maximum_fusion.1, s32[2048]{0:T(1024)S(1)} %pad_clamp_fusion), kind=kCustom, calls=%fused_computation.5.clone | custom fusion | bytes 668736 | tf_op jit(solution)/shard_map/jit(_take)/gather | solution.py:121
  120.1 1.1 fusion.30
  121.4 17.1 %all_to_all.32 = bf16[128,4,256]{2,1,0:T(4,128)(2,1)S(1)} all-to-all(bf16[128,4,256]{2,1,0:T(4,128)(2,1)S(1)} %copy.372), channel_id=1, replica_groups=mesh['tile'=64,'chan'=8] {'chan'}, dimensions={0} | all-to-all | bytes 524288 | tf_op jit(solution)/shard_map/all_to_all | solution.py:204
  138.6 0.8 copy.375
  (171 shorter events, 28.4 us)
Async XLA Ops:
  0.0 4.1 %copy-start.9 = (s32[60]{0:T(128)S(1)}, s32[60]{0:T(128)}, u32[]{:S(2)}) copy-start(s32[60]{0:T(128)} %constant.219.clone) | copy-start | bytes 724
  0.0 28.4 %copy-start.10 = (s32[68]{0:T(128)S(1)}, s32[68]{0:T(128)}, u32[]{:S(2)}) copy-start(s32[68]{0:T(128)} %constant.289) | copy-start | bytes 820
  0.0 28.4 %copy-start.6 = (s32[324]{0:T(512)S(1)}, s32[324]{0:T(512)}, u32[]{:S(2)}) copy-start(s32[324]{0:T(512)} %constant.283) | copy-start | bytes 3892
  0.0 29.8 %copy-start.8 = (s32[68]{0:T(128)S(1)}, s32[68]{0:T(128)}, u32[]{:S(2)}) copy-start(s32[68]{0:T(128)} %constant.240) | copy-start | bytes 820
  0.0 31.0 %copy-start.5 = (s32[324]{0:T(512)S(1)}, s32[324]{0:T(512)}, u32[]{:S(2)}) copy-start(s32[324]{0:T(512)} %constant.233) | copy-start | bytes 3892
  0.0 31.0 %copy-start.7 = (pred[324]{0:T(512)(128)(4,1)S(1)}, pred[324]{0:T(512)(128)(4,1)}, u32[]{:S(2)}) copy-start(pred[324]{0:T(512)(128)(4,1)} %constant.232) | copy-start | bytes 976
  0.0 28.4 %copy-start.4 = (s32[32,8]{0,1:T(8,128)S(1)}, s32[32,8]{0,1:T(8,128)}, u32[]{:S(2)}) copy-start(s32[32,8]{0,1:T(8,128)} %param.30) | copy-start | bytes 3076
  0.1 28.4 %copy-start.3 = (s32[32,8]{0,1:T(8,128)S(1)}, s32[32,8]{0,1:T(8,128)}, u32[]{:S(2)}) copy-start(s32[32,8]{0,1:T(8,128)} %param.29) | copy-start | bytes 3076
  0.1 31.4 %copy-start = (bf16[9,16,128]{2,1,0:T(8,128)(2,1)S(1)}, bf16[9,16,128]{2,1,0:T(8,128)(2,1)}, u32[]{:S(2)}) copy-start(bf16[9,16,128]{2,1,0:T(8,128)(2,1)} %param.33) | copy-start | bytes 110596
  0.1 31.4 %copy-start.1 = (bf16[9,16,128]{2,1,0:T(8,128)(2,1)S(1)}, bf16[9,16,128]{2,1,0:T(8,128)(2,1)}, u32[]{:S(2)}) copy-start(bf16[9,16,128]{2,1,0:T(8,128)(2,1)} %param.32) | copy-start | bytes 110596
  0.1 31.4 %copy-start.2 = (bf16[9,16,64]{2,1,0:T(8,128)(2,1)S(1)}, bf16[9,16,64]{2,1,0:T(8,128)(2,1)}, u32[]{:S(2)}) copy-start(bf16[9,16,64]{2,1,0:T(8,128)(2,1)} %param.31) | copy-start | bytes 55300
  6.4 29.7 %collective-permute-start.3 = (bf16[8,128]{0,1:T(8,128)(2,1)S(1)}, bf16[8,128]{0,1:T(8,128)(2,1)S(1)}, u32[]{:S(2)}, u32[]{:S(2)}) collective-permute-start(bf16[8,128]{0,1:T(8,128)(2,1)S(1)} %get-tuple-element.43), channel_id=1, source_target_pairs={{0,16},{8,24},{16,32},{24,40},{32,48},{40,56},{48,64},{56,72},{64,... | collective-permute-start | bytes 6152 | tf_op jit(solution)/shard_map/ppermute | solution.py:14
  10.5 25.6 %collective-permute-start.2 = (bf16[8,128]{0,1:T(8,128)(2,1)S(1)}, bf16[8,128]{0,1:T(8,128)(2,1)S(1)}, u32[]{:S(2)}, u32[]{:S(2)}) collective-permute-start(bf16[8,128]{0,1:T(8,128)(2,1)S(1)} %get-tuple-element.44), channel_id=1, source_target_pairs={{0,8},{8,16},{16,24},{24,32},{32,40},{40,48},{48,56},{56,64},{64,7... | collective-permute-start | bytes 6152 | tf_op jit(solution)/shard_map/ppermute | solution.py:14
  12.4 23.6 %collective-permute-start.1 = (bf16[8,128]{0,1:T(8,128)(2,1)S(1)}, bf16[8,128]{0,1:T(8,128)(2,1)S(1)}, u32[]{:S(2)}, u32[]{:S(2)}) collective-permute-start(bf16[8,128]{0,1:T(8,128)(2,1)S(1)} %get-tuple-element.46), channel_id=1, source_target_pairs={{0,504},{8,0},{16,8},{24,16},{32,24},{40,32},{48,40},{56,48},{64,5... | collective-permute-start | bytes 6152 | tf_op jit(solution)/shard_map/ppermute | solution.py:14
  22.7 13.2 %collective-permute-start = (bf16[8,128]{0,1:T(8,128)(2,1)S(1)}, bf16[8,128]{0,1:T(8,128)(2,1)S(1)}, u32[]{:S(2)}, u32[]{:S(2)}) collective-permute-start(bf16[8,128]{0,1:T(8,128)(2,1)S(1)} %get-tuple-element.47), channel_id=1, source_target_pairs={{0,496},{8,504},{16,0},{24,8},{32,16},{40,24},{48,32},{56,40},{64,... | collective-permute-start | bytes 6152 | tf_op jit(solution)/shard_map/ppermute | solution.py:14
  36.9 11.0 %all-to-all-start.1 = ((bf16[8,8,640]{2,1,0:T(8,128)(2,1)}), bf16[8,8,640]{2,1,0:T(8,128)(2,1)S(1)}, u32[]{:S(2)}, u32[]{:S(2)}) async-start(bf16[8,8,640]{2,1,0:T(8,128)(2,1)} %broadcast_in_dim.123), calls=%async_computation.1 | async-start | bytes 163840 | tf_op jit(solution)/shard_map/all_to_all | solution.py:24
  47.9 22.2 %all-to-all-start = ((bf16[8,2,23040]{2,1,0:T(2,128)(2,1)}), bf16[8,2,23040]{2,1,0:T(2,128)(2,1)S(1)}, u32[]{:S(2)}, u32[]{:S(2)}) async-start(bf16[8,2,23040]{2,1,0:T(2,128)(2,1)} %reshape.397), calls=%async_computation | async-start | bytes 1474560 | tf_op jit(solution)/shard_map/all_to_all | solution.py:24
  56.2 8.3 %collective-permute-start.4 = (bf16[64,2,60]{0,1,2:T(2,128)(2,1)S(1)}, bf16[64,2,60]{0,1,2:T(2,128)(2,1)S(1)}, u32[]{:S(2)}, u32[]{:S(2)}) collective-permute-start(bf16[64,2,60]{0,1,2:T(2,128)(2,1)S(1)} %get-tuple-element.60), channel_id=1, source_target_pairs={{0,1},{1,2},{2,3},{3,4},{4,5},{5,6},{6,7},{7,8},{8,9},{9,10},{10,1... | collective-permute-start | bytes 46088 | tf_op jit(solution)/shard_map/ppermute | solution.py:34
  59.6 6.1 %collective-permute-start.5 = (bf16[64,2,60]{0,1,2:T(2,128)(2,1)S(1)}, bf16[64,2,60]{0,1,2:T(2,128)(2,1)S(1)}, u32[]{:S(2)}, u32[]{:S(2)}) collective-permute-start(bf16[64,2,60]{0,1,2:T(2,128)(2,1)S(1)} %get-tuple-element.61), channel_id=1, source_target_pairs={{1,0},{2,1},{3,2},{4,3},{5,4},{6,5},{7,6},{8,7},{9,8},{10,9},{11,1... | collective-permute-start | bytes 46088 | tf_op jit(solution)/shard_map/ppermute | solution.py:35
  82.5 11.4 %collective-permute-start.6 = (bf16[128,2,60]{0,1,2:T(2,128)(2,1)S(1)}, bf16[128,2,60]{0,1,2:T(2,128)(2,1)S(1)}, u32[]{:S(2)}, u32[]{:S(2)}) collective-permute-start(bf16[128,2,60]{0,1,2:T(2,128)(2,1)S(1)} %get-tuple-element.58), channel_id=1, source_target_pairs={{0,1},{1,2},{2,3},{3,4},{4,5},{5,6},{6,7},{7,8},{8,9},{9,10},{10,1... | collective-permute-start | bytes 92168 | tf_op jit(solution)/shard_map/ppermute | solution.py:34
  85.5 8.4 %collective-permute-start.7 = (bf16[128,2,60]{0,1,2:T(2,128)(2,1)S(1)}, bf16[128,2,60]{0,1,2:T(2,128)(2,1)S(1)}, u32[]{:S(2)}, u32[]{:S(2)}) collective-permute-start(bf16[128,2,60]{0,1,2:T(2,128)(2,1)S(1)} %get-tuple-element.59), channel_id=1, source_target_pairs={{1,0},{2,1},{3,2},{4,3},{5,4},{6,5},{7,6},{8,7},{9,8},{10,9},{11,1... | collective-permute-start | bytes 92168 | tf_op jit(solution)/shard_map/ppermute | solution.py:35
  103.3 9.3 %collective-permute-start.8 = (bf16[128,2,60]{0,1,2:T(2,128)(2,1)S(1)}, bf16[128,2,60]{0,1,2:T(2,128)(2,1)S(1)}, u32[]{:S(2)}, u32[]{:S(2)}) collective-permute-start(bf16[128,2,60]{0,1,2:T(2,128)(2,1)S(1)} %get-tuple-element.56), channel_id=1, source_target_pairs={{0,1},{1,2},{2,3},{3,4},{4,5},{5,6},{6,7},{7,8},{8,9},{9,10},{10,1... | collective-permute-start | bytes 92168 | tf_op jit(solution)/shard_map/ppermute | solution.py:34
  105.2 7.6 %collective-permute-start.9 = (bf16[128,2,60]{0,1,2:T(2,128)(2,1)S(1)}, bf16[128,2,60]{0,1,2:T(2,128)(2,1)S(1)}, u32[]{:S(2)}, u32[]{:S(2)}) collective-permute-start(bf16[128,2,60]{0,1,2:T(2,128)(2,1)S(1)} %get-tuple-element.57), channel_id=1, source_target_pairs={{1,0},{2,1},{3,2},{4,3},{5,4},{6,5},{7,6},{8,7},{9,8},{10,9},{11,1... | collective-permute-start | bytes 92168 | tf_op jit(solution)/shard_map/ppermute | solution.py:35

commit v7 on v6

--- a/solution.py
+++ b/solution.py
@@ -118,20 +118,19 @@
     joined = jnp.concatenate(
         [activity.reshape(channels, -1), extended.reshape(channels, -1)], axis=1
     )
-    padded = jnp.take(joined, where_from.reshape(-1), axis=1).reshape(channels, tiles, -1)
     padded_side = P_SIZE + 2
-    stretch = P_SIZE * padded_side - 2
-    summed = None
-    for tap_index in range(9):
-        offset = padded_side + 1 + (tap_index // 3 - 1) * padded_side + (tap_index % 3 - 1)
-        window = padded[:, :, offset : offset + stretch]
-        partial_sum = jnp.einsum(
-            "oc,ctq->otq", kernel[tap_index], window, preferred_element_type=jnp.float32
-        )
-        summed = partial_sum if summed is None else summed + partial_sum
-    summed = jnp.pad(summed, ((0, 0), (0, 0), (0, 2)))
-    summed = summed.reshape(summed.shape[0], summed.shape[1], P_SIZE, padded_side)[:, :, :, :P_SIZE]
-    summed = summed.reshape(summed.shape[0], summed.shape[1], P_SIZE * P_SIZE)
+    padded = jnp.take(joined, where_from.reshape(-1), axis=1)
+    padded = padded.reshape(channels, tiles, padded_side, padded_side)
+    taps = kernel.reshape(3, 3, kernel.shape[1], kernel.shape[2])
+    summed = lax.conv_general_dilated(
+        padded,
+        taps,
+        window_strides=(1, 1),
+        padding="VALID",
+        dimension_numbers=("CNHW", "HWOI", "CNHW"),
+        preferred_element_type=jnp.float32,
+    )
+    summed = summed.reshape(summed.shape[0], tiles, P_SIZE * P_SIZE)
     return jax.nn.gelu(summed, approximate=False).astype(jnp.bfloat16)
 
 

time: 140 us -> 141 us (level)
  waiting for transfers between devices: 6.49 us -> 19.1 us
  starting transfers between devices: 57.5 us -> 51 us
  matrix products: 11.3 us -> 6.28 us
  other arithmetic: 11.3 us -> 8.63 us
  local copies, waits for them, and re-layouts: 34.5 us -> 36.2 us
    ppermute x3, waiting for transfers between devices: 0.01 us -> 14.1 us  [extended_2(): before = lax.ppermute(last, axis, up)]
    dot_general x27 -> x0, matrix products: 8.83 us -> none  [conv_layer(): jnp.einsum('oc,ctq->otq', kernel[tap_index], window, preferred_element_ty...]
    ppermute x3, starting transfers between devices: 16.5 us -> 8.42 us  [extended_2(): after = lax.ppermute(initial, axis, down)]
    mul x11 -> x24, local copies, waits for them, and re-layouts: 2.24 us -> 6.27 us  [conv_layer(): return jax.nn.gelu(summed, approximate=False).astype(jnp.bfloat16)]
    conv_general_dilated x0 -> x3, matrix products: none -> 3.83 us  [conv_layer(): lax.conv_general_dilated(padded, taps, window_strides=(1, 1), padding='VA...]
    ppermute x3, starting transfers between devices: 8.33 us -> 10.4 us  [extended_2(): before = lax.ppermute(last, axis, up)]
    unnamed x51 -> x52, local copies, waits for them, and re-layouts: 8.69 us -> 7.2 us
    ppermute x3, waiting for transfers between devices: 1.44 us -> 0.01 us  [extended_2(): after = lax.ppermute(initial, axis, down)]
  transfers between devices with their start and end apart: 12 -> 12, of which waited for: 3 -> 4; matrix products, arithmetic and copies ran while one was open for 14% -> 13% of each run, Pallas kernels for 0% -> 0%
where the time goes in v7:
time: 141 us; the launch traced here: 140 us
  starting transfers between devices  51 us (36%)
  local copies, waits for them, and re-layouts  36.2 us (26%)
  waiting for transfers between devices  19.1 us (14%)
  blocking collectives  17.9 us (13%)
  other arithmetic  8.63 us (6%)
  matrix products  6.28 us (4%)
    ppermute x4, starting transfers between devices, from_behind(): return lax.ppermute(value, axis, pairs)  21.4 us
    all_to_all x1, blocking collectives, on_device(): lax.all_to_all(activity, 'chan', split_axis=0, concat_axis=1, tiled=True)  17.9 us
    ppermute x3, waiting for transfers between devices, extended_2(): before = lax.ppermute(last, axis, up)  14.1 us
    all_to_all x2, starting transfers between devices, gather_by_exchange(): lax.all_to_all(copies, axis, split_axis=dim, concat_axis=dim, tiled=True)  10.8 us
    ppermute x3, starting transfers between devices, extended_2(): before = lax.ppermute(last, axis, up)  10.4 us
    gather x4, local copies, waits for them, and re-layouts, conv_layer(): padded = jnp.take(joined, where_from.reshape(-1), axis=1)  9.93 us
    ppermute x3, starting transfers between devices, extended_2(): after = lax.ppermute(initial, axis, down)  8.42 us
    unnamed x52, local copies, waits for them, and re-layouts  7.2 us
  transfers between devices with their start and end apart: 12, of which 4 were waited for; matrix products, arithmetic and copies ran while one was open for 13% of the time, Pallas kernels for 0%

profile of v7, /device:TPU:2, one launch (start us, length us, event | category | flops | bytes accessed | tf_op | source)
XLA Modules:
  0.0 140.3 jit_solution(16243598394617322990)
XLA Ops:
  0.1 1.9 %copy.232 = bf16[8,8192]{0,1:T(8,128)(2,1)S(1)} copy(bf16[8,8192]{1,0:T(8,128)(2,1)} %param.24) | data formatting | bytes 262144 | tf_op args[0]
  2.2 2.0 %gather_fusion.1 = bf16[640,8]{1,0:T(8,128)(2,1)S(1)} fusion(bf16[8,8192]{0,1:T(8,128)(2,1)S(1)} %copy.232, s32[1024]{0:T(1024)S(1)} %get-tuple-element.38), kind=kCustom, calls=%fused_computation.7 | custom fusion | bytes 23040 | tf_op jit(solution)/shard_map/jit(_take)/gather | solution.py:168
  4.5 13.0 %collective-permute-start = (bf16[8,128]{0,1:T(8,128)(2,1)S(1)}, bf16[8,128]{0,1:T(8,128)(2,1)S(1)}, u32[]{:S(2)}, u32[]{:S(2)}) collective-permute-start(bf16[8,128]{0,1:T(8,128)(2,1)S(1)} %get-tuple-element.20), channel_id=1, source_target_pairs={{0,496},{8,504},{16,0},{24,8},{32,16},{40,24},{48,32},{56,40},{64,... | collective-permute-start | bytes 6152 | tf_op jit(solution)/shard_map/ppermute | solution.py:14
  17.4 2.5 %collective-permute-start.1 = (bf16[8,128]{0,1:T(8,128)(2,1)S(1)}, bf16[8,128]{0,1:T(8,128)(2,1)S(1)}, u32[]{:S(2)}, u32[]{:S(2)}) collective-permute-start(bf16[8,128]{0,1:T(8,128)(2,1)S(1)} %get-tuple-element.19), channel_id=1, source_target_pairs={{0,504},{8,0},{16,8},{24,16},{32,24},{40,32},{48,40},{56,48},{64,5... | collective-permute-start | bytes 6152 | tf_op jit(solution)/shard_map/ppermute | solution.py:14
  19.9 1.9 %collective-permute-start.2 = (bf16[8,128]{0,1:T(8,128)(2,1)S(1)}, bf16[8,128]{0,1:T(8,128)(2,1)S(1)}, u32[]{:S(2)}, u32[]{:S(2)}) collective-permute-start(bf16[8,128]{0,1:T(8,128)(2,1)S(1)} %get-tuple-element.17), channel_id=1, source_target_pairs={{0,8},{8,16},{16,24},{24,32},{32,40},{40,48},{48,56},{56,64},{64,7... | collective-permute-start | bytes 6152 | tf_op jit(solution)/shard_map/ppermute | solution.py:14
  21.8 4.0 %collective-permute-start.3 = (bf16[8,128]{0,1:T(8,128)(2,1)S(1)}, bf16[8,128]{0,1:T(8,128)(2,1)S(1)}, u32[]{:S(2)}, u32[]{:S(2)}) collective-permute-start(bf16[8,128]{0,1:T(8,128)(2,1)S(1)} %get-tuple-element.16), channel_id=1, source_target_pairs={{0,16},{8,24},{16,32},{24,40},{32,48},{40,56},{48,64},{56,72},{64,... | collective-permute-start | bytes 6152 | tf_op jit(solution)/shard_map/ppermute | solution.py:14
  31.6 1.9 %reshape.430 = bf16[8,2,23040]{2,1,0:T(2,128)(2,1)} reshape(bf16[128,9,320]{2,1,0:T(8,128)(2,1)S(1)} %bitcast.259) | data formatting | bytes 1474560
  34.7 5.9 %all-to-all-start = ((bf16[8,8,640]{2,1,0:T(8,128)(2,1)}), bf16[8,8,640]{2,1,0:T(8,128)(2,1)S(1)}, u32[]{:S(2)}, u32[]{:S(2)}) async-start(bf16[8,8,640]{2,1,0:T(8,128)(2,1)} %broadcast_in_dim.133), calls=%async_computation | async-start | bytes 163840 | tf_op jit(solution)/shard_map/all_to_all | solution.py:24
  40.7 5.0 %all-to-all-done = bf16[8,8,640]{2,1,0:T(8,128)(2,1)S(1)} async-done(((bf16[8,8,640]{2,1,0:T(8,128)(2,1)}), bf16[8,8,640]{2,1,0:T(8,128)(2,1)S(1)}, u32[]{:S(2)}, u32[]{:S(2)}) %all-to-all-start) | async-done | bytes 81952 | tf_op jit(solution)/shard_map/all_to_all | solution.py:24
  45.7 4.8 %all-to-all-start.1 = ((bf16[8,2,23040]{2,1,0:T(2,128)(2,1)}), bf16[8,2,23040]{2,1,0:T(2,128)(2,1)S(1)}, u32[]{:S(2)}, u32[]{:S(2)}) async-start(bf16[8,2,23040]{2,1,0:T(2,128)(2,1)} %reshape.430), calls=%async_computation.1 | async-start | bytes 1474560 | tf_op jit(solution)/shard_map/all_to_all | solution.py:24
  54.0 4.6 %collective-permute-start.5 = (bf16[64,2,60]{0,1,2:T(2,128)(2,1)S(1)}, bf16[64,2,60]{0,1,2:T(2,128)(2,1)S(1)}, u32[]{:S(2)}, u32[]{:S(2)}) collective-permute-start(bf16[64,2,60]{0,1,2:T(2,128)(2,1)S(1)} %get-tuple-element.34), channel_id=1, source_target_pairs={{1,0},{2,1},{3,2},{4,3},{5,4},{6,5},{7,6},{8,7},{9,8},{10,9},{11,1... | collective-permute-start | bytes 46088 | tf_op jit(solution)/shard_map/ppermute | solution.py:35
  58.6 2.1 %collective-permute-start.4 = (bf16[64,2,60]{0,1,2:T(2,128)(2,1)S(1)}, bf16[64,2,60]{0,1,2:T(2,128)(2,1)S(1)}, u32[]{:S(2)}, u32[]{:S(2)}) collective-permute-start(bf16[64,2,60]{0,1,2:T(2,128)(2,1)S(1)} %get-tuple-element.33), channel_id=1, source_target_pairs={{0,1},{1,2},{2,3},{3,4},{4,5},{5,6},{6,7},{7,8},{8,9},{9,10},{10,1... | collective-permute-start | bytes 46088 | tf_op jit(solution)/shard_map/ppermute | solution.py:34
  60.7 5.8 %collective-permute-done.4 = bf16[64,2,60]{0,1,2:T(2,128)(2,1)S(1)} collective-permute-done((bf16[64,2,60]{0,1,2:T(2,128)(2,1)S(1)}, bf16[64,2,60]{0,1,2:T(2,128)(2,1)S(1)}, u32[]{:S(2)}, u32[]{:S(2)}) %collective-permute-start.4) | collective-permute-done | bytes 15392 | tf_op jit(solution)/shard_map/ppermute | solution.py:34
  67.2 3.3 %gather_fusion.3 = bf16[1296,64]{1,0:T(8,128)(2,1)S(1)} fusion(bf16[64,1504]{0,1:T(8,128)(2,1)S(1)} %copy.241, s32[2048]{0:T(1024)S(1)} %pad_clamp_fusion.1), kind=kCustom, calls=%fused_computation.9 | custom fusion | bytes 336960 | tf_op jit(solution)/shard_map/jit(_take)/gather | solution.py:122
  71.8 1.4 reshape.431
  73.6 1.6 %negate_multiply_fusion.2 = (f32[16,32,3,128]{3,1,2,0:T(8,128)}, f32[16,32,3,128]{3,1,2,0:T(8,128)S(1)}) fusion(bf16[3,3,128,64]{2,3,1,0:T(8,128)(2,1)S(1)} %bitcast.292, bf16[64,18,4,8,5]{0,2,4,3,1:T(4,128)(2,1)S(1)} %fusion.19, pred[32,3]{0,1:T(4,128)(4,1)S(1)} %copy-done.15), kind=kOutput, calls=%fused_computation.40 | convolution fusion | flops 227278848 | bytes 2089056 | tf_op jit(solution)/shard_map/conv_general_dilated | solution.py:125
  76.1 1.6 %copy.248 = f32[16,32,3,128]{3,0,2,1:T(8,128)S(1)} copy(f32[16,32,3,128]{3,1,2,0:T(8,128)} %get-tuple-element.14) | data formatting | bytes 1572864 | tf_op jit(solution)/shard_map/mul | solution.py:134
  77.9 1.1 fusion.30
  79.2 1.1 fusion.33
  81.2 1.9 %collective-permute-start.7 = (bf16[128,2,60]{0,1,2:T(2,128)(2,1)S(1)}, bf16[128,2,60]{0,1,2:T(2,128)(2,1)S(1)}, u32[]{:S(2)}, u32[]{:S(2)}) collective-permute-start(bf16[128,2,60]{0,1,2:T(2,128)(2,1)S(1)} %get-tuple-element.32), channel_id=1, source_target_pairs={{1,0},{2,1},{3,2},{4,3},{5,4},{6,5},{7,6},{8,7},{9,8},{10,9},{11,1... | collective-permute-start | bytes 92168 | tf_op jit(solution)/shard_map/ppermute | solution.py:35
  83.1 4.1 %collective-permute-start.6 = (bf16[128,2,60]{0,1,2:T(2,128)(2,1)S(1)}, bf16[128,2,60]{0,1,2:T(2,128)(2,1)S(1)}, u32[]{:S(2)}, u32[]{:S(2)}) collective-permute-start(bf16[128,2,60]{0,1,2:T(2,128)(2,1)S(1)} %get-tuple-element.31), channel_id=1, source_target_pairs={{0,1},{1,2},{2,3},{3,4},{4,5},{5,6},{6,7},{7,8},{8,9},{9,10},{10,1... | collective-permute-start | bytes 92168 | tf_op jit(solution)/shard_map/ppermute | solution.py:34
  87.8 3.2 %collective-permute-done.6 = bf16[128,2,60]{0,1,2:T(2,128)(2,1)S(1)} collective-permute-done((bf16[128,2,60]{0,1,2:T(2,128)(2,1)S(1)}, bf16[128,2,60]{0,1,2:T(2,128)(2,1)S(1)}, u32[]{:S(2)}, u32[]{:S(2)}) %collective-permute-start.6) | collective-permute-done | bytes 30752 | tf_op jit(solution)/shard_map/ppermute | solution.py:34
  91.2 3.3 %gather_fusion.7 = bf16[1296,128]{1,0:T(8,128)(2,1)S(1)} fusion(bf16[128,1504]{0,1:T(8,128)(2,1)S(1)} %pad_maximum_fusion, s32[2048]{0:T(1024)S(1)} %pad_clamp_fusion), kind=kCustom, calls=%fused_computation.2.clone | custom fusion | bytes 668736 | tf_op jit(solution)/shard_map/jit(_take)/gather | solution.py:122
  95.6 1.1 negate_multiply_fusion.1
  98.4 1.1 fusion.39
  100.4 1.9 %collective-permute-start.9 = (bf16[128,2,60]{0,1,2:T(2,128)(2,1)S(1)}, bf16[128,2,60]{0,1,2:T(2,128)(2,1)S(1)}, u32[]{:S(2)}, u32[]{:S(2)}) collective-permute-start(bf16[128,2,60]{0,1,2:T(2,128)(2,1)S(1)} %get-tuple-element.30), channel_id=1, source_target_pairs={{1,0},{2,1},{3,2},{4,3},{5,4},{6,5},{7,6},{8,7},{9,8},{10,9},{11,1... | collective-permute-start | bytes 92168 | tf_op jit(solution)/shard_map/ppermute | solution.py:35
  102.4 4.2 %collective-permute-start.8 = (bf16[128,2,60]{0,1,2:T(2,128)(2,1)S(1)}, bf16[128,2,60]{0,1,2:T(2,128)(2,1)S(1)}, u32[]{:S(2)}, u32[]{:S(2)}) collective-permute-start(bf16[128,2,60]{0,1,2:T(2,128)(2,1)S(1)} %get-tuple-element.29), channel_id=1, source_target_pairs={{0,1},{1,2},{2,3},{3,4},{4,5},{5,6},{6,7},{7,8},{8,9},{9,10},{10,1... | collective-permute-start | bytes 92168 | tf_op jit(solution)/shard_map/ppermute | solution.py:34
  106.5 1.1 fusion.36
  107.7 5.1 %collective-permute-done.8 = bf16[128,2,60]{0,1,2:T(2,128)(2,1)S(1)} collective-permute-done((bf16[128,2,60]{0,1,2:T(2,128)(2,1)S(1)}, bf16[128,2,60]{0,1,2:T(2,128)(2,1)S(1)}, u32[]{:S(2)}, u32[]{:S(2)}) %collective-permute-start.8) | collective-permute-done | bytes 30752 | tf_op jit(solution)/shard_map/ppermute | solution.py:34
  113.0 3.3 %gather_fusion.9 = bf16[1296,128]{1,0:T(8,128)(2,1)S(1)} fusion(bf16[128,1504]{0,1:T(8,128)(2,1)S(1)} %pad_maximum_fusion.1, s32[2048]{0:T(1024)S(1)} %pad_clamp_fusion), kind=kCustom, calls=%fused_computation.5.clone | custom fusion | bytes 668736 | tf_op jit(solution)/shard_map/jit(_take)/gather | solution.py:122
  117.4 1.1 negate_multiply_fusion
  121.5 17.9 %all_to_all.32 = bf16[128,4,256]{2,1,0:T(4,128)(2,1)S(1)} all-to-all(bf16[128,4,256]{2,1,0:T(4,128)(2,1)S(1)} %copy.290), channel_id=1, replica_groups=mesh['tile'=64,'chan'=8] {'chan'}, dimensions={0} | all-to-all | bytes 524288 | tf_op jit(solution)/shard_map/all_to_all | solution.py:203
  (169 shorter events, 24.5 us)
Async XLA Ops:
  0.0 2.2 %copy-start.12 = (s32[60]{0:T(128)S(1)}, s32[60]{0:T(128)}, u32[]{:S(2)}) copy-start(s32[60]{0:T(128)} %constant.218.clone) | copy-start | bytes 724
  0.0 25.9 %copy-start.9 = (s32[324]{0:T(512)S(1)}, s32[324]{0:T(512)}, u32[]{:S(2)}) copy-start(s32[324]{0:T(512)} %constant.295) | copy-start | bytes 3892
  0.0 25.9 %copy-start.13 = (s32[68]{0:T(128)S(1)}, s32[68]{0:T(128)}, u32[]{:S(2)}) copy-start(s32[68]{0:T(128)} %constant.301) | copy-start | bytes 820
  0.0 27.2 %copy-start.11 = (s32[68]{0:T(128)S(1)}, s32[68]{0:T(128)}, u32[]{:S(2)}) copy-start(s32[68]{0:T(128)} %constant.250) | copy-start | bytes 820
  0.0 28.5 %copy-start.8 = (s32[324]{0:T(512)S(1)}, s32[324]{0:T(512)}, u32[]{:S(2)}) copy-start(s32[324]{0:T(512)} %constant.241) | copy-start | bytes 3892
  0.0 28.5 %copy-start.10 = (pred[324]{0:T(512)(128)(4,1)S(1)}, pred[324]{0:T(512)(128)(4,1)}, u32[]{:S(2)}) copy-start(pred[324]{0:T(512)(128)(4,1)} %constant.259) | copy-start | bytes 976
  0.0 1.9 %copy-start.4 = (s32[1,5,128]{2,0,1:T(1,128)S(1)}, s32[1,5,128]{2,0,1:T(1,128)}, u32[]{:S(2)}) copy-start(s32[1,5,128]{2,0,1:T(1,128)} %param.25) | copy-start | bytes 7684
  0.1 2.0 %copy-start.14 = (s32[1,5]{1,0:T(1,128)S(1)}, s32[1,5]{1,0:T(1,128)}, u32[]{:S(2)}) copy-start(s32[1,5]{1,0:T(1,128)} %param.26) | copy-start | bytes 64
  0.1 25.9 %copy-start.5 = (s32[32,8]{0,1:T(8,128)S(1)}, s32[32,8]{0,1:T(8,128)}, u32[]{:S(2)}) copy-start(s32[32,8]{0,1:T(8,128)} %param.29) | copy-start | bytes 3076
  0.1 25.9 %copy-start.6 = (s32[32,8]{0,1:T(8,128)S(1)}, s32[32,8]{0,1:T(8,128)}, u32[]{:S(2)}) copy-start(s32[32,8]{0,1:T(8,128)} %param.30) | copy-start | bytes 3076
  2.0 27.2 %copy-start = (bf16[9,16,128]{2,1,0:T(8,128)(2,1)S(1)}, bf16[9,16,128]{2,1,0:T(8,128)(2,1)}, u32[]{:S(2)}) copy-start(bf16[9,16,128]{2,1,0:T(8,128)(2,1)} %param.33) | copy-start | bytes 110596
  2.0 27.2 %copy-start.1 = (bf16[9,16,128]{2,1,0:T(8,128)(2,1)S(1)}, bf16[9,16,128]{2,1,0:T(8,128)(2,1)}, u32[]{:S(2)}) copy-start(bf16[9,16,128]{2,1,0:T(8,128)(2,1)} %param.32) | copy-start | bytes 110596
  2.0 27.2 %copy-start.2 = (bf16[9,16,64]{2,1,0:T(8,128)(2,1)S(1)}, bf16[9,16,64]{2,1,0:T(8,128)(2,1)}, u32[]{:S(2)}) copy-start(bf16[9,16,64]{2,1,0:T(8,128)(2,1)} %param.31) | copy-start | bytes 55300
  2.0 27.3 %copy-start.3 = (s32[18,18]{1,0:T(8,128)S(1)}, s32[18,18]{1,0:T(8,128)}, u32[]{:S(2)}) copy-start(s32[18,18]{1,0:T(8,128)} %constant.242) | copy-start | bytes 3892
  2.0 27.3 %copy-start.7 = (pred[18,18]{1,0:T(8,128)(4,1)S(1)}, pred[18,18]{1,0:T(8,128)(4,1)}, u32[]{:S(2)}) copy-start(pred[18,18]{1,0:T(8,128)(4,1)} %constant.240) | copy-start | bytes 976
  4.5 29.2 %collective-permute-start = (bf16[8,128]{0,1:T(8,128)(2,1)S(1)}, bf16[8,128]{0,1:T(8,128)(2,1)S(1)}, u32[]{:S(2)}, u32[]{:S(2)}) collective-permute-start(bf16[8,128]{0,1:T(8,128)(2,1)S(1)} %get-tuple-element.20), channel_id=1, source_target_pairs={{0,496},{8,504},{16,0},{24,8},{32,16},{40,24},{48,32},{56,40},{64,... | collective-permute-start | bytes 6152 | tf_op jit(solution)/shard_map/ppermute | solution.py:14
  17.4 16.3 %collective-permute-start.1 = (bf16[8,128]{0,1:T(8,128)(2,1)S(1)}, bf16[8,128]{0,1:T(8,128)(2,1)S(1)}, u32[]{:S(2)}, u32[]{:S(2)}) collective-permute-start(bf16[8,128]{0,1:T(8,128)(2,1)S(1)} %get-tuple-element.19), channel_id=1, source_target_pairs={{0,504},{8,0},{16,8},{24,16},{32,24},{40,32},{48,40},{56,48},{64,5... | collective-permute-start | bytes 6152 | tf_op jit(solution)/shard_map/ppermute | solution.py:14
  19.9 13.9 %collective-permute-start.2 = (bf16[8,128]{0,1:T(8,128)(2,1)S(1)}, bf16[8,128]{0,1:T(8,128)(2,1)S(1)}, u32[]{:S(2)}, u32[]{:S(2)}) collective-permute-start(bf16[8,128]{0,1:T(8,128)(2,1)S(1)} %get-tuple-element.17), channel_id=1, source_target_pairs={{0,8},{8,16},{16,24},{24,32},{32,40},{40,48},{48,56},{56,64},{64,7... | collective-permute-start | bytes 6152 | tf_op jit(solution)/shard_map/ppermute | solution.py:14
  21.8 12.1 %collective-permute-start.3 = (bf16[8,128]{0,1:T(8,128)(2,1)S(1)}, bf16[8,128]{0,1:T(8,128)(2,1)S(1)}, u32[]{:S(2)}, u32[]{:S(2)}) collective-permute-start(bf16[8,128]{0,1:T(8,128)(2,1)S(1)} %get-tuple-element.16), channel_id=1, source_target_pairs={{0,16},{8,24},{16,32},{24,40},{32,48},{40,56},{48,64},{56,72},{64,... | collective-permute-start | bytes 6152 | tf_op jit(solution)/shard_map/ppermute | solution.py:14
  34.7 11.0 %all-to-all-start = ((bf16[8,8,640]{2,1,0:T(8,128)(2,1)}), bf16[8,8,640]{2,1,0:T(8,128)(2,1)S(1)}, u32[]{:S(2)}, u32[]{:S(2)}) async-start(bf16[8,8,640]{2,1,0:T(8,128)(2,1)} %broadcast_in_dim.133), calls=%async_computation | async-start | bytes 163840 | tf_op jit(solution)/shard_map/all_to_all | solution.py:24
  45.7 26.1 %all-to-all-start.1 = ((bf16[8,2,23040]{2,1,0:T(2,128)(2,1)}), bf16[8,2,23040]{2,1,0:T(2,128)(2,1)S(1)}, u32[]{:S(2)}, u32[]{:S(2)}) async-start(bf16[8,2,23040]{2,1,0:T(2,128)(2,1)} %reshape.430), calls=%async_computation.1 | async-start | bytes 1474560 | tf_op jit(solution)/shard_map/all_to_all | solution.py:24
  54.0 6.7 %collective-permute-start.5 = (bf16[64,2,60]{0,1,2:T(2,128)(2,1)S(1)}, bf16[64,2,60]{0,1,2:T(2,128)(2,1)S(1)}, u32[]{:S(2)}, u32[]{:S(2)}) collective-permute-start(bf16[64,2,60]{0,1,2:T(2,128)(2,1)S(1)} %get-tuple-element.34), channel_id=1, source_target_pairs={{1,0},{2,1},{3,2},{4,3},{5,4},{6,5},{7,6},{8,7},{9,8},{10,9},{11,1... | collective-permute-start | bytes 46088 | tf_op jit(solution)/shard_map/ppermute | solution.py:35
  58.6 7.9 %collective-permute-start.4 = (bf16[64,2,60]{0,1,2:T(2,128)(2,1)S(1)}, bf16[64,2,60]{0,1,2:T(2,128)(2,1)S(1)}, u32[]{:S(2)}, u32[]{:S(2)}) collective-permute-start(bf16[64,2,60]{0,1,2:T(2,128)(2,1)S(1)} %get-tuple-element.33), channel_id=1, source_target_pairs={{0,1},{1,2},{2,3},{3,4},{4,5},{5,6},{6,7},{7,8},{8,9},{9,10},{10,1... | collective-permute-start | bytes 46088 | tf_op jit(solution)/shard_map/ppermute | solution.py:34
  71.7 1.8 %copy-start.15 = (pred[32,3]{0,1:T(4,128)(4,1)S(1)}, pred[32,3]{0,1:T(4,128)(4,1)}, u32[]{:S(2)}) copy-start(pred[32,3]{0,1:T(4,128)(4,1)} %constant.237) | copy-start | bytes 292
  81.2 6.7 %collective-permute-start.7 = (bf16[128,2,60]{0,1,2:T(2,128)(2,1)S(1)}, bf16[128,2,60]{0,1,2:T(2,128)(2,1)S(1)}, u32[]{:S(2)}, u32[]{:S(2)}) collective-permute-start(bf16[128,2,60]{0,1,2:T(2,128)(2,1)S(1)} %get-tuple-element.32), channel_id=1, source_target_pairs={{1,0},{2,1},{3,2},{4,3},{5,4},{6,5},{7,6},{8,7},{9,8},{10,9},{11,1... | collective-permute-start | bytes 92168 | tf_op jit(solution)/shard_map/ppermute | solution.py:35
  83.1 7.9 %collective-permute-start.6 = (bf16[128,2,60]{0,1,2:T(2,128)(2,1)S(1)}, bf16[128,2,60]{0,1,2:T(2,128)(2,1)S(1)}, u32[]{:S(2)}, u32[]{:S(2)}) collective-permute-start(bf16[128,2,60]{0,1,2:T(2,128)(2,1)S(1)} %get-tuple-element.31), channel_id=1, source_target_pairs={{0,1},{1,2},{2,3},{3,4},{4,5},{5,6},{6,7},{7,8},{8,9},{9,10},{10,1... | collective-permute-start | bytes 92168 | tf_op jit(solution)/shard_map/ppermute | solution.py:34
  100.4 7.2 %collective-permute-start.9 = (bf16[128,2,60]{0,1,2:T(2,128)(2,1)S(1)}, bf16[128,2,60]{0,1,2:T(2,128)(2,1)S(1)}, u32[]{:S(2)}, u32[]{:S(2)}) collective-permute-start(bf16[128,2,60]{0,1,2:T(2,128)(2,1)S(1)} %get-tuple-element.30), channel_id=1, source_target_pairs={{1,0},{2,1},{3,2},{4,3},{5,4},{6,5},{7,6},{8,7},{9,8},{10,9},{11,1... | collective-permute-start | bytes 92168 | tf_op jit(solution)/shard_map/ppermute | solution.py:35
  102.4 10.4 %collective-permute-start.8 = (bf16[128,2,60]{0,1,2:T(2,128)(2,1)S(1)}, bf16[128,2,60]{0,1,2:T(2,128)(2,1)S(1)}, u32[]{:S(2)}, u32[]{:S(2)}) collective-permute-start(bf16[128,2,60]{0,1,2:T(2,128)(2,1)S(1)} %get-tuple-element.29), channel_id=1, source_target_pairs={{0,1},{1,2},{2,3},{3,4},{4,5},{5,6},{6,7},{7,8},{8,9},{9,10},{10,1... | collective-permute-start | bytes 92168 | tf_op jit(solution)/shard_map/ppermute | solution.py:34

commit v8 on v7

--- a/solution.py
+++ b/solution.py
@@ -96,31 +96,32 @@
     return np.array(entries, np.int32)
 
 
-def padded_index(tiles, local_beside, local_turns):
+def border_source(local_beside, local_turns):
     length = 4 * P_SIZE - 4
-    interior = P_SIZE * P_SIZE
     heading, anchor = border_tables(P_SIZE)
     near_tile = jnp.take(local_beside, heading, axis=1)
     near_turn = jnp.take(local_turns, heading, axis=1)
-    source = near_tile * length + jnp.remainder(anchor[None, :] - near_turn * (P_SIZE - 1), length)
-    layout = layout_table(P_SIZE)
-    tile_ids = jnp.arange(tiles)[:, None]
-    from_interior = tile_ids * interior + jnp.minimum(layout, interior - 1)[None, :]
-    border_at = np.maximum(layout - interior, 0)
-    from_border = tiles * interior + jnp.take(source, border_at, axis=1)
-    return jnp.where((layout < interior)[None, :], from_interior, from_border)
-
-
-def conv_layer(activity, kernel, where_from, gather_rims):
-    cycle_vals = jnp.take(activity, cycle_table(P_SIZE), axis=2)
+    return near_tile * length + jnp.remainder(anchor[None, :] - near_turn * (P_SIZE - 1), length)
+
+
+def rim_line(kernel, values, tap_ids):
+    total = None
+    for shift, tap in enumerate(tap_ids):
+        part = jnp.einsum(
+            "oc,ctq->otq",
+            kernel[tap],
+            values[:, :, shift : shift + P_SIZE],
+            preferred_element_type=jnp.float32,
+        )
+        total = part if total is None else total + part
+    return total
+
+
+def conv_layer(activity, cycle_vals, kernel, source, gather_rims):
     extended = gather_rims(cycle_vals)
     channels, tiles = activity.shape[0], activity.shape[1]
-    joined = jnp.concatenate(
-        [activity.reshape(channels, -1), extended.reshape(channels, -1)], axis=1
-    )
-    padded_side = P_SIZE + 2
-    padded = jnp.take(joined, where_from.reshape(-1), axis=1)
-    padded = padded.reshape(channels, tiles, padded_side, padded_side)
+    square = activity.reshape(channels, tiles, P_SIZE, P_SIZE)
+    padded = jnp.pad(square, ((0, 0), (0, 0), (1, 1), (1, 1)))
     taps = kernel.reshape(3, 3, kernel.shape[1], kernel.shape[2])
     summed = lax.conv_general_dilated(
         padded,
@@ -130,8 +131,24 @@
         dimension_numbers=("CNHW", "HWOI", "CNHW"),
         preferred_element_type=jnp.float32,
     )
-    summed = summed.reshape(summed.shape[0], tiles, P_SIZE * P_SIZE)
-    return jax.nn.gelu(summed, approximate=False).astype(jnp.bfloat16)
+    border = jnp.take(extended.reshape(channels, -1), source.reshape(-1), axis=1)
+    border = border.reshape(channels, tiles, 4 * P_SIZE + 4)
+    side = P_SIZE
+    rims = [border[:, :, k * side : (k + 1) * side] for k in range(4)]
+    corners = [border[:, :, 4 * side + k : 4 * side + k + 1] for k in range(4)]
+    blank = jnp.zeros((channels, tiles, 1), border.dtype)
+    top_row = jnp.concatenate([corners[0], rims[0], corners[1]], axis=2)
+    bottom_row = jnp.concatenate([corners[2], rims[1], corners[3]], axis=2)
+    left_col = jnp.concatenate([blank, rims[2], blank], axis=2)
+    right_col = jnp.concatenate([blank, rims[3], blank], axis=2)
+    summed = summed.at[:, :, 0, :].add(rim_line(kernel, top_row, (0, 1, 2)))
+    summed = summed.at[:, :, side - 1, :].add(rim_line(kernel, bottom_row, (6, 7, 8)))
+    summed = summed.at[:, :, :, 0].add(rim_line(kernel, left_col, (0, 3, 6)))
+    summed = summed.at[:, :, :, side - 1].add(rim_line(kernel, right_col, (2, 5, 8)))
+    summed = summed.reshape(summed.shape[0], tiles, side * side)
+    ring = jnp.take(summed, cycle_table(P_SIZE), axis=2)
+    next_cycles = jax.nn.gelu(ring, approximate=False).astype(jnp.bfloat16)
+    return jax.nn.gelu(summed, approximate=False).astype(jnp.bfloat16), next_cycles
 
 
 def on_device(
@@ -197,9 +214,10 @@
     def joined_rims(cycle_vals):
         return extended_2(cycle_vals, ((("tile", "chan"), 1),), REACH)
 
-    where_from = padded_index(per_group, local_beside, near_turns)
+    source = border_source(local_beside, near_turns)
+    cycle_vals = jnp.take(activity, cycle_table(P_SIZE), axis=2)
     for kernel in kernels:
-        activity = conv_layer(activity, kernel, where_from, joined_rims)
+        activity, cycle_vals = conv_layer(activity, cycle_vals, kernel, source, joined_rims)
     result = lax.all_to_all(activity, "chan", split_axis=0, concat_axis=1, tiled=True)
     return result
 

time: 141 us -> 137 us (0.972)
  waiting for transfers between devices: 19.1 us -> 5.53 us
  matrix products: 6.28 us -> 13.2 us
  starting transfers between devices: 51 us -> 56.7 us
  local copies, waits for them, and re-layouts: 36.2 us -> 32.2 us
    ppermute x3, waiting for transfers between devices: 14.1 us -> 0.01 us  [extended_2(): before = lax.ppermute(last, axis, up)]
    ppermute x3, starting transfers between devices: 8.42 us -> 16.2 us  [extended_2(): after = lax.ppermute(initial, axis, down)]
    unnamed x0 -> x36, matrix products: none -> 7.81 us
    gather x10 -> x11, local copies, waits for them, and re-layouts: 14.2 us -> 7.69 us  [the longest x4 4.14 us: conv_layer(): jnp.take(extended.reshape(channels, -1), source.reshape(-1), axis=1)]
    mul x24 -> x2, local copies, waits for them, and re-layouts: 6.27 us -> 0.62 us  [conv_layer(): jax.nn.gelu(summed, approximate=False).astype(jnp.bfloat16)]
    slice x0 -> x14, local copies, waits for them, and re-layouts: none -> 4.25 us  [the longest x2 2.9 us: rim_line(): kernel[tap]]
    ppermute x3, starting transfers between devices: 10.4 us -> 8.33 us  [extended_2(): before = lax.ppermute(last, axis, up)]
    unnamed x52 -> x112, local copies, waits for them, and re-layouts: 7.2 us -> 8.9 us
  transfers between devices with their start and end apart: 12 -> 12, of which waited for: 4 -> 2; matrix products, arithmetic and copies ran while one was open for 13% -> 14% of each run, Pallas kernels for 0% -> 0%
where the time goes in v8:
time: 137 us; the launch traced here: 136 us
  starting transfers between devices  56.7 us (41%)
  local copies, waits for them, and re-layouts  32.2 us (24%)
  blocking collectives  17.2 us (13%)
  matrix products  13.2 us (10%)
  other arithmetic  9.33 us (7%)
  waiting for transfers between devices  5.53 us (4%)
  between operations  1.62 us (1%)
    ppermute x4, starting transfers between devices, from_behind(): return lax.ppermute(value, axis, pairs)  21.4 us
    all_to_all x1, blocking collectives, on_device(): lax.all_to_all(activity, 'chan', split_axis=0, concat_axis=1, tiled=True)  17.2 us
    ppermute x3, starting transfers between devices, extended_2(): after = lax.ppermute(initial, axis, down)  16.2 us
    all_to_all x2, starting transfers between devices, gather_by_exchange(): lax.all_to_all(copies, axis, split_axis=dim, concat_axis=dim, tiled=True)  10.8 us
    unnamed x112, local copies, waits for them, and re-layouts  8.9 us
    ppermute x3, starting transfers between devices, extended_2(): before = lax.ppermute(last, axis, up)  8.33 us
    unnamed x36, matrix products  7.81 us
    all_to_all x2, waiting for transfers between devices, gather_by_exchange(): lax.all_to_all(copies, axis, split_axis=dim, concat_axis=dim, tiled=True)  4.44 us
  transfers between devices with their start and end apart: 12, of which 2 were waited for; matrix products, arithmetic and copies ran while one was open for 14% of the time, Pallas kernels for 0%

profile of v8, /device:TPU:2, one launch (start us, length us, event | category | flops | bytes accessed | tf_op | source)
XLA Modules:
  0.0 135.7 jit_solution(15249998849516454676)
XLA Ops:
  0.1 1.9 %copy.322 = bf16[8,8192]{0,1:T(8,128)(2,1)S(1)} copy(bf16[8,8192]{1,0:T(8,128)(2,1)} %param.45) | data formatting | bytes 262144 | tf_op args[0]
  2.1 2.0 %gather_fusion = bf16[640,8]{1,0:T(8,128)(2,1)S(1)} fusion(bf16[8,8192]{0,1:T(8,128)(2,1)S(1)} %copy.322, s32[1024]{0:T(1024)S(1)} %pad_clamp_fusion.4), kind=kCustom, calls=%fused_computation.6 | custom fusion | bytes 23040 | tf_op jit(solution)/shard_map/jit(_take)/gather | solution.py:185
  4.4 13.0 %collective-permute-start = (bf16[8,128]{0,1:T(8,128)(2,1)S(1)}, bf16[8,128]{0,1:T(8,128)(2,1)S(1)}, u32[]{:S(2)}, u32[]{:S(2)}) collective-permute-start(bf16[8,128]{0,1:T(8,128)(2,1)S(1)} %get-tuple-element.186), channel_id=1, source_target_pairs={{0,496},{8,504},{16,0},{24,8},{32,16},{40,24},{48,32},{56,40},{64,... | collective-permute-start | bytes 6152 | tf_op jit(solution)/shard_map/ppermute | solution.py:14
  17.4 2.5 %collective-permute-start.1 = (bf16[8,128]{0,1:T(8,128)(2,1)S(1)}, bf16[8,128]{0,1:T(8,128)(2,1)S(1)}, u32[]{:S(2)}, u32[]{:S(2)}) collective-permute-start(bf16[8,128]{0,1:T(8,128)(2,1)S(1)} %get-tuple-element.185), channel_id=1, source_target_pairs={{0,504},{8,0},{16,8},{24,16},{32,24},{40,32},{48,40},{56,48},{64,5... | collective-permute-start | bytes 6152 | tf_op jit(solution)/shard_map/ppermute | solution.py:14
  19.9 1.9 %collective-permute-start.2 = (bf16[8,128]{0,1:T(8,128)(2,1)S(1)}, bf16[8,128]{0,1:T(8,128)(2,1)S(1)}, u32[]{:S(2)}, u32[]{:S(2)}) collective-permute-start(bf16[8,128]{0,1:T(8,128)(2,1)S(1)} %get-tuple-element.183), channel_id=1, source_target_pairs={{0,8},{8,16},{16,24},{24,32},{32,40},{40,48},{48,56},{56,64},{64,7... | collective-permute-start | bytes 6152 | tf_op jit(solution)/shard_map/ppermute | solution.py:14
  21.8 4.0 %collective-permute-start.3 = (bf16[8,128]{0,1:T(8,128)(2,1)S(1)}, bf16[8,128]{0,1:T(8,128)(2,1)S(1)}, u32[]{:S(2)}, u32[]{:S(2)}) collective-permute-start(bf16[8,128]{0,1:T(8,128)(2,1)S(1)} %get-tuple-element.182), channel_id=1, source_target_pairs={{0,16},{8,24},{16,32},{24,40},{32,48},{40,56},{48,64},{56,72},{64,... | collective-permute-start | bytes 6152 | tf_op jit(solution)/shard_map/ppermute | solution.py:14
  30.7 1.9 %reshape.825 = bf16[8,2,23040]{2,1,0:T(2,128)(2,1)} reshape(bf16[128,9,320]{2,1,0:T(8,128)(2,1)S(1)} %bitcast.455) | data formatting | bytes 1474560
  33.6 5.9 %all-to-all-start = ((bf16[8,8,640]{2,1,0:T(8,128)(2,1)}), bf16[8,8,640]{2,1,0:T(8,128)(2,1)S(1)}, u32[]{:S(2)}, u32[]{:S(2)}) async-start(bf16[8,8,640]{2,1,0:T(8,128)(2,1)} %broadcast_in_dim.93), calls=%async_computation | async-start | bytes 163840 | tf_op jit(solution)/shard_map/all_to_all | solution.py:24
  40.1 4.4 %all-to-all-done = bf16[8,8,640]{2,1,0:T(8,128)(2,1)S(1)} async-done(((bf16[8,8,640]{2,1,0:T(8,128)(2,1)}), bf16[8,8,640]{2,1,0:T(8,128)(2,1)S(1)}, u32[]{:S(2)}, u32[]{:S(2)}) %all-to-all-start) | async-done | bytes 81952 | tf_op jit(solution)/shard_map/all_to_all | solution.py:24
  44.5 4.8 %all-to-all-start.1 = ((bf16[8,2,23040]{2,1,0:T(2,128)(2,1)}), bf16[8,2,23040]{2,1,0:T(2,128)(2,1)S(1)}, u32[]{:S(2)}, u32[]{:S(2)}) async-start(bf16[8,2,23040]{2,1,0:T(2,128)(2,1)} %reshape.825), calls=%async_computation.1 | async-start | bytes 1474560 | tf_op jit(solution)/shard_map/all_to_all | solution.py:24
  53.0 3.4 %collective-permute-start.4 = (bf16[64,2,60]{0,1,2:T(2,128)(2,1)S(1)}, bf16[64,2,60]{0,1,2:T(2,128)(2,1)S(1)}, u32[]{:S(2)}, u32[]{:S(2)}) collective-permute-start(bf16[64,2,60]{0,1,2:T(2,128)(2,1)S(1)} %get-tuple-element.223), channel_id=1, source_target_pairs={{0,1},{1,2},{2,3},{3,4},{4,5},{5,6},{6,7},{7,8},{8,9},{9,10},{10,1... | collective-permute-start | bytes 46088 | tf_op jit(solution)/shard_map/ppermute | solution.py:34
  56.4 4.8 %collective-permute-start.5 = (bf16[64,2,60]{0,1,2:T(2,128)(2,1)S(1)}, bf16[64,2,60]{0,1,2:T(2,128)(2,1)S(1)}, u32[]{:S(2)}, u32[]{:S(2)}) collective-permute-start(bf16[64,2,60]{0,1,2:T(2,128)(2,1)S(1)} %get-tuple-element.224), channel_id=1, source_target_pairs={{1,0},{2,1},{3,2},{4,3},{5,4},{6,5},{7,6},{8,7},{9,8},{10,9},{11,1... | collective-permute-start | bytes 46088 | tf_op jit(solution)/shard_map/ppermute | solution.py:35
  61.5 1.1 collective-permute-done.5
  62.7 1.4 %gather_fusion.2 = bf16[272,64]{1,0:T(8,128)(2,1)S(1)} fusion(bf16[64,480]{0,1:T(8,128)(2,1)S(1)} %reshape.820, s32[1024]{0:T(1024)S(1)} %pad_clamp_fusion.1), kind=kCustom, calls=%fused_computation.8 | custom fusion | bytes 70720 | tf_op jit(solution)/shard_map/jit(_take)/gather | solution.py:134
  66.9 1.3 reshape.826
  70.4 2.5 %fusion.160 = (bf16[1,128,128]{2,0,1:T(2,128)(2,1)}, bf16[1,128,128]{2,0,1:T(2,128)(2,1)}, bf16[1,128,128]{2,0,1:T(2,128)(2,1)}, bf16[1,128,128]{2,0,1:T(2,128)(...) fusion(bf16[9,128,320]{2,0,1:T(8,128)(2,1)S(1)} %bitcast.453), kind=kLoop, calls=%fused_computation.327 | loop fusion | bytes 1048576 | tf_op jit(solution)/shard_map/slice | solution.py:112
  75.5 0.8 fusion.112
  76.3 0.8 fusion.114
  77.1 0.8 fusion.120
  78.0 0.8 fusion.130
  79.7 1.1 fusion.66
  82.9 3.0 %collective-permute-start.6 = (bf16[128,2,60]{0,1,2:T(2,128)(2,1)S(1)}, bf16[128,2,60]{0,1,2:T(2,128)(2,1)S(1)}, u32[]{:S(2)}, u32[]{:S(2)}) collective-permute-start(bf16[128,2,60]{0,1,2:T(2,128)(2,1)S(1)} %get-tuple-element.221), channel_id=1, source_target_pairs={{0,1},{1,2},{2,3},{3,4},{4,5},{5,6},{6,7},{7,8},{8,9},{9,10},{10,1... | collective-permute-start | bytes 92168 | tf_op jit(solution)/shard_map/ppermute | solution.py:34
  86.0 5.4 %collective-permute-start.7 = (bf16[128,2,60]{0,1,2:T(2,128)(2,1)S(1)}, bf16[128,2,60]{0,1,2:T(2,128)(2,1)S(1)}, u32[]{:S(2)}, u32[]{:S(2)}) collective-permute-start(bf16[128,2,60]{0,1,2:T(2,128)(2,1)S(1)} %get-tuple-element.222), channel_id=1, source_target_pairs={{1,0},{2,1},{3,2},{4,3},{5,4},{6,5},{7,6},{8,7},{9,8},{10,9},{11,1... | collective-permute-start | bytes 92168 | tf_op jit(solution)/shard_map/ppermute | solution.py:35
  92.1 1.1 convolution_select_fusion.2
  94.3 1.4 %gather_fusion.6 = bf16[272,128]{1,0:T(8,128)(2,1)S(1)} fusion(bf16[128,480]{0,1:T(8,128)(2,1)S(1)} %reshape.608, s32[1024]{0:T(1024)S(1)} %copy-done.30), kind=kCustom, calls=%fused_computation.2.clone | custom fusion | bytes 140352 | tf_op jit(solution)/shard_map/jit(_take)/gather | solution.py:134
  98.7 1.1 fusion.65
  101.5 1.9 %collective-permute-start.8 = (bf16[128,2,60]{0,1,2:T(2,128)(2,1)S(1)}, bf16[128,2,60]{0,1,2:T(2,128)(2,1)S(1)}, u32[]{:S(2)}, u32[]{:S(2)}) collective-permute-start(bf16[128,2,60]{0,1,2:T(2,128)(2,1)S(1)} %get-tuple-element.219), channel_id=1, source_target_pairs={{0,1},{1,2},{2,3},{3,4},{4,5},{5,6},{6,7},{7,8},{8,9},{9,10},{10,1... | collective-permute-start | bytes 92168 | tf_op jit(solution)/shard_map/ppermute | solution.py:34
  103.5 6.0 %collective-permute-start.9 = (bf16[128,2,60]{0,1,2:T(2,128)(2,1)S(1)}, bf16[128,2,60]{0,1,2:T(2,128)(2,1)S(1)}, u32[]{:S(2)}, u32[]{:S(2)}) collective-permute-start(bf16[128,2,60]{0,1,2:T(2,128)(2,1)S(1)} %get-tuple-element.220), channel_id=1, source_target_pairs={{1,0},{2,1},{3,2},{4,3},{5,4},{6,5},{7,6},{8,7},{9,8},{10,9},{11,1... | collective-permute-start | bytes 92168 | tf_op jit(solution)/shard_map/ppermute | solution.py:35
  109.7 1.1 convolution_select_fusion.1
  111.6 1.4 %gather_fusion.8 = bf16[272,128]{1,0:T(8,128)(2,1)S(1)} fusion(bf16[128,480]{0,1:T(8,128)(2,1)S(1)} %reshape.617, s32[1024]{0:T(1024)S(1)} %copy-done.30), kind=kCustom, calls=%fused_computation.5.clone | custom fusion | bytes 140352 | tf_op jit(solution)/shard_map/jit(_take)/gather | solution.py:134
  116.4 1.1 fusion.36
  117.7 17.2 %all_to_all.32 = bf16[128,4,256]{2,1,0:T(4,128)(2,1)S(1)} all-to-all(bf16[128,4,256]{2,1,0:T(4,128)(2,1)S(1)} %copy.408), channel_id=1, replica_groups=mesh['tile'=64,'chan'=8] {'chan'}, dimensions={0} | all-to-all | bytes 524288 | tf_op jit(solution)/shard_map/all_to_all | solution.py:221
  (293 shorter events, 32.1 us)
Async XLA Ops:
  0.0 25.8 %copy-start.37 = (s32[60]{0:T(128)S(1)}, s32[60]{0:T(128)}, u32[]{:S(2)}) copy-start(s32[60]{0:T(128)} %constant.487.clone) | copy-start | bytes 724
  0.0 25.8 %copy-start.38 = (s32[68]{0:T(128)S(1)}, s32[68]{0:T(128)}, u32[]{:S(2)}) copy-start(s32[68]{0:T(128)} %constant.579) | copy-start | bytes 820
  0.0 27.3 %copy-start.36 = (s32[68]{0:T(128)S(1)}, s32[68]{0:T(128)}, u32[]{:S(2)}) copy-start(s32[68]{0:T(128)} %constant.533) | copy-start | bytes 820
  0.0 25.8 %copy-start.34 = (s32[32,8]{0,1:T(8,128)S(1)}, s32[32,8]{0,1:T(8,128)}, u32[]{:S(2)}) copy-start(s32[32,8]{0,1:T(8,128)} %param.50) | copy-start | bytes 3076
  0.0 25.8 %copy-start.35 = (s32[32,8]{0,1:T(8,128)S(1)}, s32[32,8]{0,1:T(8,128)}, u32[]{:S(2)}) copy-start(s32[32,8]{0,1:T(8,128)} %param.51) | copy-start | bytes 3076
  0.0 29.6 %copy-start.29 = (bf16[9,16,64]{2,1,0:T(8,128)(2,1)S(1)}, bf16[9,16,64]{2,1,0:T(8,128)(2,1)}, u32[]{:S(2)}) copy-start(bf16[9,16,64]{2,1,0:T(8,128)(2,1)} %param.52) | copy-start | bytes 55300
  0.1 29.6 %copy-start.28 = (bf16[9,16,128]{2,1,0:T(8,128)(2,1)S(1)}, bf16[9,16,128]{2,1,0:T(8,128)(2,1)}, u32[]{:S(2)}) copy-start(bf16[9,16,128]{2,1,0:T(8,128)(2,1)} %param.53) | copy-start | bytes 110596
  0.1 29.6 %copy-start.27 = (bf16[9,16,128]{2,1,0:T(8,128)(2,1)S(1)}, bf16[9,16,128]{2,1,0:T(8,128)(2,1)}, u32[]{:S(2)}) copy-start(bf16[9,16,128]{2,1,0:T(8,128)(2,1)} %param.54) | copy-start | bytes 110596
  4.4 28.1 %collective-permute-start = (bf16[8,128]{0,1:T(8,128)(2,1)S(1)}, bf16[8,128]{0,1:T(8,128)(2,1)S(1)}, u32[]{:S(2)}, u32[]{:S(2)}) collective-permute-start(bf16[8,128]{0,1:T(8,128)(2,1)S(1)} %get-tuple-element.186), channel_id=1, source_target_pairs={{0,496},{8,504},{16,0},{24,8},{32,16},{40,24},{48,32},{56,40},{64,... | collective-permute-start | bytes 6152 | tf_op jit(solution)/shard_map/ppermute | solution.py:14
  17.4 15.2 %collective-permute-start.1 = (bf16[8,128]{0,1:T(8,128)(2,1)S(1)}, bf16[8,128]{0,1:T(8,128)(2,1)S(1)}, u32[]{:S(2)}, u32[]{:S(2)}) collective-permute-start(bf16[8,128]{0,1:T(8,128)(2,1)S(1)} %get-tuple-element.185), channel_id=1, source_target_pairs={{0,504},{8,0},{16,8},{24,16},{32,24},{40,32},{48,40},{56,48},{64,5... | collective-permute-start | bytes 6152 | tf_op jit(solution)/shard_map/ppermute | solution.py:14
  19.9 12.9 %collective-permute-start.2 = (bf16[8,128]{0,1:T(8,128)(2,1)S(1)}, bf16[8,128]{0,1:T(8,128)(2,1)S(1)}, u32[]{:S(2)}, u32[]{:S(2)}) collective-permute-start(bf16[8,128]{0,1:T(8,128)(2,1)S(1)} %get-tuple-element.183), channel_id=1, source_target_pairs={{0,8},{8,16},{16,24},{24,32},{32,40},{40,48},{48,56},{56,64},{64,7... | collective-permute-start | bytes 6152 | tf_op jit(solution)/shard_map/ppermute | solution.py:14
  21.8 11.0 %collective-permute-start.3 = (bf16[8,128]{0,1:T(8,128)(2,1)S(1)}, bf16[8,128]{0,1:T(8,128)(2,1)S(1)}, u32[]{:S(2)}, u32[]{:S(2)}) collective-permute-start(bf16[8,128]{0,1:T(8,128)(2,1)S(1)} %get-tuple-element.182), channel_id=1, source_target_pairs={{0,16},{8,24},{16,32},{24,40},{32,48},{40,56},{48,64},{56,72},{64,... | collective-permute-start | bytes 6152 | tf_op jit(solution)/shard_map/ppermute | solution.py:14
  25.9 26.4 %copy-start.32 = (s32[1024]{0:T(1024)}, s32[1024]{0:T(1024)S(1)}, u32[]{:S(2)}) copy-start(s32[1024]{0:T(1024)S(1)} %get-tuple-element.251) | copy-start | bytes 12292
  33.6 11.0 %all-to-all-start = ((bf16[8,8,640]{2,1,0:T(8,128)(2,1)}), bf16[8,8,640]{2,1,0:T(8,128)(2,1)S(1)}, u32[]{:S(2)}, u32[]{:S(2)}) async-start(bf16[8,8,640]{2,1,0:T(8,128)(2,1)} %broadcast_in_dim.93), calls=%async_computation | async-start | bytes 163840 | tf_op jit(solution)/shard_map/all_to_all | solution.py:24
  44.5 22.3 %all-to-all-start.1 = ((bf16[8,2,23040]{2,1,0:T(2,128)(2,1)}), bf16[8,2,23040]{2,1,0:T(2,128)(2,1)S(1)}, u32[]{:S(2)}, u32[]{:S(2)}) async-start(bf16[8,2,23040]{2,1,0:T(2,128)(2,1)} %reshape.825), calls=%async_computation.1 | async-start | bytes 1474560 | tf_op jit(solution)/shard_map/all_to_all | solution.py:24
  53.0 8.5 %collective-permute-start.4 = (bf16[64,2,60]{0,1,2:T(2,128)(2,1)S(1)}, bf16[64,2,60]{0,1,2:T(2,128)(2,1)S(1)}, u32[]{:S(2)}, u32[]{:S(2)}) collective-permute-start(bf16[64,2,60]{0,1,2:T(2,128)(2,1)S(1)} %get-tuple-element.223), channel_id=1, source_target_pairs={{0,1},{1,2},{2,3},{3,4},{4,5},{5,6},{6,7},{7,8},{8,9},{9,10},{10,1... | collective-permute-start | bytes 46088 | tf_op jit(solution)/shard_map/ppermute | solution.py:34
  56.4 6.1 %collective-permute-start.5 = (bf16[64,2,60]{0,1,2:T(2,128)(2,1)S(1)}, bf16[64,2,60]{0,1,2:T(2,128)(2,1)S(1)}, u32[]{:S(2)}, u32[]{:S(2)}) collective-permute-start(bf16[64,2,60]{0,1,2:T(2,128)(2,1)S(1)} %get-tuple-element.224), channel_id=1, source_target_pairs={{1,0},{2,1},{3,2},{4,3},{5,4},{6,5},{7,6},{8,7},{9,8},{10,9},{11,1... | collective-permute-start | bytes 46088 | tf_op jit(solution)/shard_map/ppermute | solution.py:35
  70.3 3.8 %copy-start.21 = (bf16[64,4,16]{0,2,1:T(8,128)(2,1)S(1)}, bf16[64,4,16]{0,2,1:T(8,128)(2,1)}, u32[]{:S(2)}) copy-start(bf16[64,4,16]{0,2,1:T(8,128)(2,1)} %get-tuple-element.244) | copy-start | bytes 24580
  70.3 3.9 %copy-start.26 = (bf16[64,4,16]{0,2,1:T(8,128)(2,1)S(1)}, bf16[64,4,16]{0,2,1:T(8,128)(2,1)}, u32[]{:S(2)}) copy-start(bf16[64,4,16]{0,2,1:T(8,128)(2,1)} %get-tuple-element.245) | copy-start | bytes 24580
  70.3 4.2 %copy-start.20 = (bf16[64,4,16]{0,2,1:T(8,128)(2,1)S(1)}, bf16[64,4,16]{0,2,1:T(8,128)(2,1)}, u32[]{:S(2)}) copy-start(bf16[64,4,16]{0,2,1:T(8,128)(2,1)} %get-tuple-element.242) | copy-start | bytes 24580
  70.3 4.3 %copy-start.25 = (bf16[64,4,16]{0,2,1:T(8,128)(2,1)S(1)}, bf16[64,4,16]{0,2,1:T(8,128)(2,1)}, u32[]{:S(2)}) copy-start(bf16[64,4,16]{0,2,1:T(8,128)(2,1)} %get-tuple-element.246) | copy-start | bytes 24580
  70.3 4.4 %copy-start.19 = (bf16[64,4,16]{0,2,1:T(8,128)(2,1)S(1)}, bf16[64,4,16]{0,2,1:T(8,128)(2,1)}, u32[]{:S(2)}) copy-start(bf16[64,4,16]{0,2,1:T(8,128)(2,1)} %get-tuple-element.243) | copy-start | bytes 24580
  70.3 4.5 %copy-start.24 = (bf16[64,4,16]{0,2,1:T(8,128)(2,1)S(1)}, bf16[64,4,16]{0,2,1:T(8,128)(2,1)}, u32[]{:S(2)}) copy-start(bf16[64,4,16]{0,2,1:T(8,128)(2,1)} %get-tuple-element.247) | copy-start | bytes 24580
  70.3 4.7 %copy-start.18 = (bf16[64,4,16]{0,2,1:T(8,128)(2,1)S(1)}, bf16[64,4,16]{0,2,1:T(8,128)(2,1)}, u32[]{:S(2)}) copy-start(bf16[64,4,16]{0,2,1:T(8,128)(2,1)} %get-tuple-element.241) | copy-start | bytes 24580
  70.3 4.9 %copy-start.23 = (bf16[64,4,16]{0,2,1:T(8,128)(2,1)S(1)}, bf16[64,4,16]{0,2,1:T(8,128)(2,1)}, u32[]{:S(2)}) copy-start(bf16[64,4,16]{0,2,1:T(8,128)(2,1)} %get-tuple-element.248) | copy-start | bytes 24580
  82.9 11.1 %collective-permute-start.6 = (bf16[128,2,60]{0,1,2:T(2,128)(2,1)S(1)}, bf16[128,2,60]{0,1,2:T(2,128)(2,1)S(1)}, u32[]{:S(2)}, u32[]{:S(2)}) collective-permute-start(bf16[128,2,60]{0,1,2:T(2,128)(2,1)S(1)} %get-tuple-element.221), channel_id=1, source_target_pairs={{0,1},{1,2},{2,3},{3,4},{4,5},{5,6},{6,7},{7,8},{8,9},{9,10},{10,1... | collective-permute-start | bytes 92168 | tf_op jit(solution)/shard_map/ppermute | solution.py:34
  86.0 8.0 %collective-permute-start.7 = (bf16[128,2,60]{0,1,2:T(2,128)(2,1)S(1)}, bf16[128,2,60]{0,1,2:T(2,128)(2,1)S(1)}, u32[]{:S(2)}, u32[]{:S(2)}) collective-permute-start(bf16[128,2,60]{0,1,2:T(2,128)(2,1)S(1)} %get-tuple-element.222), channel_id=1, source_target_pairs={{1,0},{2,1},{3,2},{4,3},{5,4},{6,5},{7,6},{8,7},{9,8},{10,9},{11,1... | collective-permute-start | bytes 92168 | tf_op jit(solution)/shard_map/ppermute | solution.py:35
  94.1 3.9 %copy-start.11 = (bf16[1,128,128]{2,0,1:T(2,128)(2,1)S(1)}, bf16[1,128,128]{2,0,1:T(2,128)(2,1)}, u32[]{:S(2)}) copy-start(bf16[1,128,128]{2,0,1:T(2,128)(2,1)} %get-tuple-element.161) | copy-start | bytes 98308
  94.3 3.8 %copy-start.10 = (bf16[1,128,128]{2,0,1:T(2,128)(2,1)S(1)}, bf16[1,128,128]{2,0,1:T(2,128)(2,1)}, u32[]{:S(2)}) copy-start(bf16[1,128,128]{2,0,1:T(2,128)(2,1)} %get-tuple-element.162) | copy-start | bytes 98308
  101.5 9.9 %collective-permute-start.8 = (bf16[128,2,60]{0,1,2:T(2,128)(2,1)S(1)}, bf16[128,2,60]{0,1,2:T(2,128)(2,1)S(1)}, u32[]{:S(2)}, u32[]{:S(2)}) collective-permute-start(bf16[128,2,60]{0,1,2:T(2,128)(2,1)S(1)} %get-tuple-element.219), channel_id=1, source_target_pairs={{0,1},{1,2},{2,3},{3,4},{4,5},{5,6},{6,7},{7,8},{8,9},{9,10},{10,1... | collective-permute-start | bytes 92168 | tf_op jit(solution)/shard_map/ppermute | solution.py:34
  103.5 8.0 %collective-permute-start.9 = (bf16[128,2,60]{0,1,2:T(2,128)(2,1)S(1)}, bf16[128,2,60]{0,1,2:T(2,128)(2,1)S(1)}, u32[]{:S(2)}, u32[]{:S(2)}) collective-permute-start(bf16[128,2,60]{0,1,2:T(2,128)(2,1)S(1)} %get-tuple-element.220), channel_id=1, source_target_pairs={{1,0},{2,1},{3,2},{4,3},{5,4},{6,5},{7,6},{8,7},{9,8},{10,9},{11,1... | collective-permute-start | bytes 92168 | tf_op jit(solution)/shard_map/ppermute | solution.py:35
  111.6 3.8 %copy-start.6 = (bf16[1,128,128]{2,0,1:T(2,128)(2,1)S(1)}, bf16[1,128,128]{2,0,1:T(2,128)(2,1)}, u32[]{:S(2)}) copy-start(bf16[1,128,128]{2,0,1:T(2,128)(2,1)} %get-tuple-element.169) | copy-start | bytes 98308
  (22 other events, 49.2 us)

commit v9 on v8

--- a/solution.py
+++ b/solution.py
@@ -24,7 +24,7 @@
     return lax.all_to_all(copies, axis, split_axis=dim, concat_axis=dim, tiled=True)
 
 
-def extended_2(x, sides, width):
+def extended_2(x, sides, width, hold):
     for axis, dim in sides:
         size, length = (lax.axis_size(axis), x.shape[dim])
         up = [(i, (i + 1) % size) for i in range(size)]
@@ -32,6 +32,7 @@
         last = lax.slice_in_dim(x, length - width, length, axis=dim)
         initial = lax.slice_in_dim(x, 0, width, axis=dim)
         before = lax.ppermute(last, axis, up)
+        initial, _ = lax.optimization_barrier((initial, hold))
         after = lax.ppermute(initial, axis, down)
         x = jnp.concatenate([before, x, after], axis=dim)
     return x
@@ -118,7 +119,6 @@
 
 
 def conv_layer(activity, cycle_vals, kernel, source, gather_rims):
-    extended = gather_rims(cycle_vals)
     channels, tiles = activity.shape[0], activity.shape[1]
     square = activity.reshape(channels, tiles, P_SIZE, P_SIZE)
     padded = jnp.pad(square, ((0, 0), (0, 0), (1, 1), (1, 1)))
@@ -131,6 +131,7 @@
         dimension_numbers=("CNHW", "HWOI", "CNHW"),
         preferred_element_type=jnp.float32,
     )
+    extended = gather_rims(cycle_vals, summed)
     border = jnp.take(extended.reshape(channels, -1), source.reshape(-1), axis=1)
     border = border.reshape(channels, tiles, 4 * P_SIZE + 4)
     side = P_SIZE
@@ -211,8 +212,8 @@
     near_turns = lax.dynamic_slice_in_dim(quarter_turns, group_index * per_group, per_group, 0)
     local_beside = jnp.remainder(near_beside - first_tile + REACH, total_tiles)
 
-    def joined_rims(cycle_vals):
-        return extended_2(cycle_vals, ((("tile", "chan"), 1),), REACH)
+    def joined_rims(cycle_vals, hold):
+        return extended_2(cycle_vals, ((("tile", "chan"), 1),), REACH, hold)
 
     source = border_source(local_beside, near_turns)
     cycle_vals = jnp.take(activity, cycle_table(P_SIZE), axis=2)

time: 137 us -> 146 us (1.066)
  local copies, waits for them, and re-layouts: 32.2 us -> 38.7 us
  other arithmetic: 9.33 us -> 13 us
  matrix products: 13.2 us -> 11.3 us
    unnamed x112 -> x78, local copies, waits for them, and re-layouts: 8.9 us -> 13.7 us
    unnamed x36, matrix products: 7.81 us -> 4.83 us
  transfers between devices with their start and end apart: 12 -> 12, of which waited for: 2 -> 2; matrix products, arithmetic and copies ran while one was open for 14% -> 23% of each run, Pallas kernels for 0% -> 0%
where the time goes in v9:
time: 146 us; the launch traced here: 145 us
  starting transfers between devices  56.9 us (39%)
  local copies, waits for them, and re-layouts  38.7 us (27%)
  blocking collectives  17.4 us (12%)
  other arithmetic  13 us (9%)
  matrix products  11.3 us (8%)
  waiting for transfers between devices  5.96 us (4%)
    ppermute x4, starting transfers between devices, from_behind(): return lax.ppermute(value, axis, pairs)  22 us
    all_to_all x1, blocking collectives, on_device(): lax.all_to_all(activity, 'chan', split_axis=0, concat_axis=1, tiled=True)  17.4 us
    ppermute x3, starting transfers between devices, extended_2(): after = lax.ppermute(initial, axis, down)  16.8 us
    unnamed x78, local copies, waits for them, and re-layouts  13.7 us
    all_to_all x2, starting transfers between devices, gather_by_exchange(): lax.all_to_all(copies, axis, split_axis=dim, concat_axis=dim, tiled=True)  10.8 us
    ppermute x3, starting transfers between devices, extended_2(): before = lax.ppermute(last, axis, up)  7.43 us
    unnamed x36, matrix products  4.83 us
    all_to_all x2, waiting for transfers between devices, gather_by_exchange(): lax.all_to_all(copies, axis, split_axis=dim, concat_axis=dim, tiled=True)  4.45 us
  transfers between devices with their start and end apart: 12, of which 2 were waited for; matrix products, arithmetic and copies ran while one was open for 23% of the time, Pallas kernels for 0%

profile of v9, /device:TPU:2, one launch (start us, length us, event | category | flops | bytes accessed | tf_op | source)
XLA Modules:
  0.0 144.7 jit_solution(10194877685313718925)
XLA Ops:
  2.3 1.8 %copy.322 = bf16[8,8192]{0,1:T(8,128)(2,1)S(1)} copy(bf16[8,8192]{1,0:T(8,128)(2,1)} %param.45) | data formatting | bytes 262144 | tf_op args[0]
  4.1 2.0 %gather_fusion = bf16[640,8]{1,0:T(8,128)(2,1)S(1)} fusion(bf16[8,8192]{0,1:T(8,128)(2,1)S(1)} %copy.322, s32[1024]{0:T(1024)S(1)} %pad_clamp_fusion.4), kind=kCustom, calls=%fused_computation.6 | custom fusion | bytes 23040 | tf_op jit(solution)/shard_map/jit(_take)/gather | solution.py:186
  6.4 4.0 %collective-permute-start.3 = (bf16[8,128]{0,1:T(8,128)(2,1)S(1)}, bf16[8,128]{0,1:T(8,128)(2,1)S(1)}, u32[]{:S(2)}, u32[]{:S(2)}) collective-permute-start(bf16[8,128]{0,1:T(8,128)(2,1)S(1)} %get-tuple-element.188), channel_id=1, source_target_pairs={{0,16},{8,24},{16,32},{24,40},{32,48},{40,56},{48,64},{56,72},{64,... | collective-permute-start | bytes 6152 | tf_op jit(solution)/shard_map/ppermute | solution.py:14
  10.4 1.9 %collective-permute-start.2 = (bf16[8,128]{0,1:T(8,128)(2,1)S(1)}, bf16[8,128]{0,1:T(8,128)(2,1)S(1)}, u32[]{:S(2)}, u32[]{:S(2)}) collective-permute-start(bf16[8,128]{0,1:T(8,128)(2,1)S(1)} %get-tuple-element.189), channel_id=1, source_target_pairs={{0,8},{8,16},{16,24},{24,32},{32,40},{40,48},{48,56},{56,64},{64,7... | collective-permute-start | bytes 6152 | tf_op jit(solution)/shard_map/ppermute | solution.py:14
  12.3 10.3 %collective-permute-start.1 = (bf16[8,128]{0,1:T(8,128)(2,1)S(1)}, bf16[8,128]{0,1:T(8,128)(2,1)S(1)}, u32[]{:S(2)}, u32[]{:S(2)}) collective-permute-start(bf16[8,128]{0,1:T(8,128)(2,1)S(1)} %get-tuple-element.191), channel_id=1, source_target_pairs={{0,504},{8,0},{16,8},{24,16},{32,24},{40,32},{48,40},{56,48},{64,5... | collective-permute-start | bytes 6152 | tf_op jit(solution)/shard_map/ppermute | solution.py:14
  22.6 5.7 %collective-permute-start = (bf16[8,128]{0,1:T(8,128)(2,1)S(1)}, bf16[8,128]{0,1:T(8,128)(2,1)S(1)}, u32[]{:S(2)}, u32[]{:S(2)}) collective-permute-start(bf16[8,128]{0,1:T(8,128)(2,1)S(1)} %get-tuple-element.192), channel_id=1, source_target_pairs={{0,496},{8,504},{16,0},{24,8},{32,16},{40,24},{48,32},{56,40},{64,... | collective-permute-start | bytes 6152 | tf_op jit(solution)/shard_map/ppermute | solution.py:14
  33.6 1.9 %reshape.825 = bf16[8,2,23040]{2,1,0:T(2,128)(2,1)} reshape(bf16[128,9,320]{2,1,0:T(8,128)(2,1)S(1)} %bitcast.455) | data formatting | bytes 1474560
  36.6 5.9 %all-to-all-start = ((bf16[8,8,640]{2,1,0:T(8,128)(2,1)}), bf16[8,8,640]{2,1,0:T(8,128)(2,1)S(1)}, u32[]{:S(2)}, u32[]{:S(2)}) async-start(bf16[8,8,640]{2,1,0:T(8,128)(2,1)} %broadcast_in_dim.93), calls=%async_computation | async-start | bytes 163840 | tf_op jit(solution)/shard_map/all_to_all | solution.py:24
  43.1 4.4 %all-to-all-done = bf16[8,8,640]{2,1,0:T(8,128)(2,1)S(1)} async-done(((bf16[8,8,640]{2,1,0:T(8,128)(2,1)}), bf16[8,8,640]{2,1,0:T(8,128)(2,1)S(1)}, u32[]{:S(2)}, u32[]{:S(2)}) %all-to-all-start) | async-done | bytes 81952 | tf_op jit(solution)/shard_map/all_to_all | solution.py:24
  47.6 4.8 %all-to-all-start.1 = ((bf16[8,2,23040]{2,1,0:T(2,128)(2,1)}), bf16[8,2,23040]{2,1,0:T(2,128)(2,1)S(1)}, u32[]{:S(2)}, u32[]{:S(2)}) async-start(bf16[8,2,23040]{2,1,0:T(2,128)(2,1)} %reshape.825), calls=%async_computation.1 | async-start | bytes 1474560 | tf_op jit(solution)/shard_map/all_to_all | solution.py:24
  56.8 3.4 %collective-permute-start.4 = (bf16[64,2,60]{0,1,2:T(2,128)(2,1)}, bf16[64,2,60]{0,1,2:T(2,128)(2,1)}, u32[]{:S(2)}, u32[]{:S(2)}) collective-permute-start(bf16[64,2,60]{0,1,2:T(2,128)(2,1)} %get-tuple-element.229), channel_id=1, source_target_pairs={{0,1},{1,2},{2,3},{3,4},{4,5},{5,6},{6,7},{7,8},{8,9},{9,10},{10,1... | collective-permute-start | bytes 46088 | tf_op jit(solution)/shard_map/ppermute | solution.py:34
  61.2 1.3 reshape.826
  63.4 1.8 %convolution_select_fusion = f32[16,32,3,128]{3,1,2,0:T(8,128)S(1)} fusion(bf16[3,3,128,64]{2,3,1,0:T(8,128)(2,1)S(1)} %bitcast.480, bf16[64,16,4,8,5]{0,1,4,3,2:T(8,128)(2,1)} %fusion.19, pred[32,3]{0,1:T(4,128)(4,1)S(1)} %copy-done.23), kind=kOutput, calls=%fused_computation.26 | convolution fusion | flops 217251840 | bytes 1261664 | tf_op jit(solution)/shard_map/conv_general_dilated | solution.py:126
  65.8 4.6 %collective-permute-start.5 = (bf16[64,2,60]{0,1,2:T(2,128)(2,1)}, bf16[64,2,60]{0,1,2:T(2,128)(2,1)}, u32[]{:S(2)}, u32[]{:S(2)}) collective-permute-start(bf16[64,2,60]{0,1,2:T(2,128)(2,1)} %get-tuple-element.155), channel_id=1, source_target_pairs={{1,0},{2,1},{3,2},{4,3},{5,4},{6,5},{7,6},{8,7},{9,8},{10,9},{11,1... | collective-permute-start | bytes 46088 | tf_op jit(solution)/shard_map/ppermute | solution.py:36
  70.3 1.0 fusion.161
  72.0 1.5 %copy.424 = bf16[1,128,64]{1,2,0:T(8,128)(2,1)} copy(bf16[1,128,64]{2,0,1:T(2,128)(2,1)} %get-tuple-element.176) | data formatting | bytes 32768
  73.5 1.5 %copy.422 = bf16[1,128,64]{1,2,0:T(8,128)(2,1)} copy(bf16[1,128,64]{2,0,1:T(2,128)(2,1)} %get-tuple-element.178) | data formatting | bytes 32768
  80.9 1.5 %gather_fusion.2 = bf16[272,64]{1,0:T(8,128)(2,1)S(1)} fusion(bf16[64,480]{0,1:T(8,128)(2,1)S(1)} %reshape.820, s32[1024]{0:T(1024)} %pad_clamp_fusion.1), kind=kCustom, calls=%fused_computation.8 | custom fusion | bytes 70720 | tf_op jit(solution)/shard_map/jit(_take)/gather | solution.py:135
  85.6 1.1 fusion.66
  88.8 1.9 %collective-permute-start.6 = (bf16[128,2,60]{0,1,2:T(2,128)(2,1)S(1)}, bf16[128,2,60]{0,1,2:T(2,128)(2,1)S(1)}, u32[]{:S(2)}, u32[]{:S(2)}) collective-permute-start(bf16[128,2,60]{0,1,2:T(2,128)(2,1)S(1)} %get-tuple-element.227), channel_id=1, source_target_pairs={{0,1},{1,2},{2,3},{3,4},{4,5},{5,6},{6,7},{7,8},{8,9},{9,10},{10,1... | collective-permute-start | bytes 92168 | tf_op jit(solution)/shard_map/ppermute | solution.py:34
  90.9 1.1 convolution_select_fusion.2
  92.5 6.0 %collective-permute-start.7 = (bf16[128,2,60]{0,1,2:T(2,128)(2,1)S(1)}, bf16[128,2,60]{0,1,2:T(2,128)(2,1)S(1)}, u32[]{:S(2)}, u32[]{:S(2)}) collective-permute-start(bf16[128,2,60]{0,1,2:T(2,128)(2,1)S(1)} %get-tuple-element.156), channel_id=1, source_target_pairs={{1,0},{2,1},{3,2},{4,3},{5,4},{6,5},{7,6},{8,7},{9,8},{10,9},{11,1... | collective-permute-start | bytes 92168 | tf_op jit(solution)/shard_map/ppermute | solution.py:36
  98.5 2.4 %fusion.160 = (bf16[1,128,128]{2,0,1:T(2,128)(2,1)}, bf16[1,128,128]{2,0,1:T(2,128)(2,1)S(1)}, bf16[1,128,128]{2,0,1:T(2,128)(2,1)}, bf16[1,128,128]{2,0,1:T(2,1...) fusion(bf16[9,128,320]{2,0,1:T(8,128)(2,1)S(1)} %bitcast.454), kind=kLoop, calls=%fused_computation.327 | loop fusion | bytes 1048576 | tf_op jit(solution)/shard_map/slice | solution.py:113
  101.3 1.4 gather_fusion.6
  105.3 1.1 fusion.65
  108.5 2.1 %collective-permute-start.8 = (bf16[128,2,60]{0,1,2:T(2,128)(2,1)S(1)}, bf16[128,2,60]{0,1,2:T(2,128)(2,1)S(1)}, u32[]{:S(2)}, u32[]{:S(2)}) collective-permute-start(bf16[128,2,60]{0,1,2:T(2,128)(2,1)S(1)} %get-tuple-element.225), channel_id=1, source_target_pairs={{0,1},{1,2},{2,3},{3,4},{4,5},{5,6},{6,7},{7,8},{8,9},{9,10},{10,1... | collective-permute-start | bytes 92168 | tf_op jit(solution)/shard_map/ppermute | solution.py:34
  110.8 1.1 convolution_select_fusion.1
  112.4 6.2 %collective-permute-start.9 = (bf16[128,2,60]{0,1,2:T(2,128)(2,1)S(1)}, bf16[128,2,60]{0,1,2:T(2,128)(2,1)S(1)}, u32[]{:S(2)}, u32[]{:S(2)}) collective-permute-start(bf16[128,2,60]{0,1,2:T(2,128)(2,1)S(1)} %get-tuple-element.157), channel_id=1, source_target_pairs={{1,0},{2,1},{3,2},{4,3},{5,4},{6,5},{7,6},{8,7},{9,8},{10,9},{11,1... | collective-permute-start | bytes 92168 | tf_op jit(solution)/shard_map/ppermute | solution.py:36
  118.7 1.5 %collective-permute-done.9 = bf16[128,2,60]{0,1,2:T(2,128)(2,1)S(1)} collective-permute-done((bf16[128,2,60]{0,1,2:T(2,128)(2,1)S(1)}, bf16[128,2,60]{0,1,2:T(2,128)(2,1)S(1)}, u32[]{:S(2)}, u32[]{:S(2)}) %collective-permute-start.9) | collective-permute-done | bytes 30752 | tf_op jit(solution)/shard_map/ppermute | solution.py:36
  120.3 1.4 gather_fusion.8
  125.1 1.1 fusion.36
  126.4 17.4 %all_to_all.32 = bf16[128,4,256]{2,1,0:T(4,128)(2,1)S(1)} all-to-all(bf16[128,4,256]{2,1,0:T(4,128)(2,1)S(1)} %copy.408), channel_id=1, replica_groups=mesh['tile'=64,'chan'=8] {'chan'}, dimensions={0} | all-to-all | bytes 524288 | tf_op jit(solution)/shard_map/all_to_all | solution.py:222
  (259 shorter events, 37.9 us)
Async XLA Ops:
  0.0 28.4 %copy-start.21 = (s32[68]{0:T(128)S(1)}, s32[68]{0:T(128)}, u32[]{:S(2)}) copy-start(s32[68]{0:T(128)} %constant.579) | copy-start | bytes 820
  0.0 28.4 %copy-start.22 = (s32[60]{0:T(128)S(1)}, s32[60]{0:T(128)}, u32[]{:S(2)}) copy-start(s32[60]{0:T(128)} %constant.487.clone) | copy-start | bytes 724
  0.0 28.4 %copy-start.19 = (s32[32,8]{0,1:T(8,128)S(1)}, s32[32,8]{0,1:T(8,128)}, u32[]{:S(2)}) copy-start(s32[32,8]{0,1:T(8,128)} %param.51) | copy-start | bytes 3076
  0.0 28.4 %copy-start.18 = (s32[32,8]{0,1:T(8,128)S(1)}, s32[32,8]{0,1:T(8,128)}, u32[]{:S(2)}) copy-start(s32[32,8]{0,1:T(8,128)} %param.50) | copy-start | bytes 3076
  2.2 27.7 %copy-start.20 = (s32[68]{0:T(128)S(1)}, s32[68]{0:T(128)}, u32[]{:S(2)}) copy-start(s32[68]{0:T(128)} %constant.533) | copy-start | bytes 820
  2.2 30.5 %copy-start.13 = (bf16[9,16,128]{2,1,0:T(8,128)(2,1)S(1)}, bf16[9,16,128]{2,1,0:T(8,128)(2,1)}, u32[]{:S(2)}) copy-start(bf16[9,16,128]{2,1,0:T(8,128)(2,1)} %param.54) | copy-start | bytes 110596
  2.2 30.5 %copy-start.14 = (bf16[9,16,128]{2,1,0:T(8,128)(2,1)S(1)}, bf16[9,16,128]{2,1,0:T(8,128)(2,1)}, u32[]{:S(2)}) copy-start(bf16[9,16,128]{2,1,0:T(8,128)(2,1)} %param.53) | copy-start | bytes 110596
  2.3 30.5 %copy-start.15 = (bf16[9,16,64]{2,1,0:T(8,128)(2,1)S(1)}, bf16[9,16,64]{2,1,0:T(8,128)(2,1)}, u32[]{:S(2)}) copy-start(bf16[9,16,64]{2,1,0:T(8,128)(2,1)} %param.52) | copy-start | bytes 55300
  6.4 29.5 %collective-permute-start.3 = (bf16[8,128]{0,1:T(8,128)(2,1)S(1)}, bf16[8,128]{0,1:T(8,128)(2,1)S(1)}, u32[]{:S(2)}, u32[]{:S(2)}) collective-permute-start(bf16[8,128]{0,1:T(8,128)(2,1)S(1)} %get-tuple-element.188), channel_id=1, source_target_pairs={{0,16},{8,24},{16,32},{24,40},{32,48},{40,56},{48,64},{56,72},{64,... | collective-permute-start | bytes 6152 | tf_op jit(solution)/shard_map/ppermute | solution.py:14
  10.4 25.4 %collective-permute-start.2 = (bf16[8,128]{0,1:T(8,128)(2,1)S(1)}, bf16[8,128]{0,1:T(8,128)(2,1)S(1)}, u32[]{:S(2)}, u32[]{:S(2)}) collective-permute-start(bf16[8,128]{0,1:T(8,128)(2,1)S(1)} %get-tuple-element.189), channel_id=1, source_target_pairs={{0,8},{8,16},{16,24},{24,32},{32,40},{40,48},{48,56},{56,64},{64,7... | collective-permute-start | bytes 6152 | tf_op jit(solution)/shard_map/ppermute | solution.py:14
  12.3 23.3 %collective-permute-start.1 = (bf16[8,128]{0,1:T(8,128)(2,1)S(1)}, bf16[8,128]{0,1:T(8,128)(2,1)S(1)}, u32[]{:S(2)}, u32[]{:S(2)}) collective-permute-start(bf16[8,128]{0,1:T(8,128)(2,1)S(1)} %get-tuple-element.191), channel_id=1, source_target_pairs={{0,504},{8,0},{16,8},{24,16},{32,24},{40,32},{48,40},{56,48},{64,5... | collective-permute-start | bytes 6152 | tf_op jit(solution)/shard_map/ppermute | solution.py:14
  22.6 12.9 %collective-permute-start = (bf16[8,128]{0,1:T(8,128)(2,1)S(1)}, bf16[8,128]{0,1:T(8,128)(2,1)S(1)}, u32[]{:S(2)}, u32[]{:S(2)}) collective-permute-start(bf16[8,128]{0,1:T(8,128)(2,1)S(1)} %get-tuple-element.192), channel_id=1, source_target_pairs={{0,496},{8,504},{16,0},{24,8},{32,16},{40,24},{48,32},{56,40},{64,... | collective-permute-start | bytes 6152 | tf_op jit(solution)/shard_map/ppermute | solution.py:14
  28.4 27.0 %copy-start.16 = (s32[1024]{0:T(1024)}, s32[1024]{0:T(1024)S(1)}, u32[]{:S(2)}) copy-start(s32[1024]{0:T(1024)S(1)} %get-tuple-element.257) | copy-start | bytes 12292
  36.6 11.0 %all-to-all-start = ((bf16[8,8,640]{2,1,0:T(8,128)(2,1)}), bf16[8,8,640]{2,1,0:T(8,128)(2,1)S(1)}, u32[]{:S(2)}, u32[]{:S(2)}) async-start(bf16[8,8,640]{2,1,0:T(8,128)(2,1)} %broadcast_in_dim.93), calls=%async_computation | async-start | bytes 163840 | tf_op jit(solution)/shard_map/all_to_all | solution.py:24
  47.6 13.6 %all-to-all-start.1 = ((bf16[8,2,23040]{2,1,0:T(2,128)(2,1)}), bf16[8,2,23040]{2,1,0:T(2,128)(2,1)S(1)}, u32[]{:S(2)}, u32[]{:S(2)}) async-start(bf16[8,2,23040]{2,1,0:T(2,128)(2,1)} %reshape.825), calls=%async_computation.1 | async-start | bytes 1474560 | tf_op jit(solution)/shard_map/all_to_all | solution.py:24
  56.8 23.1 %collective-permute-start.4 = (bf16[64,2,60]{0,1,2:T(2,128)(2,1)}, bf16[64,2,60]{0,1,2:T(2,128)(2,1)}, u32[]{:S(2)}, u32[]{:S(2)}) collective-permute-start(bf16[64,2,60]{0,1,2:T(2,128)(2,1)} %get-tuple-element.229), channel_id=1, source_target_pairs={{0,1},{1,2},{2,3},{3,4},{4,5},{5,6},{6,7},{7,8},{8,9},{9,10},{10,1... | collective-permute-start | bytes 46088 | tf_op jit(solution)/shard_map/ppermute | solution.py:34
  65.8 14.2 %collective-permute-start.5 = (bf16[64,2,60]{0,1,2:T(2,128)(2,1)}, bf16[64,2,60]{0,1,2:T(2,128)(2,1)}, u32[]{:S(2)}, u32[]{:S(2)}) collective-permute-start(bf16[64,2,60]{0,1,2:T(2,128)(2,1)} %get-tuple-element.155), channel_id=1, source_target_pairs={{1,0},{2,1},{3,2},{4,3},{5,4},{6,5},{7,6},{8,7},{9,8},{10,9},{11,1... | collective-permute-start | bytes 46088 | tf_op jit(solution)/shard_map/ppermute | solution.py:36
  78.9 5.2 %copy-start.7 = (bf16[1,128,64]{1,2,0:T(8,128)(2,1)S(1)}, bf16[1,128,64]{1,2,0:T(8,128)(2,1)}, u32[]{:S(2)}) copy-start(bf16[1,128,64]{1,2,0:T(8,128)(2,1)} %copy.422) | copy-start | bytes 49156
  79.0 4.3 %copy-start.12 = (bf16[1,128,64]{1,2,0:T(8,128)(2,1)S(1)}, bf16[1,128,64]{1,2,0:T(8,128)(2,1)}, u32[]{:S(2)}) copy-start(bf16[1,128,64]{1,2,0:T(8,128)(2,1)} %copy.418) | copy-start | bytes 49156
  79.0 4.4 %copy-start.8 = (bf16[1,128,64]{1,2,0:T(8,128)(2,1)S(1)}, bf16[1,128,64]{1,2,0:T(8,128)(2,1)}, u32[]{:S(2)}) copy-start(bf16[1,128,64]{1,2,0:T(8,128)(2,1)} %copy.419) | copy-start | bytes 49156
  79.0 5.7 %copy-start.11 = (bf16[1,128,64]{1,2,0:T(8,128)(2,1)S(1)}, bf16[1,128,64]{1,2,0:T(8,128)(2,1)}, u32[]{:S(2)}) copy-start(bf16[1,128,64]{1,2,0:T(8,128)(2,1)} %copy.421) | copy-start | bytes 49156
  79.0 5.8 %copy-start.10 = (bf16[1,128,64]{1,2,0:T(8,128)(2,1)S(1)}, bf16[1,128,64]{1,2,0:T(8,128)(2,1)}, u32[]{:S(2)}) copy-start(bf16[1,128,64]{1,2,0:T(8,128)(2,1)} %copy.423) | copy-start | bytes 49156
  79.0 6.0 %copy-start.9 = (bf16[1,128,64]{1,2,0:T(8,128)(2,1)S(1)}, bf16[1,128,64]{1,2,0:T(8,128)(2,1)}, u32[]{:S(2)}) copy-start(bf16[1,128,64]{1,2,0:T(8,128)(2,1)} %copy.424) | copy-start | bytes 49156
  88.8 12.3 %collective-permute-start.6 = (bf16[128,2,60]{0,1,2:T(2,128)(2,1)S(1)}, bf16[128,2,60]{0,1,2:T(2,128)(2,1)S(1)}, u32[]{:S(2)}, u32[]{:S(2)}) collective-permute-start(bf16[128,2,60]{0,1,2:T(2,128)(2,1)S(1)} %get-tuple-element.227), channel_id=1, source_target_pairs={{0,1},{1,2},{2,3},{3,4},{4,5},{5,6},{6,7},{7,8},{8,9},{9,10},{10,1... | collective-permute-start | bytes 92168 | tf_op jit(solution)/shard_map/ppermute | solution.py:34
  92.5 8.6 %collective-permute-start.7 = (bf16[128,2,60]{0,1,2:T(2,128)(2,1)S(1)}, bf16[128,2,60]{0,1,2:T(2,128)(2,1)S(1)}, u32[]{:S(2)}, u32[]{:S(2)}) collective-permute-start(bf16[128,2,60]{0,1,2:T(2,128)(2,1)S(1)} %get-tuple-element.156), channel_id=1, source_target_pairs={{1,0},{2,1},{3,2},{4,3},{5,4},{6,5},{7,6},{8,7},{9,8},{10,9},{11,1... | collective-permute-start | bytes 92168 | tf_op jit(solution)/shard_map/ppermute | solution.py:36
  101.2 3.7 %copy-start.4 = (bf16[1,128,128]{2,0,1:T(2,128)(2,1)S(1)}, bf16[1,128,128]{2,0,1:T(2,128)(2,1)}, u32[]{:S(2)}) copy-start(bf16[1,128,128]{2,0,1:T(2,128)(2,1)} %get-tuple-element.167) | copy-start | bytes 98308
  101.3 3.8 %copy-start.3 = (bf16[1,128,128]{2,0,1:T(2,128)(2,1)S(1)}, bf16[1,128,128]{2,0,1:T(2,128)(2,1)}, u32[]{:S(2)}) copy-start(bf16[1,128,128]{2,0,1:T(2,128)(2,1)} %get-tuple-element.168) | copy-start | bytes 98308
  108.5 10.2 %collective-permute-start.8 = (bf16[128,2,60]{0,1,2:T(2,128)(2,1)S(1)}, bf16[128,2,60]{0,1,2:T(2,128)(2,1)S(1)}, u32[]{:S(2)}, u32[]{:S(2)}) collective-permute-start(bf16[128,2,60]{0,1,2:T(2,128)(2,1)S(1)} %get-tuple-element.225), channel_id=1, source_target_pairs={{0,1},{1,2},{2,3},{3,4},{4,5},{5,6},{6,7},{7,8},{8,9},{9,10},{10,1... | collective-permute-start | bytes 92168 | tf_op jit(solution)/shard_map/ppermute | solution.py:34
  112.4 9.5 %copy-start.2 = (bf16[1,128,128]{2,0,1:T(2,128)(2,1)S(1)}, bf16[1,128,128]{2,0,1:T(2,128)(2,1)}, u32[]{:S(2)}) copy-start(bf16[1,128,128]{2,0,1:T(2,128)(2,1)} %get-tuple-element.165) | copy-start | bytes 98308
  112.4 10.2 %copy-start.1 = (bf16[1,128,128]{2,0,1:T(2,128)(2,1)S(1)}, bf16[1,128,128]{2,0,1:T(2,128)(2,1)}, u32[]{:S(2)}) copy-start(bf16[1,128,128]{2,0,1:T(2,128)(2,1)} %get-tuple-element.162) | copy-start | bytes 98308
  112.4 7.7 %collective-permute-start.9 = (bf16[128,2,60]{0,1,2:T(2,128)(2,1)S(1)}, bf16[128,2,60]{0,1,2:T(2,128)(2,1)S(1)}, u32[]{:S(2)}, u32[]{:S(2)}) collective-permute-start(bf16[128,2,60]{0,1,2:T(2,128)(2,1)S(1)} %get-tuple-element.157), channel_id=1, source_target_pairs={{1,0},{2,1},{3,2},{4,3},{5,4},{6,5},{7,6},{8,7},{9,8},{10,9},{11,1... | collective-permute-start | bytes 92168 | tf_op jit(solution)/shard_map/ppermute | solution.py:36
  120.3 3.7 %copy-start = (bf16[1,128,128]{2,0,1:T(2,128)(2,1)S(1)}, bf16[1,128,128]{2,0,1:T(2,128)(2,1)}, u32[]{:S(2)}) copy-start(bf16[1,128,128]{2,0,1:T(2,128)(2,1)} %get-tuple-element.160) | copy-start | bytes 98308
  (5 other events, 9.8 us)

commit v10 on v8

--- a/solution.py
+++ b/solution.py
@@ -72,28 +72,6 @@
     heading += [4, 5, 6, 7]
     anchor += [2 * extent - 2, extent - 1, 3 * extent - 3, 0]
     return (np.array(heading, np.int32), np.array(anchor, np.int32))
-
-
-def layout_table(extent):
-    padded_side = extent + 2
-    interior = extent * extent
-    entries = []
-    for row_at in range(padded_side):
-        for col_at in range(padded_side):
-            if 1 <= row_at <= extent and 1 <= col_at <= extent:
-                entries.append((row_at - 1) * extent + col_at - 1)
-            elif row_at == 0 and 1 <= col_at <= extent:
-                entries.append(interior + col_at - 1)
-            elif row_at == padded_side - 1 and 1 <= col_at <= extent:
-                entries.append(interior + extent + col_at - 1)
-            elif col_at == 0 and 1 <= row_at <= extent:
-                entries.append(interior + 2 * extent + row_at - 1)
-            elif col_at == padded_side - 1 and 1 <= row_at <= extent:
-                entries.append(interior + 3 * extent + row_at - 1)
-            else:
-                corner = (0 if row_at == 0 else 2) + (0 if col_at == 0 else 1)
-                entries.append(interior + 4 * extent + corner)
-    return np.array(entries, np.int32)
 
 
 def border_source(local_beside, local_turns):
@@ -148,7 +126,8 @@
     summed = summed.reshape(summed.shape[0], tiles, side * side)
     ring = jnp.take(summed, cycle_table(P_SIZE), axis=2)
     next_cycles = jax.nn.gelu(ring, approximate=False).astype(jnp.bfloat16)
-    return jax.nn.gelu(summed, approximate=False).astype(jnp.bfloat16), next_cycles
+    full = jax.nn.gelu(summed, approximate=False).astype(jnp.bfloat16)
+    return full, next_cycles
 
 
 def on_device(
@@ -168,7 +147,6 @@
     tiles_here = corner_slot.shape[1]
     near_count = send_rows.shape[1]
     capacity = send_rows.shape[2]
-    channels_here = analysis.shape[0]
     pixels = corner_slot.shape[2]
     total_tiles = tiles_here * shards
     per_group = tiles_here // groups
@@ -223,7 +201,7 @@
 
 
 def solution(mesh):
-    step = jax.shard_map(
+    return jax.shard_map(
         on_device,
         mesh=mesh,
         in_specs=(
@@ -241,4 +219,3 @@
         out_specs=P("chan", "tile", None),
         check_vma=False,
     )
-    return step

time: 137 us -> 137 us (level)
  no operation moved by 1% of the time
where the time goes in v10:
time: 137 us; the launch traced here: 136 us
  starting transfers between devices  56.7 us (41%)
  local copies, waits for them, and re-layouts  32.2 us (24%)
  blocking collectives  17.2 us (13%)
  matrix products  13.2 us (10%)
  other arithmetic  9.33 us (7%)
  waiting for transfers between devices  5.53 us (4%)
  between operations  1.62 us (1%)
    ppermute x4, starting transfers between devices, from_behind(): return lax.ppermute(value, axis, pairs)  21.4 us
    all_to_all x1, blocking collectives, on_device(): lax.all_to_all(activity, 'chan', split_axis=0, concat_axis=1, tiled=True)  17.2 us
    ppermute x3, starting transfers between devices, extended_2(): after = lax.ppermute(initial, axis, down)  16.2 us
    all_to_all x2, starting transfers between devices, gather_by_exchange(): lax.all_to_all(copies, axis, split_axis=dim, concat_axis=dim, tiled=True)  10.8 us
    unnamed x112, local copies, waits for them, and re-layouts  8.9 us
    ppermute x3, starting transfers between devices, extended_2(): before = lax.ppermute(last, axis, up)  8.33 us
    unnamed x36, matrix products  7.81 us
    all_to_all x2, waiting for transfers between devices, gather_by_exchange(): lax.all_to_all(copies, axis, split_axis=dim, concat_axis=dim, tiled=True)  4.44 us
  transfers between devices with their start and end apart: 12, of which 2 were waited for; matrix products, arithmetic and copies ran while one was open for 14% of the time, Pallas kernels for 0%

profile of v10, /device:TPU:2, one launch (start us, length us, event | category | flops | bytes accessed | tf_op | source)
XLA Modules:
  0.0 135.7 jit_solution(15249998849516454676)
XLA Ops:
  0.1 1.9 %copy.322 = bf16[8,8192]{0,1:T(8,128)(2,1)S(1)} copy(bf16[8,8192]{1,0:T(8,128)(2,1)} %param.45) | data formatting | bytes 262144 | tf_op args[0]
  2.1 2.0 %gather_fusion = bf16[640,8]{1,0:T(8,128)(2,1)S(1)} fusion(bf16[8,8192]{0,1:T(8,128)(2,1)S(1)} %copy.322, s32[1024]{0:T(1024)S(1)} %pad_clamp_fusion.4), kind=kCustom, calls=%fused_computation.6 | custom fusion | bytes 23040 | tf_op jit(solution)/shard_map/jit(_take)/gather | solution.py:163
  4.4 13.0 %collective-permute-start = (bf16[8,128]{0,1:T(8,128)(2,1)S(1)}, bf16[8,128]{0,1:T(8,128)(2,1)S(1)}, u32[]{:S(2)}, u32[]{:S(2)}) collective-permute-start(bf16[8,128]{0,1:T(8,128)(2,1)S(1)} %get-tuple-element.186), channel_id=1, source_target_pairs={{0,496},{8,504},{16,0},{24,8},{32,16},{40,24},{48,32},{56,40},{64,... | collective-permute-start | bytes 6152 | tf_op jit(solution)/shard_map/ppermute | solution.py:14
  17.4 2.5 %collective-permute-start.1 = (bf16[8,128]{0,1:T(8,128)(2,1)S(1)}, bf16[8,128]{0,1:T(8,128)(2,1)S(1)}, u32[]{:S(2)}, u32[]{:S(2)}) collective-permute-start(bf16[8,128]{0,1:T(8,128)(2,1)S(1)} %get-tuple-element.185), channel_id=1, source_target_pairs={{0,504},{8,0},{16,8},{24,16},{32,24},{40,32},{48,40},{56,48},{64,5... | collective-permute-start | bytes 6152 | tf_op jit(solution)/shard_map/ppermute | solution.py:14
  19.9 1.9 %collective-permute-start.2 = (bf16[8,128]{0,1:T(8,128)(2,1)S(1)}, bf16[8,128]{0,1:T(8,128)(2,1)S(1)}, u32[]{:S(2)}, u32[]{:S(2)}) collective-permute-start(bf16[8,128]{0,1:T(8,128)(2,1)S(1)} %get-tuple-element.183), channel_id=1, source_target_pairs={{0,8},{8,16},{16,24},{24,32},{32,40},{40,48},{48,56},{56,64},{64,7... | collective-permute-start | bytes 6152 | tf_op jit(solution)/shard_map/ppermute | solution.py:14
  21.8 4.0 %collective-permute-start.3 = (bf16[8,128]{0,1:T(8,128)(2,1)S(1)}, bf16[8,128]{0,1:T(8,128)(2,1)S(1)}, u32[]{:S(2)}, u32[]{:S(2)}) collective-permute-start(bf16[8,128]{0,1:T(8,128)(2,1)S(1)} %get-tuple-element.182), channel_id=1, source_target_pairs={{0,16},{8,24},{16,32},{24,40},{32,48},{40,56},{48,64},{56,72},{64,... | collective-permute-start | bytes 6152 | tf_op jit(solution)/shard_map/ppermute | solution.py:14
  30.7 1.9 %reshape.825 = bf16[8,2,23040]{2,1,0:T(2,128)(2,1)} reshape(bf16[128,9,320]{2,1,0:T(8,128)(2,1)S(1)} %bitcast.455) | data formatting | bytes 1474560
  33.6 5.9 %all-to-all-start = ((bf16[8,8,640]{2,1,0:T(8,128)(2,1)}), bf16[8,8,640]{2,1,0:T(8,128)(2,1)S(1)}, u32[]{:S(2)}, u32[]{:S(2)}) async-start(bf16[8,8,640]{2,1,0:T(8,128)(2,1)} %broadcast_in_dim.93), calls=%async_computation | async-start | bytes 163840 | tf_op jit(solution)/shard_map/all_to_all | solution.py:24
  40.1 4.4 %all-to-all-done = bf16[8,8,640]{2,1,0:T(8,128)(2,1)S(1)} async-done(((bf16[8,8,640]{2,1,0:T(8,128)(2,1)}), bf16[8,8,640]{2,1,0:T(8,128)(2,1)S(1)}, u32[]{:S(2)}, u32[]{:S(2)}) %all-to-all-start) | async-done | bytes 81952 | tf_op jit(solution)/shard_map/all_to_all | solution.py:24
  44.5 4.8 %all-to-all-start.1 = ((bf16[8,2,23040]{2,1,0:T(2,128)(2,1)}), bf16[8,2,23040]{2,1,0:T(2,128)(2,1)S(1)}, u32[]{:S(2)}, u32[]{:S(2)}) async-start(bf16[8,2,23040]{2,1,0:T(2,128)(2,1)} %reshape.825), calls=%async_computation.1 | async-start | bytes 1474560 | tf_op jit(solution)/shard_map/all_to_all | solution.py:24
  53.0 3.4 %collective-permute-start.4 = (bf16[64,2,60]{0,1,2:T(2,128)(2,1)S(1)}, bf16[64,2,60]{0,1,2:T(2,128)(2,1)S(1)}, u32[]{:S(2)}, u32[]{:S(2)}) collective-permute-start(bf16[64,2,60]{0,1,2:T(2,128)(2,1)S(1)} %get-tuple-element.223), channel_id=1, source_target_pairs={{0,1},{1,2},{2,3},{3,4},{4,5},{5,6},{6,7},{7,8},{8,9},{9,10},{10,1... | collective-permute-start | bytes 46088 | tf_op jit(solution)/shard_map/ppermute | solution.py:34
  56.4 4.8 %collective-permute-start.5 = (bf16[64,2,60]{0,1,2:T(2,128)(2,1)S(1)}, bf16[64,2,60]{0,1,2:T(2,128)(2,1)S(1)}, u32[]{:S(2)}, u32[]{:S(2)}) collective-permute-start(bf16[64,2,60]{0,1,2:T(2,128)(2,1)S(1)} %get-tuple-element.224), channel_id=1, source_target_pairs={{1,0},{2,1},{3,2},{4,3},{5,4},{6,5},{7,6},{8,7},{9,8},{10,9},{11,1... | collective-permute-start | bytes 46088 | tf_op jit(solution)/shard_map/ppermute | solution.py:35
  61.5 1.1 collective-permute-done.5
  62.7 1.4 %gather_fusion.2 = bf16[272,64]{1,0:T(8,128)(2,1)S(1)} fusion(bf16[64,480]{0,1:T(8,128)(2,1)S(1)} %reshape.820, s32[1024]{0:T(1024)S(1)} %pad_clamp_fusion.1), kind=kCustom, calls=%fused_computation.8 | custom fusion | bytes 70720 | tf_op jit(solution)/shard_map/jit(_take)/gather | solution.py:112
  66.9 1.3 reshape.826
  70.4 2.5 %fusion.160 = (bf16[1,128,128]{2,0,1:T(2,128)(2,1)}, bf16[1,128,128]{2,0,1:T(2,128)(2,1)}, bf16[1,128,128]{2,0,1:T(2,128)(2,1)}, bf16[1,128,128]{2,0,1:T(2,128)(...) fusion(bf16[9,128,320]{2,0,1:T(8,128)(2,1)S(1)} %bitcast.453), kind=kLoop, calls=%fused_computation.327 | loop fusion | bytes 1048576 | tf_op jit(solution)/shard_map/slice | solution.py:90
  75.5 0.8 fusion.112
  76.3 0.8 fusion.114
  77.1 0.8 fusion.120
  78.0 0.8 fusion.130
  79.7 1.1 fusion.66
  82.9 3.0 %collective-permute-start.6 = (bf16[128,2,60]{0,1,2:T(2,128)(2,1)S(1)}, bf16[128,2,60]{0,1,2:T(2,128)(2,1)S(1)}, u32[]{:S(2)}, u32[]{:S(2)}) collective-permute-start(bf16[128,2,60]{0,1,2:T(2,128)(2,1)S(1)} %get-tuple-element.221), channel_id=1, source_target_pairs={{0,1},{1,2},{2,3},{3,4},{4,5},{5,6},{6,7},{7,8},{8,9},{9,10},{10,1... | collective-permute-start | bytes 92168 | tf_op jit(solution)/shard_map/ppermute | solution.py:34
  86.0 5.4 %collective-permute-start.7 = (bf16[128,2,60]{0,1,2:T(2,128)(2,1)S(1)}, bf16[128,2,60]{0,1,2:T(2,128)(2,1)S(1)}, u32[]{:S(2)}, u32[]{:S(2)}) collective-permute-start(bf16[128,2,60]{0,1,2:T(2,128)(2,1)S(1)} %get-tuple-element.222), channel_id=1, source_target_pairs={{1,0},{2,1},{3,2},{4,3},{5,4},{6,5},{7,6},{8,7},{9,8},{10,9},{11,1... | collective-permute-start | bytes 92168 | tf_op jit(solution)/shard_map/ppermute | solution.py:35
  92.1 1.1 convolution_select_fusion.2
  94.3 1.4 %gather_fusion.6 = bf16[272,128]{1,0:T(8,128)(2,1)S(1)} fusion(bf16[128,480]{0,1:T(8,128)(2,1)S(1)} %reshape.608, s32[1024]{0:T(1024)S(1)} %copy-done.30), kind=kCustom, calls=%fused_computation.2.clone | custom fusion | bytes 140352 | tf_op jit(solution)/shard_map/jit(_take)/gather | solution.py:112
  98.7 1.1 fusion.65
  101.5 1.9 %collective-permute-start.8 = (bf16[128,2,60]{0,1,2:T(2,128)(2,1)S(1)}, bf16[128,2,60]{0,1,2:T(2,128)(2,1)S(1)}, u32[]{:S(2)}, u32[]{:S(2)}) collective-permute-start(bf16[128,2,60]{0,1,2:T(2,128)(2,1)S(1)} %get-tuple-element.219), channel_id=1, source_target_pairs={{0,1},{1,2},{2,3},{3,4},{4,5},{5,6},{6,7},{7,8},{8,9},{9,10},{10,1... | collective-permute-start | bytes 92168 | tf_op jit(solution)/shard_map/ppermute | solution.py:34
  103.5 6.0 %collective-permute-start.9 = (bf16[128,2,60]{0,1,2:T(2,128)(2,1)S(1)}, bf16[128,2,60]{0,1,2:T(2,128)(2,1)S(1)}, u32[]{:S(2)}, u32[]{:S(2)}) collective-permute-start(bf16[128,2,60]{0,1,2:T(2,128)(2,1)S(1)} %get-tuple-element.220), channel_id=1, source_target_pairs={{1,0},{2,1},{3,2},{4,3},{5,4},{6,5},{7,6},{8,7},{9,8},{10,9},{11,1... | collective-permute-start | bytes 92168 | tf_op jit(solution)/shard_map/ppermute | solution.py:35
  109.7 1.1 convolution_select_fusion.1
  111.6 1.4 %gather_fusion.8 = bf16[272,128]{1,0:T(8,128)(2,1)S(1)} fusion(bf16[128,480]{0,1:T(8,128)(2,1)S(1)} %reshape.617, s32[1024]{0:T(1024)S(1)} %copy-done.30), kind=kCustom, calls=%fused_computation.5.clone | custom fusion | bytes 140352 | tf_op jit(solution)/shard_map/jit(_take)/gather | solution.py:112
  116.4 1.1 fusion.36
  117.7 17.2 %all_to_all.32 = bf16[128,4,256]{2,1,0:T(4,128)(2,1)S(1)} all-to-all(bf16[128,4,256]{2,1,0:T(4,128)(2,1)S(1)} %copy.408), channel_id=1, replica_groups=mesh['tile'=64,'chan'=8] {'chan'}, dimensions={0} | all-to-all | bytes 524288 | tf_op jit(solution)/shard_map/all_to_all | solution.py:199
  (293 shorter events, 32.1 us)
Async XLA Ops:
  0.0 25.8 %copy-start.37 = (s32[60]{0:T(128)S(1)}, s32[60]{0:T(128)}, u32[]{:S(2)}) copy-start(s32[60]{0:T(128)} %constant.487.clone) | copy-start | bytes 724
  0.0 25.8 %copy-start.38 = (s32[68]{0:T(128)S(1)}, s32[68]{0:T(128)}, u32[]{:S(2)}) copy-start(s32[68]{0:T(128)} %constant.579) | copy-start | bytes 820
  0.0 27.3 %copy-start.36 = (s32[68]{0:T(128)S(1)}, s32[68]{0:T(128)}, u32[]{:S(2)}) copy-start(s32[68]{0:T(128)} %constant.533) | copy-start | bytes 820
  0.0 25.8 %copy-start.34 = (s32[32,8]{0,1:T(8,128)S(1)}, s32[32,8]{0,1:T(8,128)}, u32[]{:S(2)}) copy-start(s32[32,8]{0,1:T(8,128)} %param.50) | copy-start | bytes 3076
  0.0 25.8 %copy-start.35 = (s32[32,8]{0,1:T(8,128)S(1)}, s32[32,8]{0,1:T(8,128)}, u32[]{:S(2)}) copy-start(s32[32,8]{0,1:T(8,128)} %param.51) | copy-start | bytes 3076
  0.0 29.6 %copy-start.29 = (bf16[9,16,64]{2,1,0:T(8,128)(2,1)S(1)}, bf16[9,16,64]{2,1,0:T(8,128)(2,1)}, u32[]{:S(2)}) copy-start(bf16[9,16,64]{2,1,0:T(8,128)(2,1)} %param.52) | copy-start | bytes 55300
  0.1 29.6 %copy-start.28 = (bf16[9,16,128]{2,1,0:T(8,128)(2,1)S(1)}, bf16[9,16,128]{2,1,0:T(8,128)(2,1)}, u32[]{:S(2)}) copy-start(bf16[9,16,128]{2,1,0:T(8,128)(2,1)} %param.53) | copy-start | bytes 110596
  0.1 29.6 %copy-start.27 = (bf16[9,16,128]{2,1,0:T(8,128)(2,1)S(1)}, bf16[9,16,128]{2,1,0:T(8,128)(2,1)}, u32[]{:S(2)}) copy-start(bf16[9,16,128]{2,1,0:T(8,128)(2,1)} %param.54) | copy-start | bytes 110596
  4.4 28.1 %collective-permute-start = (bf16[8,128]{0,1:T(8,128)(2,1)S(1)}, bf16[8,128]{0,1:T(8,128)(2,1)S(1)}, u32[]{:S(2)}, u32[]{:S(2)}) collective-permute-start(bf16[8,128]{0,1:T(8,128)(2,1)S(1)} %get-tuple-element.186), channel_id=1, source_target_pairs={{0,496},{8,504},{16,0},{24,8},{32,16},{40,24},{48,32},{56,40},{64,... | collective-permute-start | bytes 6152 | tf_op jit(solution)/shard_map/ppermute | solution.py:14
  17.4 15.2 %collective-permute-start.1 = (bf16[8,128]{0,1:T(8,128)(2,1)S(1)}, bf16[8,128]{0,1:T(8,128)(2,1)S(1)}, u32[]{:S(2)}, u32[]{:S(2)}) collective-permute-start(bf16[8,128]{0,1:T(8,128)(2,1)S(1)} %get-tuple-element.185), channel_id=1, source_target_pairs={{0,504},{8,0},{16,8},{24,16},{32,24},{40,32},{48,40},{56,48},{64,5... | collective-permute-start | bytes 6152 | tf_op jit(solution)/shard_map/ppermute | solution.py:14
  19.9 12.9 %collective-permute-start.2 = (bf16[8,128]{0,1:T(8,128)(2,1)S(1)}, bf16[8,128]{0,1:T(8,128)(2,1)S(1)}, u32[]{:S(2)}, u32[]{:S(2)}) collective-permute-start(bf16[8,128]{0,1:T(8,128)(2,1)S(1)} %get-tuple-element.183), channel_id=1, source_target_pairs={{0,8},{8,16},{16,24},{24,32},{32,40},{40,48},{48,56},{56,64},{64,7... | collective-permute-start | bytes 6152 | tf_op jit(solution)/shard_map/ppermute | solution.py:14
  21.8 11.0 %collective-permute-start.3 = (bf16[8,128]{0,1:T(8,128)(2,1)S(1)}, bf16[8,128]{0,1:T(8,128)(2,1)S(1)}, u32[]{:S(2)}, u32[]{:S(2)}) collective-permute-start(bf16[8,128]{0,1:T(8,128)(2,1)S(1)} %get-tuple-element.182), channel_id=1, source_target_pairs={{0,16},{8,24},{16,32},{24,40},{32,48},{40,56},{48,64},{56,72},{64,... | collective-permute-start | bytes 6152 | tf_op jit(solution)/shard_map/ppermute | solution.py:14
  25.9 26.4 %copy-start.32 = (s32[1024]{0:T(1024)}, s32[1024]{0:T(1024)S(1)}, u32[]{:S(2)}) copy-start(s32[1024]{0:T(1024)S(1)} %get-tuple-element.251) | copy-start | bytes 12292
  33.6 11.0 %all-to-all-start = ((bf16[8,8,640]{2,1,0:T(8,128)(2,1)}), bf16[8,8,640]{2,1,0:T(8,128)(2,1)S(1)}, u32[]{:S(2)}, u32[]{:S(2)}) async-start(bf16[8,8,640]{2,1,0:T(8,128)(2,1)} %broadcast_in_dim.93), calls=%async_computation | async-start | bytes 163840 | tf_op jit(solution)/shard_map/all_to_all | solution.py:24
  44.5 22.3 %all-to-all-start.1 = ((bf16[8,2,23040]{2,1,0:T(2,128)(2,1)}), bf16[8,2,23040]{2,1,0:T(2,128)(2,1)S(1)}, u32[]{:S(2)}, u32[]{:S(2)}) async-start(bf16[8,2,23040]{2,1,0:T(2,128)(2,1)} %reshape.825), calls=%async_computation.1 | async-start | bytes 1474560 | tf_op jit(solution)/shard_map/all_to_all | solution.py:24
  53.0 8.5 %collective-permute-start.4 = (bf16[64,2,60]{0,1,2:T(2,128)(2,1)S(1)}, bf16[64,2,60]{0,1,2:T(2,128)(2,1)S(1)}, u32[]{:S(2)}, u32[]{:S(2)}) collective-permute-start(bf16[64,2,60]{0,1,2:T(2,128)(2,1)S(1)} %get-tuple-element.223), channel_id=1, source_target_pairs={{0,1},{1,2},{2,3},{3,4},{4,5},{5,6},{6,7},{7,8},{8,9},{9,10},{10,1... | collective-permute-start | bytes 46088 | tf_op jit(solution)/shard_map/ppermute | solution.py:34
  56.4 6.1 %collective-permute-start.5 = (bf16[64,2,60]{0,1,2:T(2,128)(2,1)S(1)}, bf16[64,2,60]{0,1,2:T(2,128)(2,1)S(1)}, u32[]{:S(2)}, u32[]{:S(2)}) collective-permute-start(bf16[64,2,60]{0,1,2:T(2,128)(2,1)S(1)} %get-tuple-element.224), channel_id=1, source_target_pairs={{1,0},{2,1},{3,2},{4,3},{5,4},{6,5},{7,6},{8,7},{9,8},{10,9},{11,1... | collective-permute-start | bytes 46088 | tf_op jit(solution)/shard_map/ppermute | solution.py:35
  70.3 3.8 %copy-start.21 = (bf16[64,4,16]{0,2,1:T(8,128)(2,1)S(1)}, bf16[64,4,16]{0,2,1:T(8,128)(2,1)}, u32[]{:S(2)}) copy-start(bf16[64,4,16]{0,2,1:T(8,128)(2,1)} %get-tuple-element.244) | copy-start | bytes 24580
  70.3 3.9 %copy-start.26 = (bf16[64,4,16]{0,2,1:T(8,128)(2,1)S(1)}, bf16[64,4,16]{0,2,1:T(8,128)(2,1)}, u32[]{:S(2)}) copy-start(bf16[64,4,16]{0,2,1:T(8,128)(2,1)} %get-tuple-element.245) | copy-start | bytes 24580
  70.3 4.2 %copy-start.20 = (bf16[64,4,16]{0,2,1:T(8,128)(2,1)S(1)}, bf16[64,4,16]{0,2,1:T(8,128)(2,1)}, u32[]{:S(2)}) copy-start(bf16[64,4,16]{0,2,1:T(8,128)(2,1)} %get-tuple-element.242) | copy-start | bytes 24580
  70.3 4.3 %copy-start.25 = (bf16[64,4,16]{0,2,1:T(8,128)(2,1)S(1)}, bf16[64,4,16]{0,2,1:T(8,128)(2,1)}, u32[]{:S(2)}) copy-start(bf16[64,4,16]{0,2,1:T(8,128)(2,1)} %get-tuple-element.246) | copy-start | bytes 24580
  70.3 4.4 %copy-start.19 = (bf16[64,4,16]{0,2,1:T(8,128)(2,1)S(1)}, bf16[64,4,16]{0,2,1:T(8,128)(2,1)}, u32[]{:S(2)}) copy-start(bf16[64,4,16]{0,2,1:T(8,128)(2,1)} %get-tuple-element.243) | copy-start | bytes 24580
  70.3 4.5 %copy-start.24 = (bf16[64,4,16]{0,2,1:T(8,128)(2,1)S(1)}, bf16[64,4,16]{0,2,1:T(8,128)(2,1)}, u32[]{:S(2)}) copy-start(bf16[64,4,16]{0,2,1:T(8,128)(2,1)} %get-tuple-element.247) | copy-start | bytes 24580
  70.3 4.7 %copy-start.18 = (bf16[64,4,16]{0,2,1:T(8,128)(2,1)S(1)}, bf16[64,4,16]{0,2,1:T(8,128)(2,1)}, u32[]{:S(2)}) copy-start(bf16[64,4,16]{0,2,1:T(8,128)(2,1)} %get-tuple-element.241) | copy-start | bytes 24580
  70.3 4.9 %copy-start.23 = (bf16[64,4,16]{0,2,1:T(8,128)(2,1)S(1)}, bf16[64,4,16]{0,2,1:T(8,128)(2,1)}, u32[]{:S(2)}) copy-start(bf16[64,4,16]{0,2,1:T(8,128)(2,1)} %get-tuple-element.248) | copy-start | bytes 24580
  82.9 11.1 %collective-permute-start.6 = (bf16[128,2,60]{0,1,2:T(2,128)(2,1)S(1)}, bf16[128,2,60]{0,1,2:T(2,128)(2,1)S(1)}, u32[]{:S(2)}, u32[]{:S(2)}) collective-permute-start(bf16[128,2,60]{0,1,2:T(2,128)(2,1)S(1)} %get-tuple-element.221), channel_id=1, source_target_pairs={{0,1},{1,2},{2,3},{3,4},{4,5},{5,6},{6,7},{7,8},{8,9},{9,10},{10,1... | collective-permute-start | bytes 92168 | tf_op jit(solution)/shard_map/ppermute | solution.py:34
  86.0 8.0 %collective-permute-start.7 = (bf16[128,2,60]{0,1,2:T(2,128)(2,1)S(1)}, bf16[128,2,60]{0,1,2:T(2,128)(2,1)S(1)}, u32[]{:S(2)}, u32[]{:S(2)}) collective-permute-start(bf16[128,2,60]{0,1,2:T(2,128)(2,1)S(1)} %get-tuple-element.222), channel_id=1, source_target_pairs={{1,0},{2,1},{3,2},{4,3},{5,4},{6,5},{7,6},{8,7},{9,8},{10,9},{11,1... | collective-permute-start | bytes 92168 | tf_op jit(solution)/shard_map/ppermute | solution.py:35
  94.1 3.9 %copy-start.11 = (bf16[1,128,128]{2,0,1:T(2,128)(2,1)S(1)}, bf16[1,128,128]{2,0,1:T(2,128)(2,1)}, u32[]{:S(2)}) copy-start(bf16[1,128,128]{2,0,1:T(2,128)(2,1)} %get-tuple-element.161) | copy-start | bytes 98308
  94.3 3.8 %copy-start.10 = (bf16[1,128,128]{2,0,1:T(2,128)(2,1)S(1)}, bf16[1,128,128]{2,0,1:T(2,128)(2,1)}, u32[]{:S(2)}) copy-start(bf16[1,128,128]{2,0,1:T(2,128)(2,1)} %get-tuple-element.162) | copy-start | bytes 98308
  101.5 9.9 %collective-permute-start.8 = (bf16[128,2,60]{0,1,2:T(2,128)(2,1)S(1)}, bf16[128,2,60]{0,1,2:T(2,128)(2,1)S(1)}, u32[]{:S(2)}, u32[]{:S(2)}) collective-permute-start(bf16[128,2,60]{0,1,2:T(2,128)(2,1)S(1)} %get-tuple-element.219), channel_id=1, source_target_pairs={{0,1},{1,2},{2,3},{3,4},{4,5},{5,6},{6,7},{7,8},{8,9},{9,10},{10,1... | collective-permute-start | bytes 92168 | tf_op jit(solution)/shard_map/ppermute | solution.py:34
  103.5 8.0 %collective-permute-start.9 = (bf16[128,2,60]{0,1,2:T(2,128)(2,1)S(1)}, bf16[128,2,60]{0,1,2:T(2,128)(2,1)S(1)}, u32[]{:S(2)}, u32[]{:S(2)}) collective-permute-start(bf16[128,2,60]{0,1,2:T(2,128)(2,1)S(1)} %get-tuple-element.220), channel_id=1, source_target_pairs={{1,0},{2,1},{3,2},{4,3},{5,4},{6,5},{7,6},{8,7},{9,8},{10,9},{11,1... | collective-permute-start | bytes 92168 | tf_op jit(solution)/shard_map/ppermute | solution.py:35
  111.6 3.8 %copy-start.6 = (bf16[1,128,128]{2,0,1:T(2,128)(2,1)S(1)}, bf16[1,128,128]{2,0,1:T(2,128)(2,1)}, u32[]{:S(2)}) copy-start(bf16[1,128,128]{2,0,1:T(2,128)(2,1)} %get-tuple-element.169) | copy-start | bytes 98308
  (22 other events, 49.2 us)

commit v11 on v8

--- a/solution.py
+++ b/solution.py
@@ -141,10 +141,16 @@
     bottom_row = jnp.concatenate([corners[2], rims[1], corners[3]], axis=2)
     left_col = jnp.concatenate([blank, rims[2], blank], axis=2)
     right_col = jnp.concatenate([blank, rims[3], blank], axis=2)
-    summed = summed.at[:, :, 0, :].add(rim_line(kernel, top_row, (0, 1, 2)))
-    summed = summed.at[:, :, side - 1, :].add(rim_line(kernel, bottom_row, (6, 7, 8)))
-    summed = summed.at[:, :, :, 0].add(rim_line(kernel, left_col, (0, 3, 6)))
-    summed = summed.at[:, :, :, side - 1].add(rim_line(kernel, right_col, (2, 5, 8)))
+    lines = jnp.stack([top_row, bottom_row, left_col, right_col])
+    windows = jnp.stack([lines[..., k : k + side] for k in range(3)], axis=1)
+    line_taps = kernel[np.array([[0, 1, 2], [6, 7, 8], [0, 3, 6], [2, 5, 8]])]
+    fixes = jnp.einsum(
+        "lkoc,lkctq->lotq", line_taps, windows, preferred_element_type=jnp.float32
+    )
+    summed = summed.at[:, :, 0, :].add(fixes[0])
+    summed = summed.at[:, :, side - 1, :].add(fixes[1])
+    summed = summed.at[:, :, :, 0].add(fixes[2])
+    summed = summed.at[:, :, :, side - 1].add(fixes[3])
     summed = summed.reshape(summed.shape[0], tiles, side * side)
     ring = jnp.take(summed, cycle_table(P_SIZE), axis=2)
     next_cycles = jax.nn.gelu(ring, approximate=False).astype(jnp.bfloat16)

time: 137 us -> 132 us (0.964)
  waiting for transfers between devices: 5.53 us -> 18.7 us
  starting transfers between devices: 56.7 us -> 50.5 us
  matrix products: 13.2 us -> 7.32 us
  local copies, waits for them, and re-layouts: 32.2 us -> 27.9 us
  other arithmetic: 9.33 us -> 7.5 us
    ppermute x3, waiting for transfers between devices: 0.01 us -> 13.6 us  [extended_2(): before = lax.ppermute(last, axis, up)]
    ppermute x3, starting transfers between devices: 16.2 us -> 8.41 us  [extended_2(): after = lax.ppermute(initial, axis, down)]
    unnamed x36 -> x0, matrix products: 7.81 us -> none
    slice x8 -> x3, local copies, waits for them, and re-layouts: 4.19 us -> 0.03 us  [conv_layer(): summed = summed.at[:, :, side - 1, :].add(fixes[1])]
    gather x0 -> x3, local copies, waits for them, and re-layouts: none -> 1.83 us  [conv_layer(): line_taps = kernel[np.array([[0, 1, 2], [6, 7, 8], [0, 3, 6], [2, 5, 8]])]]
    ppermute x3, starting transfers between devices: 8.33 us -> 9.99 us  [extended_2(): before = lax.ppermute(last, axis, up)]
    unnamed x112 -> x51, local copies, waits for them, and re-layouts: 8.9 us -> 7.44 us
    concatenate x6 -> x0, other arithmetic: 1.43 us -> none  [the longest x3 0.72 us: conv_layer(): bottom_row = jnp.concatenate([corners[2], rims[1], corners[3]], axis=2)]
  transfers between devices with their start and end apart: 12 -> 12, of which waited for: 2 -> 4; matrix products, arithmetic and copies ran while one was open for 14% -> 11% of each run, Pallas kernels for 0% -> 0%
where the time goes in v11:
time: 132 us; the launch traced here: 131 us
  starting transfers between devices  50.5 us (38%)
  local copies, waits for them, and re-layouts  27.9 us (21%)
  waiting for transfers between devices  18.7 us (14%)
  blocking collectives  17.9 us (14%)
  other arithmetic  7.5 us (6%)
  matrix products  7.32 us (6%)
  between operations  1.32 us (1%)
    ppermute x4, starting transfers between devices, from_behind(): return lax.ppermute(value, axis, pairs)  21.4 us
    all_to_all x1, blocking collectives, on_device(): lax.all_to_all(activity, 'chan', split_axis=0, concat_axis=1, tiled=True)  17.9 us
    ppermute x3, waiting for transfers between devices, extended_2(): before = lax.ppermute(last, axis, up)  13.6 us
    all_to_all x2, starting transfers between devices, gather_by_exchange(): lax.all_to_all(copies, axis, split_axis=dim, concat_axis=dim, tiled=True)  10.8 us
    ppermute x3, starting transfers between devices, extended_2(): before = lax.ppermute(last, axis, up)  9.99 us
    ppermute x3, starting transfers between devices, extended_2(): after = lax.ppermute(initial, axis, down)  8.41 us
    unnamed x51, local copies, waits for them, and re-layouts  7.44 us
    all_to_all x2, waiting for transfers between devices, gather_by_exchange(): lax.all_to_all(copies, axis, split_axis=dim, concat_axis=dim, tiled=True)  5.03 us
  transfers between devices with their start and end apart: 12, of which 4 were waited for; matrix products, arithmetic and copies ran while one was open for 11% of the time, Pallas kernels for 0%

profile of v11, /device:TPU:2, one launch (start us, length us, event | category | flops | bytes accessed | tf_op | source)
XLA Modules:
  0.0 131.2 jit_solution(13237870903928937463)
XLA Ops:
  0.1 1.9 %copy.270 = bf16[8,8192]{0,1:T(8,128)(2,1)S(1)} copy(bf16[8,8192]{1,0:T(8,128)(2,1)} %param.51) | data formatting | bytes 262144 | tf_op args[0]
  2.2 2.0 %gather_fusion = bf16[640,8]{1,0:T(8,128)(2,1)S(1)} fusion(bf16[8,8192]{0,1:T(8,128)(2,1)S(1)} %copy.270, s32[1024]{0:T(1024)S(1)} %get-tuple-element.227), kind=kCustom, calls=%fused_computation.6 | custom fusion | bytes 23040 | tf_op jit(solution)/shard_map/jit(_take)/gather | solution.py:191
  4.4 13.0 %collective-permute-start = (bf16[8,128]{0,1:T(8,128)(2,1)S(1)}, bf16[8,128]{0,1:T(8,128)(2,1)S(1)}, u32[]{:S(2)}, u32[]{:S(2)}) collective-permute-start(bf16[8,128]{0,1:T(8,128)(2,1)S(1)} %get-tuple-element.162), channel_id=1, source_target_pairs={{0,496},{8,504},{16,0},{24,8},{32,16},{40,24},{48,32},{56,40},{64,... | collective-permute-start | bytes 6152 | tf_op jit(solution)/shard_map/ppermute | solution.py:14
  17.4 2.5 %collective-permute-start.1 = (bf16[8,128]{0,1:T(8,128)(2,1)S(1)}, bf16[8,128]{0,1:T(8,128)(2,1)S(1)}, u32[]{:S(2)}, u32[]{:S(2)}) collective-permute-start(bf16[8,128]{0,1:T(8,128)(2,1)S(1)} %get-tuple-element.161), channel_id=1, source_target_pairs={{0,504},{8,0},{16,8},{24,16},{32,24},{40,32},{48,40},{56,48},{64,5... | collective-permute-start | bytes 6152 | tf_op jit(solution)/shard_map/ppermute | solution.py:14
  19.9 1.9 %collective-permute-start.2 = (bf16[8,128]{0,1:T(8,128)(2,1)S(1)}, bf16[8,128]{0,1:T(8,128)(2,1)S(1)}, u32[]{:S(2)}, u32[]{:S(2)}) collective-permute-start(bf16[8,128]{0,1:T(8,128)(2,1)S(1)} %get-tuple-element.159), channel_id=1, source_target_pairs={{0,8},{8,16},{16,24},{24,32},{32,40},{40,48},{48,56},{56,64},{64,7... | collective-permute-start | bytes 6152 | tf_op jit(solution)/shard_map/ppermute | solution.py:14
  21.8 4.0 %collective-permute-start.3 = (bf16[8,128]{0,1:T(8,128)(2,1)S(1)}, bf16[8,128]{0,1:T(8,128)(2,1)S(1)}, u32[]{:S(2)}, u32[]{:S(2)}) collective-permute-start(bf16[8,128]{0,1:T(8,128)(2,1)S(1)} %get-tuple-element.158), channel_id=1, source_target_pairs={{0,16},{8,24},{16,32},{24,40},{32,48},{40,56},{48,64},{56,72},{64,... | collective-permute-start | bytes 6152 | tf_op jit(solution)/shard_map/ppermute | solution.py:14
  29.9 1.9 %reshape.786 = bf16[8,2,23040]{2,1,0:T(2,128)(2,1)} reshape(bf16[128,9,320]{2,1,0:T(8,128)(2,1)S(1)} %bitcast.365) | data formatting | bytes 1474560
  33.0 5.9 %all-to-all-start = ((bf16[8,8,640]{2,1,0:T(8,128)(2,1)}), bf16[8,8,640]{2,1,0:T(8,128)(2,1)S(1)}, u32[]{:S(2)}, u32[]{:S(2)}) async-start(bf16[8,8,640]{2,1,0:T(8,128)(2,1)} %broadcast_in_dim.104), calls=%async_computation | async-start | bytes 163840 | tf_op jit(solution)/shard_map/all_to_all | solution.py:24
  38.9 5.0 %all-to-all-done = bf16[8,8,640]{2,1,0:T(8,128)(2,1)S(1)} async-done(((bf16[8,8,640]{2,1,0:T(8,128)(2,1)}), bf16[8,8,640]{2,1,0:T(8,128)(2,1)S(1)}, u32[]{:S(2)}, u32[]{:S(2)}) %all-to-all-start) | async-done | bytes 81952 | tf_op jit(solution)/shard_map/all_to_all | solution.py:24
  44.0 4.8 %all-to-all-start.1 = ((bf16[8,2,23040]{2,1,0:T(2,128)(2,1)}), bf16[8,2,23040]{2,1,0:T(2,128)(2,1)S(1)}, u32[]{:S(2)}, u32[]{:S(2)}) async-start(bf16[8,2,23040]{2,1,0:T(2,128)(2,1)} %reshape.786), calls=%async_computation.1 | async-start | bytes 1474560 | tf_op jit(solution)/shard_map/all_to_all | solution.py:24
  52.6 4.6 %collective-permute-start.5 = (bf16[64,2,60]{0,1,2:T(2,128)(2,1)S(1)}, bf16[64,2,60]{0,1,2:T(2,128)(2,1)S(1)}, u32[]{:S(2)}, u32[]{:S(2)}) collective-permute-start(bf16[64,2,60]{0,1,2:T(2,128)(2,1)S(1)} %get-tuple-element.215), channel_id=1, source_target_pairs={{1,0},{2,1},{3,2},{4,3},{5,4},{6,5},{7,6},{8,7},{9,8},{10,9},{11,1... | collective-permute-start | bytes 46088 | tf_op jit(solution)/shard_map/ppermute | solution.py:35
  57.2 1.9 %collective-permute-start.4 = (bf16[64,2,60]{0,1,2:T(2,128)(2,1)S(1)}, bf16[64,2,60]{0,1,2:T(2,128)(2,1)S(1)}, u32[]{:S(2)}, u32[]{:S(2)}) collective-permute-start(bf16[64,2,60]{0,1,2:T(2,128)(2,1)S(1)} %get-tuple-element.214), channel_id=1, source_target_pairs={{0,1},{1,2},{2,3},{3,4},{4,5},{5,6},{6,7},{7,8},{8,9},{9,10},{10,1... | collective-permute-start | bytes 46088 | tf_op jit(solution)/shard_map/ppermute | solution.py:34
  59.1 1.0 fusion.19
  60.1 5.0 %collective-permute-done.4 = bf16[64,2,60]{0,1,2:T(2,128)(2,1)S(1)} collective-permute-done((bf16[64,2,60]{0,1,2:T(2,128)(2,1)S(1)}, bf16[64,2,60]{0,1,2:T(2,128)(2,1)S(1)}, u32[]{:S(2)}, u32[]{:S(2)}) %collective-permute-start.4) | collective-permute-done | bytes 15392 | tf_op jit(solution)/shard_map/ppermute | solution.py:34
  65.3 1.4 %gather_fusion.3 = bf16[272,64]{1,0:T(8,128)(2,1)S(1)} fusion(bf16[64,480]{0,1:T(8,128)(2,1)S(1)} %reshape.781, s32[1024]{0:T(1024)S(1)} %pad_clamp_fusion.1), kind=kCustom, calls=%fused_computation.9 | custom fusion | bytes 70720 | tf_op jit(solution)/shard_map/jit(_take)/gather | solution.py:134
  67.0 1.4 %reshape.787 = bf16[128,9,320]{2,1,0:T(8,128)(2,1)S(1)} reshape(bf16[8,2,23040]{2,1,0:T(2,128)(2,1)S(1)} %all-to-all-done.1) | data formatting | bytes 1474560
  69.3 1.8 %convolution_select_fusion = f32[16,32,3,128]{3,1,2,0:T(8,128)S(1)} fusion(bf16[3,3,128,64]{2,3,1,0:T(8,128)(2,1)S(1)} %bitcast.378, bf16[64,16,4,8,5]{0,1,4,3,2:T(8,128)(2,1)} %fusion.19, pred[32,3]{0,1:T(4,128)(4,1)S(1)} %copy-done.11), kind=kOutput, calls=%fused_computation.29 | convolution fusion | flops 217251840 | bytes 1261664 | tf_op jit(solution)/shard_map/conv_general_dilated | solution.py:126
  73.2 1.1 fusion.66
  74.9 1.1 convolution_select_fusion.2
  78.0 1.9 %collective-permute-start.7 = (bf16[128,2,60]{0,1,2:T(2,128)(2,1)S(1)}, bf16[128,2,60]{0,1,2:T(2,128)(2,1)S(1)}, u32[]{:S(2)}, u32[]{:S(2)}) collective-permute-start(bf16[128,2,60]{0,1,2:T(2,128)(2,1)S(1)} %get-tuple-element.213), channel_id=1, source_target_pairs={{1,0},{2,1},{3,2},{4,3},{5,4},{6,5},{7,6},{8,7},{9,8},{10,9},{11,1... | collective-permute-start | bytes 92168 | tf_op jit(solution)/shard_map/ppermute | solution.py:35
  80.0 3.9 %collective-permute-start.6 = (bf16[128,2,60]{0,1,2:T(2,128)(2,1)S(1)}, bf16[128,2,60]{0,1,2:T(2,128)(2,1)S(1)}, u32[]{:S(2)}, u32[]{:S(2)}) collective-permute-start(bf16[128,2,60]{0,1,2:T(2,128)(2,1)S(1)} %get-tuple-element.212), channel_id=1, source_target_pairs={{0,1},{1,2},{2,3},{3,4},{4,5},{5,6},{6,7},{7,8},{8,9},{9,10},{10,1... | collective-permute-start | bytes 92168 | tf_op jit(solution)/shard_map/ppermute | solution.py:34
  85.4 2.5 %collective-permute-done.6 = bf16[128,2,60]{0,1,2:T(2,128)(2,1)S(1)} collective-permute-done((bf16[128,2,60]{0,1,2:T(2,128)(2,1)S(1)}, bf16[128,2,60]{0,1,2:T(2,128)(2,1)S(1)}, u32[]{:S(2)}, u32[]{:S(2)}) %collective-permute-start.6) | collective-permute-done | bytes 30752 | tf_op jit(solution)/shard_map/ppermute | solution.py:34
  88.0 1.4 %gather_fusion.9 = bf16[272,128]{1,0:T(8,128)(2,1)S(1)} fusion(bf16[128,480]{0,1:T(8,128)(2,1)S(1)} %reshape.608, s32[1024]{0:T(1024)S(1)} %pad_clamp_fusion), kind=kCustom, calls=%fused_computation.2.clone | custom fusion | bytes 140352 | tf_op jit(solution)/shard_map/jit(_take)/gather | solution.py:134
  90.6 1.1 fusion.65
  92.2 1.1 convolution_select_fusion.1
  95.3 1.9 %collective-permute-start.9 = (bf16[128,2,60]{0,1,2:T(2,128)(2,1)S(1)}, bf16[128,2,60]{0,1,2:T(2,128)(2,1)S(1)}, u32[]{:S(2)}, u32[]{:S(2)}) collective-permute-start(bf16[128,2,60]{0,1,2:T(2,128)(2,1)S(1)} %get-tuple-element.211), channel_id=1, source_target_pairs={{1,0},{2,1},{3,2},{4,3},{5,4},{6,5},{7,6},{8,7},{9,8},{10,9},{11,1... | collective-permute-start | bytes 92168 | tf_op jit(solution)/shard_map/ppermute | solution.py:35
  97.3 4.1 %collective-permute-start.8 = (bf16[128,2,60]{0,1,2:T(2,128)(2,1)S(1)}, bf16[128,2,60]{0,1,2:T(2,128)(2,1)S(1)}, u32[]{:S(2)}, u32[]{:S(2)}) collective-permute-start(bf16[128,2,60]{0,1,2:T(2,128)(2,1)S(1)} %get-tuple-element.210), channel_id=1, source_target_pairs={{0,1},{1,2},{2,3},{3,4},{4,5},{5,6},{6,7},{7,8},{8,9},{9,10},{10,1... | collective-permute-start | bytes 92168 | tf_op jit(solution)/shard_map/ppermute | solution.py:34
  101.6 6.2 %collective-permute-done.8 = bf16[128,2,60]{0,1,2:T(2,128)(2,1)S(1)} collective-permute-done((bf16[128,2,60]{0,1,2:T(2,128)(2,1)S(1)}, bf16[128,2,60]{0,1,2:T(2,128)(2,1)S(1)}, u32[]{:S(2)}, u32[]{:S(2)}) %collective-permute-start.8) | collective-permute-done | bytes 30752 | tf_op jit(solution)/shard_map/ppermute | solution.py:34
  107.9 1.4 %gather_fusion.11 = bf16[272,128]{1,0:T(8,128)(2,1)S(1)} fusion(bf16[128,480]{0,1:T(8,128)(2,1)S(1)} %reshape.617, s32[1024]{0:T(1024)S(1)} %pad_clamp_fusion), kind=kCustom, calls=%fused_computation.5.clone | custom fusion | bytes 140352 | tf_op jit(solution)/shard_map/jit(_take)/gather | solution.py:134
  111.2 1.1 fusion.36
  112.5 17.9 %all_to_all.32 = bf16[128,4,256]{2,1,0:T(4,128)(2,1)S(1)} all-to-all(bf16[128,4,256]{2,1,0:T(4,128)(2,1)S(1)} %copy.324), channel_id=1, replica_groups=mesh['tile'=64,'chan'=8] {'chan'}, dimensions={0} | all-to-all | bytes 524288 | tf_op jit(solution)/shard_map/all_to_all | solution.py:227
  130.4 0.8 copy.327
  (199 shorter events, 22.4 us)
Async XLA Ops:
  0.0 2.1 %copy-start.9 = (s32[12]{0:T(128)S(1)}, s32[12]{0:T(128)}, u32[]{:S(2)}) copy-start(s32[12]{0:T(128)} %constant.559) | copy-start | bytes 148
  0.0 25.9 %copy-start.7 = (s32[60]{0:T(128)S(1)}, s32[60]{0:T(128)}, u32[]{:S(2)}) copy-start(s32[60]{0:T(128)} %constant.493.clone) | copy-start | bytes 724
  0.0 25.9 %copy-start.8 = (s32[68]{0:T(128)S(1)}, s32[68]{0:T(128)}, u32[]{:S(2)}) copy-start(s32[68]{0:T(128)} %constant.567) | copy-start | bytes 820
  0.0 27.4 %copy-start.6 = (s32[68]{0:T(128)S(1)}, s32[68]{0:T(128)}, u32[]{:S(2)}) copy-start(s32[68]{0:T(128)} %constant.518) | copy-start | bytes 820
  0.0 2.0 %copy-start.3 = (s32[1,5,128]{2,0,1:T(1,128)S(1)}, s32[1,5,128]{2,0,1:T(1,128)}, u32[]{:S(2)}) copy-start(s32[1,5,128]{2,0,1:T(1,128)} %param.52) | copy-start | bytes 7684
  0.0 2.0 %copy-start.10 = (s32[1,5]{1,0:T(1,128)S(1)}, s32[1,5]{1,0:T(1,128)}, u32[]{:S(2)}) copy-start(s32[1,5]{1,0:T(1,128)} %param.53) | copy-start | bytes 64
  0.0 25.9 %copy-start.4 = (s32[32,8]{0,1:T(8,128)S(1)}, s32[32,8]{0,1:T(8,128)}, u32[]{:S(2)}) copy-start(s32[32,8]{0,1:T(8,128)} %param.56) | copy-start | bytes 3076
  0.1 25.9 %copy-start.5 = (s32[32,8]{0,1:T(8,128)S(1)}, s32[32,8]{0,1:T(8,128)}, u32[]{:S(2)}) copy-start(s32[32,8]{0,1:T(8,128)} %param.57) | copy-start | bytes 3076
  0.1 29.1 %copy-start = (bf16[9,16,128]{2,1,0:T(8,128)(2,1)S(1)}, bf16[9,16,128]{2,1,0:T(8,128)(2,1)}, u32[]{:S(2)}) copy-start(bf16[9,16,128]{2,1,0:T(8,128)(2,1)} %param.60) | copy-start | bytes 110596
  0.1 29.0 %copy-start.1 = (bf16[9,16,128]{2,1,0:T(8,128)(2,1)S(1)}, bf16[9,16,128]{2,1,0:T(8,128)(2,1)}, u32[]{:S(2)}) copy-start(bf16[9,16,128]{2,1,0:T(8,128)(2,1)} %param.59) | copy-start | bytes 110596
  0.1 29.0 %copy-start.2 = (bf16[9,16,64]{2,1,0:T(8,128)(2,1)S(1)}, bf16[9,16,64]{2,1,0:T(8,128)(2,1)}, u32[]{:S(2)}) copy-start(bf16[9,16,64]{2,1,0:T(8,128)(2,1)} %param.58) | copy-start | bytes 55300
  4.4 27.5 %collective-permute-start = (bf16[8,128]{0,1:T(8,128)(2,1)S(1)}, bf16[8,128]{0,1:T(8,128)(2,1)S(1)}, u32[]{:S(2)}, u32[]{:S(2)}) collective-permute-start(bf16[8,128]{0,1:T(8,128)(2,1)S(1)} %get-tuple-element.162), channel_id=1, source_target_pairs={{0,496},{8,504},{16,0},{24,8},{32,16},{40,24},{48,32},{56,40},{64,... | collective-permute-start | bytes 6152 | tf_op jit(solution)/shard_map/ppermute | solution.py:14
  17.4 14.6 %collective-permute-start.1 = (bf16[8,128]{0,1:T(8,128)(2,1)S(1)}, bf16[8,128]{0,1:T(8,128)(2,1)S(1)}, u32[]{:S(2)}, u32[]{:S(2)}) collective-permute-start(bf16[8,128]{0,1:T(8,128)(2,1)S(1)} %get-tuple-element.161), channel_id=1, source_target_pairs={{0,504},{8,0},{16,8},{24,16},{32,24},{40,32},{48,40},{56,48},{64,5... | collective-permute-start | bytes 6152 | tf_op jit(solution)/shard_map/ppermute | solution.py:14
  19.9 12.3 %collective-permute-start.2 = (bf16[8,128]{0,1:T(8,128)(2,1)S(1)}, bf16[8,128]{0,1:T(8,128)(2,1)S(1)}, u32[]{:S(2)}, u32[]{:S(2)}) collective-permute-start(bf16[8,128]{0,1:T(8,128)(2,1)S(1)} %get-tuple-element.159), channel_id=1, source_target_pairs={{0,8},{8,16},{16,24},{24,32},{32,40},{40,48},{48,56},{56,64},{64,7... | collective-permute-start | bytes 6152 | tf_op jit(solution)/shard_map/ppermute | solution.py:14
  21.8 10.4 %collective-permute-start.3 = (bf16[8,128]{0,1:T(8,128)(2,1)S(1)}, bf16[8,128]{0,1:T(8,128)(2,1)S(1)}, u32[]{:S(2)}, u32[]{:S(2)}) collective-permute-start(bf16[8,128]{0,1:T(8,128)(2,1)S(1)} %get-tuple-element.158), channel_id=1, source_target_pairs={{0,16},{8,24},{16,32},{24,40},{32,48},{40,56},{48,64},{56,72},{64,... | collective-permute-start | bytes 6152 | tf_op jit(solution)/shard_map/ppermute | solution.py:14
  33.0 11.0 %all-to-all-start = ((bf16[8,8,640]{2,1,0:T(8,128)(2,1)}), bf16[8,8,640]{2,1,0:T(8,128)(2,1)S(1)}, u32[]{:S(2)}, u32[]{:S(2)}) async-start(bf16[8,8,640]{2,1,0:T(8,128)(2,1)} %broadcast_in_dim.104), calls=%async_computation | async-start | bytes 163840 | tf_op jit(solution)/shard_map/all_to_all | solution.py:24
  44.0 23.1 %all-to-all-start.1 = ((bf16[8,2,23040]{2,1,0:T(2,128)(2,1)}), bf16[8,2,23040]{2,1,0:T(2,128)(2,1)S(1)}, u32[]{:S(2)}, u32[]{:S(2)}) async-start(bf16[8,2,23040]{2,1,0:T(2,128)(2,1)} %reshape.786), calls=%async_computation.1 | async-start | bytes 1474560 | tf_op jit(solution)/shard_map/all_to_all | solution.py:24
  52.6 7.5 %collective-permute-start.5 = (bf16[64,2,60]{0,1,2:T(2,128)(2,1)S(1)}, bf16[64,2,60]{0,1,2:T(2,128)(2,1)S(1)}, u32[]{:S(2)}, u32[]{:S(2)}) collective-permute-start(bf16[64,2,60]{0,1,2:T(2,128)(2,1)S(1)} %get-tuple-element.215), channel_id=1, source_target_pairs={{1,0},{2,1},{3,2},{4,3},{5,4},{6,5},{7,6},{8,7},{9,8},{10,9},{11,1... | collective-permute-start | bytes 46088 | tf_op jit(solution)/shard_map/ppermute | solution.py:35
  57.2 7.9 %collective-permute-start.4 = (bf16[64,2,60]{0,1,2:T(2,128)(2,1)S(1)}, bf16[64,2,60]{0,1,2:T(2,128)(2,1)S(1)}, u32[]{:S(2)}, u32[]{:S(2)}) collective-permute-start(bf16[64,2,60]{0,1,2:T(2,128)(2,1)S(1)} %get-tuple-element.214), channel_id=1, source_target_pairs={{0,1},{1,2},{2,3},{3,4},{4,5},{5,6},{6,7},{7,8},{8,9},{9,10},{10,1... | collective-permute-start | bytes 46088 | tf_op jit(solution)/shard_map/ppermute | solution.py:34
  68.4 0.8 copy-start.11
  78.0 7.3 %collective-permute-start.7 = (bf16[128,2,60]{0,1,2:T(2,128)(2,1)S(1)}, bf16[128,2,60]{0,1,2:T(2,128)(2,1)S(1)}, u32[]{:S(2)}, u32[]{:S(2)}) collective-permute-start(bf16[128,2,60]{0,1,2:T(2,128)(2,1)S(1)} %get-tuple-element.213), channel_id=1, source_target_pairs={{1,0},{2,1},{3,2},{4,3},{5,4},{6,5},{7,6},{8,7},{9,8},{10,9},{11,1... | collective-permute-start | bytes 92168 | tf_op jit(solution)/shard_map/ppermute | solution.py:35
  80.0 7.9 %collective-permute-start.6 = (bf16[128,2,60]{0,1,2:T(2,128)(2,1)S(1)}, bf16[128,2,60]{0,1,2:T(2,128)(2,1)S(1)}, u32[]{:S(2)}, u32[]{:S(2)}) collective-permute-start(bf16[128,2,60]{0,1,2:T(2,128)(2,1)S(1)} %get-tuple-element.212), channel_id=1, source_target_pairs={{0,1},{1,2},{2,3},{3,4},{4,5},{5,6},{6,7},{7,8},{8,9},{9,10},{10,1... | collective-permute-start | bytes 92168 | tf_op jit(solution)/shard_map/ppermute | solution.py:34
  95.3 6.2 %collective-permute-start.9 = (bf16[128,2,60]{0,1,2:T(2,128)(2,1)S(1)}, bf16[128,2,60]{0,1,2:T(2,128)(2,1)S(1)}, u32[]{:S(2)}, u32[]{:S(2)}) collective-permute-start(bf16[128,2,60]{0,1,2:T(2,128)(2,1)S(1)} %get-tuple-element.211), channel_id=1, source_target_pairs={{1,0},{2,1},{3,2},{4,3},{5,4},{6,5},{7,6},{8,7},{9,8},{10,9},{11,1... | collective-permute-start | bytes 92168 | tf_op jit(solution)/shard_map/ppermute | solution.py:35
  97.3 10.5 %collective-permute-start.8 = (bf16[128,2,60]{0,1,2:T(2,128)(2,1)S(1)}, bf16[128,2,60]{0,1,2:T(2,128)(2,1)S(1)}, u32[]{:S(2)}, u32[]{:S(2)}) collective-permute-start(bf16[128,2,60]{0,1,2:T(2,128)(2,1)S(1)} %get-tuple-element.210), channel_id=1, source_target_pairs={{0,1},{1,2},{2,3},{3,4},{4,5},{5,6},{6,7},{7,8},{8,9},{9,10},{10,1... | collective-permute-start | bytes 92168 | tf_op jit(solution)/shard_map/ppermute | solution.py:34
